TPU v7x, 128 devices: a whole 4x4x4 slice. The times are simulated.
128 devices in a mesh: ctx: 16 (over y, z_hi, core), tp: 8 (over z_lo, x).
Axes of the slice: x: 4, y: 4, z: 4 (z_hi: 2, z_lo: 2; z = z_hi * 2 + z_lo), core: 2. Of those that a mesh axis runs over, the one named last changes fastest.
Arguments:
- queries: bfloat16 [32768, 8192], P('ctx', 'tp'), may hold values from -48 to 48
- keys: bfloat16 [32768, 1024], P(('ctx', 'tp')), may hold values from -6 to 6
- values: bfloat16 [32768, 1024], P(('ctx', 'tp')), may hold values from -6 to 6
- rope_factors: float32 [64], replicated, may hold values from 1 to 32
- doc_lengths: int32 [128], replicated, may hold values from 1 to 512, 32768 in all
- owner_map: int32 [16, 8], replicated, may hold values from 0 to 15, as said below
Outputs:
- attended: bfloat16 [32768, 8192], P('ctx', 'tp')
Inputs may be any that keep to these rules, and one draw needn't show every extreme that they name: `owner_map`: row c lists the owners of the 8 blocks of index c: they are different devices, and every device owns exactly one block of each in-device number r, so exactly 8 blocks in all.
All inputs are finite; a program needn't handle non-finite values.
Results may differ from a plain program's by a relative error of at most 0.0051.
Values may be sent and summed in bfloat16 or wider, within the bound.
No kernel may reach another device: no remote copies, remote signals or barrier semaphores. Data moves between devices by JAX's collectives and lax.ppermute only.
A program may use at most 128 MiB of HBM per device.

v0:
```python
import functools
import math

import jax
import jax.numpy as jnp
from jax import lax
from jax.experimental import pallas as pl
from jax.experimental.pallas import tpu as pltpu
from jax.sharding import PartitionSpec as P

THETA = 500000.0


def passed_along(shard, axis, by):
    length = lax.axis_size(axis)
    pairs = [(i, i + by) for i in range(length) if 0 <= i + by < length]
    return lax.ppermute(shard, axis, pairs)


def doc_tables(lengths, positions):
    doc_ends = jnp.cumsum(lengths, dtype=jnp.int32)
    before = positions[:, None] >= doc_ends[None, :]
    doc_index = jnp.sum(before.astype(jnp.int32), axis=1, dtype=jnp.int32)
    doc_start = jnp.sum(jnp.where(before, lengths[None, :], 0), axis=1, dtype=jnp.int32)
    return (doc_index, positions - doc_start)


def inverse_freqs(factors, head_dim):
    half_dim = head_dim // 2
    exponent = jnp.arange(half_dim, dtype=jnp.float32) * (2.0 / head_dim)
    return 1.0 / (factors * jnp.power(jnp.float32(THETA), exponent))


def rotation_tables(offsets, inverse):
    angles = offsets.astype(jnp.float32)[:, None] * inverse[None, :]
    cosine = jnp.cos(angles)
    sine = jnp.sin(angles)
    return (
        jnp.concatenate([cosine, cosine], axis=1),
        jnp.concatenate([-sine, sine], axis=1),
    )


def rotate(vectors, offsets, inverse):
    half_dim = vectors.shape[-1] // 2
    angles = offsets.astype(jnp.float32)[:, None] * inverse[None, :]
    cosine = jnp.cos(angles)
    sine_part = jnp.sin(angles)
    first_half = vectors[..., :half_dim]
    second_half = vectors[..., half_dim:]
    return jnp.concatenate(
        [
            first_half * cosine - second_half * sine_part,
            second_half * cosine + first_half * sine_part,
        ],
        axis=-1,
    )


def attend_kernel(
    slot_ref, has_ref, q_ref, cos_ref, sin_ref, k_ref, v_ref, dq_ref, dk_ref, o_ref,
    *, heads, head_dim, block_rows, span, scale,
):
    d = pl.program_id(0)

    @pl.when(has_ref[d] == 0)
    def _():
        o_ref[...] = jnp.zeros_like(o_ref)

    @pl.when(has_ref[d] != 0)
    def _():
        start = pl.multiple_of(slot_ref[d] * block_rows, block_rows)
        k = k_ref[pl.ds(start, span), :]
        v = v_ref[pl.ds(start, span), :]
        doc_q = dq_ref[0]
        doc_k = dk_ref[0]
        tail = span - block_rows
        row = lax.broadcasted_iota(jnp.int32, (block_rows, span), 0)
        col = lax.broadcasted_iota(jnp.int32, (block_rows, span), 1)
        visible = (doc_q == doc_k) & (col <= row + tail)
        cos = cos_ref[...]
        sin = sin_ref[...]
        for h in range(heads):
            cols = slice(h * head_dim, (h + 1) * head_dim)
            qh = q_ref[:, cols].astype(jnp.float32)
            qr = (qh * cos + pltpu.roll(qh, head_dim // 2, 1) * sin).astype(jnp.bfloat16)
            s = lax.dot_general(
                qr, k, (((1,), (1,)), ((), ())), preferred_element_type=jnp.float32
            ) * scale
            s = jnp.where(visible, s, -1e30)
            m = jnp.max(s, axis=1, keepdims=True)
            p = jnp.exp(s - m)
            l = jnp.sum(p, axis=1, keepdims=True)
            o = jnp.dot(p.astype(jnp.bfloat16), v, preferred_element_type=jnp.float32)
            o_ref[0, :, cols] = (o / l).astype(o_ref.dtype)


def attend(slot, has, q, cos_t, sin_t, k_ext, v_ext, doc_q, doc_k, n_dest, head_dim):
    rows, width = q.shape
    per_dev, block_rows, _ = doc_q.shape
    span = doc_k.shape[2]
    ext_rows = k_ext.shape[0]
    heads = width // head_dim
    kernel = functools.partial(
        attend_kernel,
        heads=heads,
        head_dim=head_dim,
        block_rows=block_rows,
        span=span,
        scale=1.0 / math.sqrt(head_dim),
    )
    flops = 4 * per_dev * heads * block_rows * span * head_dim
    grid_spec = pltpu.PrefetchScalarGridSpec(
        num_scalar_prefetch=2,
        grid=(n_dest,),
        in_specs=[
            pl.BlockSpec((block_rows, width), lambda d, s, h: (s[d], 0)),
            pl.BlockSpec((block_rows, head_dim), lambda d, s, h: (s[d], 0)),
            pl.BlockSpec((block_rows, head_dim), lambda d, s, h: (s[d], 0)),
            pl.BlockSpec((ext_rows, head_dim), lambda d, s, h: (0, 0)),
            pl.BlockSpec((ext_rows, head_dim), lambda d, s, h: (0, 0)),
            pl.BlockSpec((1, block_rows, 1), lambda d, s, h: (s[d], 0, 0)),
            pl.BlockSpec((1, 1, span), lambda d, s, h: (s[d], 0, 0)),
        ],
        out_specs=pl.BlockSpec((1, block_rows, width), lambda d, s, h: (d, 0, 0)),
    )
    return pl.pallas_call(
        kernel,
        grid_spec=grid_spec,
        out_shape=jax.ShapeDtypeStruct((n_dest, block_rows, width), q.dtype),
        cost_estimate=pl.CostEstimate(
            flops=flops,
            transcendentals=per_dev * heads * block_rows * span,
            bytes_accessed=2 * rows * width * 2 + 2 * ext_rows * head_dim * 2,
        ),
    )(slot, has, q, cos_t, sin_t, k_ext, v_ext, doc_q, doc_k)


def local(queries, keys, values, rope_factors, doc_lengths, owner_map):
    ctx_size = lax.axis_size("ctx")
    ctx_index = lax.axis_index("ctx")
    tp_size = lax.axis_size("tp")
    row_count = queries.shape[0]
    per_dev = owner_map.shape[1]
    block_rows = row_count // per_dev
    tail_rows = row_count // 4
    span = tail_rows + block_rows
    head_dim = 2 * rope_factors.shape[0]
    kv_heads = keys.shape[1] // head_dim
    kv_local = kv_heads // tp_size
    shard_rows = keys.shape[0]

    kv = jnp.stack(
        [
            keys.reshape(shard_rows, tp_size, kv_local * head_dim),
            values.reshape(shard_rows, tp_size, kv_local * head_dim),
        ],
        axis=2,
    ).reshape(shard_rows, tp_size * 2 * kv_local * head_dim)
    kv = lax.all_to_all(kv, "tp", split_axis=1, concat_axis=0, tiled=True)
    kv_tail = passed_along(kv[row_count - tail_rows :], "ctx", 1)
    kv_ext = jnp.concatenate([kv_tail, kv], axis=0)
    kv_width = kv_local * head_dim
    k_raw = kv_ext[:, :kv_width]
    v_ext = kv_ext[:, kv_width:]

    ext_rows = row_count + tail_rows
    pos_ext = ctx_index * row_count - tail_rows + jnp.arange(ext_rows, dtype=jnp.int32)
    doc_ext, off_ext = doc_tables(doc_lengths, pos_ext)
    doc_ext = jnp.where(pos_ext >= 0, doc_ext, -1)
    inverse = inverse_freqs(rope_factors, head_dim)
    k_ext = rotate(k_raw.astype(jnp.float32), off_ext, inverse).astype(jnp.bfloat16)
    cos_t, sin_t = rotation_tables(off_ext[tail_rows:], inverse)

    doc_q = doc_ext[tail_rows:].reshape(per_dev, block_rows, 1)
    doc_k = jnp.stack(
        [doc_ext[slot * block_rows : slot * block_rows + span] for slot in range(per_dev)]
    ).reshape(per_dev, 1, span)

    devices = jnp.arange(ctx_size, dtype=jnp.int32)
    owner_row = lax.dynamic_index_in_dim(owner_map, ctx_index, 0, keepdims=False)
    match = owner_row[None, :] == devices[:, None]
    has = jnp.sum(match.astype(jnp.int32), axis=1, dtype=jnp.int32)
    slot = jnp.sum(
        jnp.where(match, jnp.arange(per_dev, dtype=jnp.int32)[None, :], 0), axis=1, dtype=jnp.int32
    )

    send = attend(
        slot, has, queries, cos_t, sin_t, k_ext, v_ext, doc_q, doc_k, ctx_size, head_dim
    )
    arrived = lax.all_to_all(send, "ctx", split_axis=0, concat_axis=0, tiled=True)

    sources_match = owner_map == ctx_index
    my_sources = jnp.sum(
        jnp.where(sources_match, devices[:, None], 0), axis=0, dtype=jnp.int32
    )
    finished = jnp.take(arrived, my_sources, axis=0)
    return finished.reshape(row_count, queries.shape[1])


def solution(mesh):
    in_specs = (P("ctx", "tp"), P(("ctx", "tp"), None), P(("ctx", "tp"), None), P(), P(), P())
    out_specs = P("ctx", "tp")
    return jax.shard_map(local, mesh=mesh, in_specs=in_specs, out_specs=out_specs, check_vma=False)
```

profile of v0, /device:TPU:1, one launch (start us, length us, event | category | flops | bytes accessed | tf_op | source)
XLA Modules:
  0.0 234.9 jit_solution(1985925847807298390)
XLA Ops:
  0.0 1.2 copy.19
  1.2 0.1 copy.20
  1.3 0.1 pad_maximum_fusion.2
  1.4 1.1 copy.16
  2.5 1.5 all_to_all.17
  4.0 6.3 %all-to-all-start = ((bf16[256,8,256]{2,0,1:T(8,128)(2,1)}), bf16[256,8,256]{2,0,1:T(8,128)(2,1)S(1)}, u32[]{:S(2)}, u32[]{:S(2)}) async-start(bf16[256,8,256]{2,0,1:T(8,128)(2,1)} %all_to_all.17), calls=%async_computation | async-start | bytes 2097152 | tf_op jit(solution)/shard_map/all_to_all | solution.py:160
  10.3 0.0 copy-start.1
  10.4 0.1 copy.15
  10.5 0.2 reduce-window.8
  10.7 0.1 reduce.1
  10.8 2.0 fusion.5
  12.8 1.1 reduce_sum.56
  14.0 0.1 stack.39
  14.1 0.6 reshape.100.dk_ref
  14.7 0.2 dynamic-slice_reduce_fusion
  14.9 0.7 convert_reduce_fusion
  15.6 1.2 slice_select_fusion.dq_ref
  16.8 5.3 %fusion.14 = (f32[2048,64]{1,0:T(8,128)S(1)}, f32[2048,64]{1,0:T(8,128)S(1)}, f32[2048,64]{1,0:T(8,128)}) fusion(f32[64]{0:T(128)S(1)} %multiply_divide_fusion, f32[2048]{0:T(1024)S(1)} %slice_convert_fusion), kind=kLoop, calls=%fused_computation.32 | loop fusion | flops 262144 | bytes 1581312 | tf_op jit(solution)/shard_map/neg | solution.py:40
  22.2 4.0 %all-to-all-done = bf16[256,8,256]{2,0,1:T(8,128)(2,1)S(1)} async-done(((bf16[256,8,256]{2,0,1:T(8,128)(2,1)}), bf16[256,8,256]{2,0,1:T(8,128)(2,1)S(1)}, u32[]{:S(2)}, u32[]{:S(2)}) %all-to-all-start) | async-done | bytes 1048608 | tf_op jit(solution)/shard_map/all_to_all | solution.py:160
  26.2 5.9 %collective-permute-start = (bf16[512,256]{1,0:T(8,128)(2,1)S(1)}, bf16[512,256]{1,0:T(8,128)(2,1)S(1)}, u32[]{:S(2)}, u32[]{:S(2)}) collective-permute-start(bf16[512,256]{1,0:T(8,128)(2,1)S(1)} %bitcast.27), channel_id=1, source_target_pairs={{0,8},{8,16},{16,24},{24,32},{32,40},{40,48},{48,56},{56,64},{64,7... | collective-permute-start | bytes 786440 | tf_op jit(solution)/shard_map/ppermute | solution.py:17
  32.1 3.5 %pad_maximum_fusion = (f32[2048,128]{1,0:T(8,128)}, f32[2048,128]{1,0:T(8,128)}) fusion(f32[2048,64]{1,0:T(8,128)} %get-tuple-element.25, f32[2048,64]{1,0:T(8,128)S(1)} %get-tuple-element.24, f32[2048,64]{1,0:T(8,128)S(1)} %get-tuple-element.23), kind=kLoop, calls=%fused_computation.25 | loop fusion | flops 524288 | bytes 3670016 | tf_op jit(solution)/shard_map/concatenate | solution.py:39
  35.6 0.0 collective-permute-done
  35.6 1.0 pad_maximum_fusion.3
  36.6 6.0 %fusion.7 = (bf16[2560,64]{1,0:T(8,128)(2,1)S(1)}, bf16[2560,64]{1,0:T(8,128)(2,1)S(1)}) fusion(f32[2560,128]{1,0:T(8,128)S(1)} %get-tuple-element.14, f32[2560]{0:T(1024)S(1)} %get-tuple-element.9, f32[64]{0:T(128)S(1)} %multiply_divide_fusion), kind=kLoop, calls=%fused_computation.15 | loop fusion | flops 1474560 | bytes 1976576 | tf_op jit(solution)/shard_map/convert
  42.6 1.2 pad_maximum_fusion.4.k_ref
  43.8 40.6 %shard_map.64 = bf16[16,256,1024]{2,1,0:T(8,128)(2,1)} custom-call(s32[16]{0:T(128)} %get-tuple-element.8.slot_ref, s32[16]{0:T(128)} %get-tuple-element.7.has_ref, bf16[2048,1024]{1,0:T(8,128)(2,1)} %q_ref.1, f32[2048,128]{1,0:T(8,128)} %get-tuple-element.26.cos_ref, f32[2048,128]{1,0:T(8,128)} %get-tuple-element.27.sin_ref, ...), custom_call_target="tpu_custom_call" | custom-call | flops 6442450944 | bytes 9699328 | tf_op jit(solution)/shard_map/pallas_call | solution.py:127
  84.4 9.0 %all-to-all-start.1 = ((bf16[16,256,1024]{2,1,0:T(8,128)(2,1)}), bf16[16,256,1024]{2,1,0:T(8,128)(2,1)}, u32[]{:S(2)}, u32[]{:S(2)}) async-start(bf16[16,256,1024]{2,1,0:T(8,128)(2,1)} %shard_map.64), calls=%async_computation.1 | async-start | bytes 16777216 | tf_op jit(solution)/shard_map/all_to_all | solution.py:191
  93.4 0.1 select_reduce_fusion.1
  93.5 0.1 broadcast_in_dim.69
  93.6 131.3 %all-to-all-done.1 = bf16[16,256,1024]{2,1,0:T(8,128)(2,1)} async-done(((bf16[16,256,1024]{2,1,0:T(8,128)(2,1)}), bf16[16,256,1024]{2,1,0:T(8,128)(2,1)}, u32[]{:S(2)}, u32[]{:S(2)}) %all-to-all-start.1) | async-done | bytes 8388640 | tf_op jit(solution)/shard_map/all_to_all | solution.py:191
  224.9 6.1 %gather_fusion = bf16[8,256,1024]{2,1,0:T(8,128)(2,1)} fusion(bf16[16,256,1024]{2,1,0:T(8,128)(2,1)} %all-to-all-done.1, s32[1024]{0:T(1024)S(1)} %pad_clamp_fusion), kind=kCustom, calls=%fused_computation | custom fusion | bytes 8388640 | tf_op jit(solution)/shard_map/jit(_take)/gather | solution.py:197
  231.0 3.9 %bitcast_select_fusion = bf16[2048,1024]{1,0:T(8,128)(2,1)} fusion(bf16[8,256,1024]{2,1,0:T(8,128)(2,1)} %gather_fusion, pred[2048]{0:T(1024)(128)(4,1)S(1)} %broadcast_in_dim.70), kind=kLoop, calls=%fused_computation.1 | loop fusion | flops 2097152 | bytes 8390656 | tf_op jit(solution)/shard_map/jit(_take)/select_n | solution.py:197
  (26 shorter events, 0.1 us)
Async XLA Ops:
  0.0 1.2 copy-start
  4.0 6.4 %copy-start.2 = (s32[128]{0:T(128)S(1)}, s32[128]{0:T(128)}, u32[]{:S(2)}) copy-start(s32[128]{0:T(128)} %param.10) | copy-start | bytes 1540
  4.0 22.2 %all-to-all-start = ((bf16[256,8,256]{2,0,1:T(8,128)(2,1)}), bf16[256,8,256]{2,0,1:T(8,128)(2,1)S(1)}, u32[]{:S(2)}, u32[]{:S(2)}) async-start(bf16[256,8,256]{2,0,1:T(8,128)(2,1)} %all_to_all.17), calls=%async_computation | async-start | bytes 2097152 | tf_op jit(solution)/shard_map/all_to_all | solution.py:160
  10.3 4.4 %copy-start.3 = (f32[64]{0:T(128)S(1)}, f32[64]{0:T(128)}, u32[]{:S(2)}) copy-start(f32[64]{0:T(128)} %param.9) | copy-start | bytes 772
  10.3 4.4 %copy-start.1 = (s32[16,8]{0,1:T(8,128)S(1)}, s32[16,8]{0,1:T(8,128)}, u32[]{:S(2)}) copy-start(s32[16,8]{0,1:T(8,128)} %param.11) | copy-start | bytes 1540
  26.2 9.4 %collective-permute-start = (bf16[512,256]{1,0:T(8,128)(2,1)S(1)}, bf16[512,256]{1,0:T(8,128)(2,1)S(1)}, u32[]{:S(2)}, u32[]{:S(2)}) collective-permute-start(bf16[512,256]{1,0:T(8,128)(2,1)S(1)} %bitcast.27), channel_id=1, source_target_pairs={{0,8},{8,16},{16,24},{24,32},{32,40},{40,48},{48,56},{56,64},{64,7... | collective-permute-start | bytes 786440 | tf_op jit(solution)/shard_map/ppermute | solution.py:17
  84.4 140.5 %all-to-all-start.1 = ((bf16[16,256,1024]{2,1,0:T(8,128)(2,1)}), bf16[16,256,1024]{2,1,0:T(8,128)(2,1)}, u32[]{:S(2)}, u32[]{:S(2)}) async-start(bf16[16,256,1024]{2,1,0:T(8,128)(2,1)} %shard_map.64), calls=%async_computation.1 | async-start | bytes 16777216 | tf_op jit(solution)/shard_map/all_to_all | solution.py:191
where the time goes:
time: 235 us
  waiting for transfers between devices  135 us (57%)
  Pallas kernels  40.6 us (17%)
  other arithmetic  25.3 us (11%)
  starting transfers between devices  21.2 us (9%)
  local copies, waits for them, and re-layouts  12.3 us (5%)
    all_to_all x1, waiting for transfers between devices, local(): lax.all_to_all(send, 'ctx', split_axis=0, concat_axis=0, tiled=True)  131 us
    pallas_call x1, Pallas kernels, attend(): pl.pallas_call(kernel, grid_spec=grid_spec, out_shape=jax.ShapeDtypeStruc...  40.6 us
    all_to_all x1, starting transfers between devices, local(): lax.all_to_all(send, 'ctx', split_axis=0, concat_axis=0, tiled=True)  8.98 us
    all_to_all x1, starting transfers between devices, local(): kv = lax.all_to_all(kv, 'tp', split_axis=1, concat_axis=0, tiled=True)  6.32 us
    another operation x3, other arithmetic  6.24 us
    gather x1, local copies, waits for them, and re-layouts, local(): finished = jnp.take(arrived, my_sources, axis=0)  6.12 us
    ppermute x1, starting transfers between devices, passed_along(): return lax.ppermute(shard, axis, pairs)  5.89 us
    neg x1, other arithmetic, rotation_tables(): -sine  5.34 us
  transfers between devices with their start and end apart: 3, of which 2 were waited for; matrix products, arithmetic and copies ran while one was open for 7% of the time, Pallas kernels for 0%

commit v1 on v0

--- a/solution.py
+++ b/solution.py
@@ -179,7 +179,8 @@
 
     devices = jnp.arange(ctx_size, dtype=jnp.int32)
     owner_row = lax.dynamic_index_in_dim(owner_map, ctx_index, 0, keepdims=False)
-    match = owner_row[None, :] == devices[:, None]
+    dest = lax.rem(ctx_index + devices, ctx_size)
+    match = owner_row[None, :] == dest[:, None]
     has = jnp.sum(match.astype(jnp.int32), axis=1, dtype=jnp.int32)
     slot = jnp.sum(
         jnp.where(match, jnp.arange(per_dev, dtype=jnp.int32)[None, :], 0), axis=1, dtype=jnp.int32
@@ -188,13 +189,18 @@
     send = attend(
         slot, has, queries, cos_t, sin_t, k_ext, v_ext, doc_q, doc_k, ctx_size, head_dim
     )
-    arrived = lax.all_to_all(send, "ctx", split_axis=0, concat_axis=0, tiled=True)
+    pieces = [send[0]]
+    for shift in range(1, ctx_size):
+        pairs = [(i, (i + shift) % ctx_size) for i in range(ctx_size)]
+        pieces.append(lax.ppermute(send[shift], "ctx", pairs))
+    arrived = jnp.stack(pieces)
 
     sources_match = owner_map == ctx_index
     my_sources = jnp.sum(
         jnp.where(sources_match, devices[:, None], 0), axis=0, dtype=jnp.int32
     )
-    finished = jnp.take(arrived, my_sources, axis=0)
+    shifts = lax.rem(ctx_index - my_sources + ctx_size, ctx_size)
+    finished = jnp.take(arrived, shifts, axis=0)
     return finished.reshape(row_count, queries.shape[1])
 
 

time: 235 us -> 251 us (1.068); the launches traced: 235 us -> 247 us
  waiting for transfers between devices: 135 us -> 47.2 us
  starting transfers between devices: 21.2 us -> 99.2 us
  local copies, waits for them, and re-layouts: 12.3 us -> 34.8 us
    all_to_all x1 -> x0, waiting for transfers between devices: 131 us -> none  [local(): lax.all_to_all(send, 'ctx', split_axis=0, concat_axis=0, tiled=True)]
    ppermute x0 -> x15, starting transfers between devices: none -> 87.1 us  [local(): pieces.append(lax.ppermute(send[shift], 'ctx', pairs))]
    ppermute x0 -> x15, waiting for transfers between devices: none -> 43.3 us  [local(): pieces.append(lax.ppermute(send[shift], 'ctx', pairs))]
    unnamed x10 -> x22, local copies, waits for them, and re-layouts: 1.3 us -> 17.2 us
    all_to_all x1 -> x0, starting transfers between devices: 8.98 us -> none  [local(): lax.all_to_all(send, 'ctx', split_axis=0, concat_axis=0, tiled=True)]
    squeeze x0 -> x1, local copies, waits for them, and re-layouts: none -> 5.78 us  [local(): pieces.append(lax.ppermute(send[shift], 'ctx', pairs))]
  transfers between devices with their start and end apart: 3 -> 17, of which waited for: 2 -> 7; matrix products, arithmetic and copies ran while one was open for 7% -> 12% of each run, Pallas kernels for 0% -> 0%
where the time goes in v1:
time: 251 us; the launch traced here: 247 us
  starting transfers between devices  99.2 us (40%)
  waiting for transfers between devices  47.2 us (19%)
  Pallas kernels  40.2 us (16%)
  local copies, waits for them, and re-layouts  34.8 us (14%)
  other arithmetic  25.3 us (10%)
    ppermute x15, starting transfers between devices, local(): pieces.append(lax.ppermute(send[shift], 'ctx', pairs))  87.1 us
    ppermute x15, waiting for transfers between devices, local(): pieces.append(lax.ppermute(send[shift], 'ctx', pairs))  43.3 us
    pallas_call x1, Pallas kernels, attend(): pl.pallas_call(kernel, grid_spec=grid_spec, out_shape=jax.ShapeDtypeStruc...  40.2 us
    unnamed x22, local copies, waits for them, and re-layouts  17.2 us
    another operation x3, other arithmetic  6.24 us
    all_to_all x1, starting transfers between devices, local(): kv = lax.all_to_all(kv, 'tp', split_axis=1, concat_axis=0, tiled=True)  6.19 us
    gather x1, local copies, waits for them, and re-layouts, local(): finished = jnp.take(arrived, shifts, axis=0)  6.14 us
    ppermute x1, starting transfers between devices, passed_along(): return lax.ppermute(shard, axis, pairs)  5.89 us
  transfers between devices with their start and end apart: 17, of which 7 were waited for; matrix products, arithmetic and copies ran while one was open for 12% of the time, Pallas kernels for 0%

profile of v1, /device:TPU:1, one launch (start us, length us, event | category | flops | bytes accessed | tf_op | source)
XLA Modules:
  0.0 246.9 jit_solution(15692687210394246537)
XLA Ops:
  0.0 1.2 copy.19
  3.5 1.5 all_to_all.14
  5.0 6.2 %all-to-all-start = ((bf16[256,8,256]{2,0,1:T(8,128)(2,1)}), bf16[256,8,256]{2,0,1:T(8,128)(2,1)S(1)}, u32[]{:S(2)}, u32[]{:S(2)}) async-start(bf16[256,8,256]{2,0,1:T(8,128)(2,1)} %all_to_all.14), calls=%async_computation | async-start | bytes 2097152 | tf_op jit(solution)/shard_map/all_to_all | solution.py:160
  11.6 2.0 fusion.5
  16.6 1.2 slice_select_fusion.dq_ref
  17.8 5.3 %fusion.14 = (f32[2048,64]{1,0:T(8,128)S(1)}, f32[2048,64]{1,0:T(8,128)S(1)}, f32[2048,64]{1,0:T(8,128)}) fusion(f32[64]{0:T(128)S(1)} %multiply_divide_fusion, f32[2048]{0:T(1024)S(1)} %slice_convert_fusion), kind=kLoop, calls=%fused_computation.63 | loop fusion | flops 262144 | bytes 1581312 | tf_op jit(solution)/shard_map/neg | solution.py:40
  23.1 3.9 %all-to-all-done = bf16[256,8,256]{2,0,1:T(8,128)(2,1)S(1)} async-done(((bf16[256,8,256]{2,0,1:T(8,128)(2,1)}), bf16[256,8,256]{2,0,1:T(8,128)(2,1)S(1)}, u32[]{:S(2)}, u32[]{:S(2)}) %all-to-all-start) | async-done | bytes 1048608 | tf_op jit(solution)/shard_map/all_to_all | solution.py:160
  27.1 5.9 %collective-permute-start = (bf16[512,256]{1,0:T(8,128)(2,1)S(1)}, bf16[512,256]{1,0:T(8,128)(2,1)S(1)}, u32[]{:S(2)}, u32[]{:S(2)}) collective-permute-start(bf16[512,256]{1,0:T(8,128)(2,1)S(1)} %bitcast.87), channel_id=1, source_target_pairs={{0,8},{8,16},{16,24},{24,32},{32,40},{40,48},{48,56},{56,64},{64,7... | collective-permute-start | bytes 786440 | tf_op jit(solution)/shard_map/ppermute | solution.py:17
  33.0 3.5 %pad_maximum_fusion = (f32[2048,128]{1,0:T(8,128)}, f32[2048,128]{1,0:T(8,128)}) fusion(f32[2048,64]{1,0:T(8,128)} %get-tuple-element.41, f32[2048,64]{1,0:T(8,128)S(1)} %get-tuple-element.40, f32[2048,64]{1,0:T(8,128)S(1)} %get-tuple-element.39), kind=kLoop, calls=%fused_computation.25 | loop fusion | flops 524288 | bytes 3670016 | tf_op jit(solution)/shard_map/concatenate | solution.py:39
  37.5 6.0 %fusion.7 = (bf16[2560,64]{1,0:T(8,128)(2,1)S(1)}, bf16[2560,64]{1,0:T(8,128)(2,1)S(1)}) fusion(f32[2560,128]{1,0:T(8,128)S(1)} %get-tuple-element.30, f32[2560]{0:T(1024)S(1)} %get-tuple-element.9, f32[64]{0:T(128)S(1)} %multiply_divide_fusion), kind=kLoop, calls=%fused_computation.15 | loop fusion | flops 1474560 | bytes 1976576 | tf_op jit(solution)/shard_map/convert
  43.5 1.2 pad_maximum_fusion.4.k_ref
  44.7 40.2 %shard_map.64 = bf16[16,256,1024]{2,1,0:T(8,128)(2,1)} custom-call(s32[16]{0:T(128)} %get-tuple-element.8.slot_ref, s32[16]{0:T(128)} %get-tuple-element.7.has_ref, bf16[2048,1024]{1,0:T(8,128)(2,1)} %q_ref.1, f32[2048,128]{1,0:T(8,128)} %get-tuple-element.42.cos_ref, f32[2048,128]{1,0:T(8,128)} %get-tuple-element.43.sin_ref, ...), custom_call_target="tpu_custom_call" | custom-call | flops 6442450944 | bytes 9699328 | tf_op jit(solution)/shard_map/pallas_call | solution.py:127
  84.9 5.8 %slice_bitcast_fusion = (bf16[256,1024]{1,0:T(8,128)(2,1)S(1)}, bf16[256,1024]{1,0:T(8,128)(2,1)S(1)}, bf16[256,1024]{1,0:T(8,128)(2,1)S(1)}, bf16[256,1024]{1,0...) fusion(bf16[16,256,1024]{2,1,0:T(8,128)(2,1)} %shard_map.64), kind=kLoop, calls=%fused_computation.32 | loop fusion | bytes 16777216 | tf_op jit(solution)/shard_map/squeeze | solution.py:195
  90.7 5.5 %collective-permute-start.1 = (bf16[256,1024]{1,0:T(8,128)(2,1)}, bf16[256,1024]{1,0:T(8,128)(2,1)}, u32[]{:S(2)}, u32[]{:S(2)}) collective-permute-start(bf16[256,1024]{1,0:T(8,128)(2,1)} %get-tuple-element.25), channel_id=1, source_target_pairs={{0,8},{8,16},{16,24},{24,32},{32,40},{40,48},{48,56},{56,64},{64,7... | collective-permute-start | bytes 1572872 | tf_op jit(solution)/shard_map/ppermute | solution.py:195
  97.0 2.0 collective-permute-start.4
  99.0 4.0 %collective-permute-start.5 = (bf16[256,1024]{1,0:T(8,128)(2,1)}, bf16[256,1024]{1,0:T(8,128)(2,1)S(1)}, u32[]{:S(2)}, u32[]{:S(2)}) collective-permute-start(bf16[256,1024]{1,0:T(8,128)(2,1)} %get-tuple-element.21), channel_id=1, source_target_pairs={{0,40},{8,48},{16,56},{24,64},{32,72},{40,80},{48,88},{56,96},{64,... | collective-permute-start | bytes 1572872 | tf_op jit(solution)/shard_map/ppermute | solution.py:195
  103.1 4.3 %collective-permute-done.1 = bf16[256,1024]{1,0:T(8,128)(2,1)} collective-permute-done((bf16[256,1024]{1,0:T(8,128)(2,1)}, bf16[256,1024]{1,0:T(8,128)(2,1)}, u32[]{:S(2)}, u32[]{:S(2)}) %collective-permute-start.1) | collective-permute-done | bytes 524320 | tf_op jit(solution)/shard_map/ppermute | solution.py:195
  107.3 2.2 collective-permute-start.6
  109.5 1.9 bitcast_dynamic-update-slice_fusion.14
  111.5 7.1 %collective-permute-done.2 = bf16[256,1024]{1,0:T(8,128)(2,1)} collective-permute-done((bf16[256,1024]{1,0:T(8,128)(2,1)}, bf16[256,1024]{1,0:T(8,128)(2,1)}, u32[]{:S(2)}, u32[]{:S(2)}) %collective-permute-start.2) | collective-permute-done | bytes 524320 | tf_op jit(solution)/shard_map/ppermute | solution.py:195
  118.6 1.9 bitcast_dynamic-update-slice_fusion.13
  120.4 4.4 %collective-permute-start.8 = (bf16[256,1024]{1,0:T(8,128)(2,1)}, bf16[256,1024]{1,0:T(8,128)(2,1)S(1)}, u32[]{:S(2)}, u32[]{:S(2)}) collective-permute-start(bf16[256,1024]{1,0:T(8,128)(2,1)} %get-tuple-element.18), channel_id=1, source_target_pairs={{0,64},{8,72},{16,80},{24,88},{32,96},{40,104},{48,112},{56,120},{... | collective-permute-start | bytes 1572872 | tf_op jit(solution)/shard_map/ppermute | solution.py:195
  124.9 1.9 bitcast_dynamic-update-slice_fusion.12
  126.7 25.8 %collective-permute-start.9 = (bf16[256,1024]{1,0:T(8,128)(2,1)}, bf16[256,1024]{1,0:T(8,128)(2,1)S(1)}, u32[]{:S(2)}, u32[]{:S(2)}) collective-permute-start(bf16[256,1024]{1,0:T(8,128)(2,1)} %get-tuple-element.17), channel_id=1, source_target_pairs={{0,72},{8,80},{16,88},{24,96},{32,104},{40,112},{48,120},{56,0},{6... | collective-permute-start | bytes 1572872 | tf_op jit(solution)/shard_map/ppermute | solution.py:195
  153.4 23.1 %collective-permute-start.10 = (bf16[256,1024]{1,0:T(8,128)(2,1)S(1)}, bf16[256,1024]{1,0:T(8,128)(2,1)S(1)}, u32[]{:S(2)}, u32[]{:S(2)}) collective-permute-start(bf16[256,1024]{1,0:T(8,128)(2,1)S(1)} %get-tuple-element.16), channel_id=1, source_target_pairs={{0,80},{8,88},{16,96},{24,104},{32,112},{40,120},{48,0},{56,8},{64... | collective-permute-start | bytes 1572872 | tf_op jit(solution)/shard_map/ppermute | solution.py:195
  177.4 14.5 %collective-permute-done.6 = bf16[256,1024]{1,0:T(8,128)(2,1)S(1)} collective-permute-done((bf16[256,1024]{1,0:T(8,128)(2,1)}, bf16[256,1024]{1,0:T(8,128)(2,1)S(1)}, u32[]{:S(2)}, u32[]{:S(2)}) %collective-permute-start.6) | collective-permute-done | bytes 524320 | tf_op jit(solution)/shard_map/ppermute | solution.py:195
  195.2 8.2 %collective-permute-start.14 = (bf16[256,1024]{1,0:T(8,128)(2,1)S(1)}, bf16[256,1024]{1,0:T(8,128)(2,1)S(1)}, u32[]{:S(2)}, u32[]{:S(2)}) collective-permute-start(bf16[256,1024]{1,0:T(8,128)(2,1)S(1)} %get-tuple-element.12), channel_id=1, source_target_pairs={{0,112},{8,120},{16,0},{24,8},{32,16},{40,24},{48,32},{56,40},{64,... | collective-permute-start | bytes 1572872 | tf_op jit(solution)/shard_map/ppermute | solution.py:195
  204.2 11.1 %collective-permute-start.15 = (bf16[256,1024]{1,0:T(8,128)(2,1)S(1)}, bf16[256,1024]{1,0:T(8,128)(2,1)S(1)}, u32[]{:S(2)}, u32[]{:S(2)}) collective-permute-start(bf16[256,1024]{1,0:T(8,128)(2,1)S(1)} %get-tuple-element.11), channel_id=1, source_target_pairs={{0,120},{8,0},{16,8},{24,16},{32,24},{40,32},{48,40},{56,48},{64,5... | collective-permute-start | bytes 1572872 | tf_op jit(solution)/shard_map/ppermute | solution.py:195
  217.8 6.2 %collective-permute-done.13 = bf16[256,1024]{1,0:T(8,128)(2,1)S(1)} collective-permute-done((bf16[256,1024]{1,0:T(8,128)(2,1)S(1)}, bf16[256,1024]{1,0:T(8,128)(2,1)S(1)}, u32[]{:S(2)}, u32[]{:S(2)}) %collective-permute-start.13) | collective-permute-done | bytes 524320 | tf_op jit(solution)/shard_map/ppermute | solution.py:195
  224.8 10.4 %collective-permute-done.14 = bf16[256,1024]{1,0:T(8,128)(2,1)S(1)} collective-permute-done((bf16[256,1024]{1,0:T(8,128)(2,1)S(1)}, bf16[256,1024]{1,0:T(8,128)(2,1)S(1)}, u32[]{:S(2)}, u32[]{:S(2)}) %collective-permute-start.14) | collective-permute-done | bytes 524320 | tf_op jit(solution)/shard_map/ppermute | solution.py:195
  236.9 6.1 %gather_fusion = bf16[8,256,1024]{2,1,0:T(8,128)(2,1)} fusion(bf16[16,256,1024]{2,1,0:T(8,128)(2,1)} %bitcast_dynamic-update-slice_fusion, s32[1024]{0:T(1024)S(1)} %pad_clamp_fusion), kind=kCustom, calls=%fused_computation | custom fusion | bytes 8388640 | tf_op jit(solution)/shard_map/jit(_take)/gather | solution.py:203
  243.1 3.9 %bitcast_select_fusion = bf16[2048,1024]{1,0:T(8,128)(2,1)} fusion(bf16[8,256,1024]{2,1,0:T(8,128)(2,1)} %gather_fusion, pred[2048]{0:T(1024)(128)(4,1)S(1)} %broadcast_in_dim.68), kind=kLoop, calls=%fused_computation.1 | loop fusion | flops 2097152 | bytes 8390656 | tf_op jit(solution)/shard_map/jit(_take)/select_n | solution.py:203
  (69 shorter events, 18.4 us)
Async XLA Ops:
  0.0 11.2 %copy-start.1 = (s32[128]{0:T(128)S(1)}, s32[128]{0:T(128)}, u32[]{:S(2)}) copy-start(s32[128]{0:T(128)} %param.10) | copy-start | bytes 1540
  0.0 14.9 %copy-start.2 = (f32[64]{0:T(128)S(1)}, f32[64]{0:T(128)}, u32[]{:S(2)}) copy-start(f32[64]{0:T(128)} %param.9) | copy-start | bytes 772
  0.0 14.9 %copy-start = (s32[16,8]{0,1:T(8,128)S(1)}, s32[16,8]{0,1:T(8,128)}, u32[]{:S(2)}) copy-start(s32[16,8]{0,1:T(8,128)} %param.11) | copy-start | bytes 1540
  5.0 22.1 %all-to-all-start = ((bf16[256,8,256]{2,0,1:T(8,128)(2,1)}), bf16[256,8,256]{2,0,1:T(8,128)(2,1)S(1)}, u32[]{:S(2)}, u32[]{:S(2)}) async-start(bf16[256,8,256]{2,0,1:T(8,128)(2,1)} %all_to_all.14), calls=%async_computation | async-start | bytes 2097152 | tf_op jit(solution)/shard_map/all_to_all | solution.py:160
  27.1 9.4 %collective-permute-start = (bf16[512,256]{1,0:T(8,128)(2,1)S(1)}, bf16[512,256]{1,0:T(8,128)(2,1)S(1)}, u32[]{:S(2)}, u32[]{:S(2)}) collective-permute-start(bf16[512,256]{1,0:T(8,128)(2,1)S(1)} %bitcast.87), channel_id=1, source_target_pairs={{0,8},{8,16},{16,24},{24,32},{32,40},{40,48},{48,56},{56,64},{64,7... | collective-permute-start | bytes 786440 | tf_op jit(solution)/shard_map/ppermute | solution.py:17
  90.7 16.7 %collective-permute-start.1 = (bf16[256,1024]{1,0:T(8,128)(2,1)}, bf16[256,1024]{1,0:T(8,128)(2,1)}, u32[]{:S(2)}, u32[]{:S(2)}) collective-permute-start(bf16[256,1024]{1,0:T(8,128)(2,1)} %get-tuple-element.25), channel_id=1, source_target_pairs={{0,8},{8,16},{16,24},{24,32},{32,40},{40,48},{48,56},{56,64},{64,7... | collective-permute-start | bytes 1572872 | tf_op jit(solution)/shard_map/ppermute | solution.py:195
  96.1 22.4 %collective-permute-start.2 = (bf16[256,1024]{1,0:T(8,128)(2,1)}, bf16[256,1024]{1,0:T(8,128)(2,1)}, u32[]{:S(2)}, u32[]{:S(2)}) collective-permute-start(bf16[256,1024]{1,0:T(8,128)(2,1)} %get-tuple-element.24), channel_id=1, source_target_pairs={{0,16},{8,24},{16,32},{24,40},{32,48},{40,56},{48,64},{56,72},{64,... | collective-permute-start | bytes 1572872 | tf_op jit(solution)/shard_map/ppermute | solution.py:195
  96.2 24.3 %collective-permute-start.3 = (bf16[256,1024]{1,0:T(8,128)(2,1)}, bf16[256,1024]{1,0:T(8,128)(2,1)}, u32[]{:S(2)}, u32[]{:S(2)}) collective-permute-start(bf16[256,1024]{1,0:T(8,128)(2,1)} %get-tuple-element.23), channel_id=1, source_target_pairs={{0,24},{8,32},{16,40},{24,48},{32,56},{40,64},{48,72},{56,80},{64,... | collective-permute-start | bytes 1572872 | tf_op jit(solution)/shard_map/ppermute | solution.py:195
  97.0 29.7 %collective-permute-start.4 = (bf16[256,1024]{1,0:T(8,128)(2,1)}, bf16[256,1024]{1,0:T(8,128)(2,1)S(1)}, u32[]{:S(2)}, u32[]{:S(2)}) collective-permute-start(bf16[256,1024]{1,0:T(8,128)(2,1)} %get-tuple-element.22), channel_id=1, source_target_pairs={{0,32},{8,40},{16,48},{24,56},{32,64},{40,72},{48,80},{56,88},{64,... | collective-permute-start | bytes 1572872 | tf_op jit(solution)/shard_map/ppermute | solution.py:195
  99.0 54.4 %collective-permute-start.5 = (bf16[256,1024]{1,0:T(8,128)(2,1)}, bf16[256,1024]{1,0:T(8,128)(2,1)S(1)}, u32[]{:S(2)}, u32[]{:S(2)}) collective-permute-start(bf16[256,1024]{1,0:T(8,128)(2,1)} %get-tuple-element.21), channel_id=1, source_target_pairs={{0,40},{8,48},{16,56},{24,64},{32,72},{40,80},{48,88},{56,96},{64,... | collective-permute-start | bytes 1572872 | tf_op jit(solution)/shard_map/ppermute | solution.py:195
  107.3 84.6 %collective-permute-start.6 = (bf16[256,1024]{1,0:T(8,128)(2,1)}, bf16[256,1024]{1,0:T(8,128)(2,1)S(1)}, u32[]{:S(2)}, u32[]{:S(2)}) collective-permute-start(bf16[256,1024]{1,0:T(8,128)(2,1)} %get-tuple-element.20), channel_id=1, source_target_pairs={{0,48},{8,56},{16,64},{24,72},{32,80},{40,88},{48,96},{56,104},{64... | collective-permute-start | bytes 1572872 | tf_op jit(solution)/shard_map/ppermute | solution.py:195
  118.6 74.9 %collective-permute-start.7 = (bf16[256,1024]{1,0:T(8,128)(2,1)}, bf16[256,1024]{1,0:T(8,128)(2,1)S(1)}, u32[]{:S(2)}, u32[]{:S(2)}) collective-permute-start(bf16[256,1024]{1,0:T(8,128)(2,1)} %get-tuple-element.19), channel_id=1, source_target_pairs={{0,56},{8,64},{16,72},{24,80},{32,88},{40,96},{48,104},{56,112},{6... | collective-permute-start | bytes 1572872 | tf_op jit(solution)/shard_map/ppermute | solution.py:195
  120.4 73.9 %collective-permute-start.8 = (bf16[256,1024]{1,0:T(8,128)(2,1)}, bf16[256,1024]{1,0:T(8,128)(2,1)S(1)}, u32[]{:S(2)}, u32[]{:S(2)}) collective-permute-start(bf16[256,1024]{1,0:T(8,128)(2,1)} %get-tuple-element.18), channel_id=1, source_target_pairs={{0,64},{8,72},{16,80},{24,88},{32,96},{40,104},{48,112},{56,120},{... | collective-permute-start | bytes 1572872 | tf_op jit(solution)/shard_map/ppermute | solution.py:195
  126.7 68.5 %collective-permute-start.9 = (bf16[256,1024]{1,0:T(8,128)(2,1)}, bf16[256,1024]{1,0:T(8,128)(2,1)S(1)}, u32[]{:S(2)}, u32[]{:S(2)}) collective-permute-start(bf16[256,1024]{1,0:T(8,128)(2,1)} %get-tuple-element.17), channel_id=1, source_target_pairs={{0,72},{8,80},{16,88},{24,96},{32,104},{40,112},{48,120},{56,0},{6... | collective-permute-start | bytes 1572872 | tf_op jit(solution)/shard_map/ppermute | solution.py:195
  153.4 50.8 %collective-permute-start.10 = (bf16[256,1024]{1,0:T(8,128)(2,1)S(1)}, bf16[256,1024]{1,0:T(8,128)(2,1)S(1)}, u32[]{:S(2)}, u32[]{:S(2)}) collective-permute-start(bf16[256,1024]{1,0:T(8,128)(2,1)S(1)} %get-tuple-element.16), channel_id=1, source_target_pairs={{0,80},{8,88},{16,96},{24,104},{32,112},{40,120},{48,0},{56,8},{64... | collective-permute-start | bytes 1572872 | tf_op jit(solution)/shard_map/ppermute | solution.py:195
  191.9 24.2 %collective-permute-start.11 = (bf16[256,1024]{1,0:T(8,128)(2,1)S(1)}, bf16[256,1024]{1,0:T(8,128)(2,1)S(1)}, u32[]{:S(2)}, u32[]{:S(2)}) collective-permute-start(bf16[256,1024]{1,0:T(8,128)(2,1)S(1)} %get-tuple-element.15), channel_id=1, source_target_pairs={{0,88},{8,96},{16,104},{24,112},{32,120},{40,0},{48,8},{56,16},{64... | collective-permute-start | bytes 1572872 | tf_op jit(solution)/shard_map/ppermute | solution.py:195
  193.5 23.4 %collective-permute-start.12 = (bf16[256,1024]{1,0:T(8,128)(2,1)S(1)}, bf16[256,1024]{1,0:T(8,128)(2,1)S(1)}, u32[]{:S(2)}, u32[]{:S(2)}) collective-permute-start(bf16[256,1024]{1,0:T(8,128)(2,1)S(1)} %get-tuple-element.14), channel_id=1, source_target_pairs={{0,96},{8,104},{16,112},{24,120},{32,0},{40,8},{48,16},{56,24},{64... | collective-permute-start | bytes 1572872 | tf_op jit(solution)/shard_map/ppermute | solution.py:195
  194.3 29.6 %collective-permute-start.13 = (bf16[256,1024]{1,0:T(8,128)(2,1)S(1)}, bf16[256,1024]{1,0:T(8,128)(2,1)S(1)}, u32[]{:S(2)}, u32[]{:S(2)}) collective-permute-start(bf16[256,1024]{1,0:T(8,128)(2,1)S(1)} %get-tuple-element.13), channel_id=1, source_target_pairs={{0,104},{8,112},{16,120},{24,0},{32,8},{40,16},{48,24},{56,32},{64... | collective-permute-start | bytes 1572872 | tf_op jit(solution)/shard_map/ppermute | solution.py:195
  195.2 40.0 %collective-permute-start.14 = (bf16[256,1024]{1,0:T(8,128)(2,1)S(1)}, bf16[256,1024]{1,0:T(8,128)(2,1)S(1)}, u32[]{:S(2)}, u32[]{:S(2)}) collective-permute-start(bf16[256,1024]{1,0:T(8,128)(2,1)S(1)} %get-tuple-element.12), channel_id=1, source_target_pairs={{0,112},{8,120},{16,0},{24,8},{32,16},{40,24},{48,32},{56,40},{64,... | collective-permute-start | bytes 1572872 | tf_op jit(solution)/shard_map/ppermute | solution.py:195
  204.2 31.8 %collective-permute-start.15 = (bf16[256,1024]{1,0:T(8,128)(2,1)S(1)}, bf16[256,1024]{1,0:T(8,128)(2,1)S(1)}, u32[]{:S(2)}, u32[]{:S(2)}) collective-permute-start(bf16[256,1024]{1,0:T(8,128)(2,1)S(1)} %get-tuple-element.11), channel_id=1, source_target_pairs={{0,120},{8,0},{16,8},{24,16},{32,24},{40,32},{48,40},{56,48},{64,5... | collective-permute-start | bytes 1572872 | tf_op jit(solution)/shard_map/ppermute | solution.py:195

commit v2 on v0

--- a/solution.py
+++ b/solution.py
@@ -95,8 +95,9 @@
             o_ref[0, :, cols] = (o / l).astype(o_ref.dtype)
 
 
-def attend(slot, has, q, cos_t, sin_t, k_ext, v_ext, doc_q, doc_k, n_dest, head_dim):
-    rows, width = q.shape
+def attend(slot, has, q, cos_t, sin_t, k_ext, v_ext, doc_q, doc_k, n_dest, head_dim, group, groups):
+    rows, all_width = q.shape
+    width = all_width // groups
     per_dev, block_rows, _ = doc_q.shape
     span = doc_k.shape[2]
     ext_rows = k_ext.shape[0]
@@ -114,7 +115,7 @@
         num_scalar_prefetch=2,
         grid=(n_dest,),
         in_specs=[
-            pl.BlockSpec((block_rows, width), lambda d, s, h: (s[d], 0)),
+            pl.BlockSpec((block_rows, width), lambda d, s, h: (s[d], group)),
             pl.BlockSpec((block_rows, head_dim), lambda d, s, h: (s[d], 0)),
             pl.BlockSpec((block_rows, head_dim), lambda d, s, h: (s[d], 0)),
             pl.BlockSpec((ext_rows, head_dim), lambda d, s, h: (0, 0)),
@@ -131,7 +132,8 @@
         cost_estimate=pl.CostEstimate(
             flops=flops,
             transcendentals=per_dev * heads * block_rows * span,
-            bytes_accessed=2 * rows * width * 2 + 2 * ext_rows * head_dim * 2,
+            bytes_accessed=rows * width * 2 + n_dest * block_rows * width * 2
+            + 2 * ext_rows * head_dim * 2,
         ),
     )(slot, has, q, cos_t, sin_t, k_ext, v_ext, doc_q, doc_k)
 
@@ -169,8 +171,11 @@
     doc_ext, off_ext = doc_tables(doc_lengths, pos_ext)
     doc_ext = jnp.where(pos_ext >= 0, doc_ext, -1)
     inverse = inverse_freqs(rope_factors, head_dim)
-    k_ext = rotate(k_raw.astype(jnp.float32), off_ext, inverse).astype(jnp.bfloat16)
-    cos_t, sin_t = rotation_tables(off_ext[tail_rows:], inverse)
+    cos_ext, sin_ext = rotation_tables(off_ext, inverse)
+    k_f = k_raw.astype(jnp.float32)
+    k_ext = (k_f * cos_ext + jnp.roll(k_f, head_dim // 2, axis=1) * sin_ext).astype(jnp.bfloat16)
+    cos_t = cos_ext[tail_rows:]
+    sin_t = sin_ext[tail_rows:]
 
     doc_q = doc_ext[tail_rows:].reshape(per_dev, block_rows, 1)
     doc_k = jnp.stack(
@@ -185,16 +190,20 @@
         jnp.where(match, jnp.arange(per_dev, dtype=jnp.int32)[None, :], 0), axis=1, dtype=jnp.int32
     )
 
-    send = attend(
-        slot, has, queries, cos_t, sin_t, k_ext, v_ext, doc_q, doc_k, ctx_size, head_dim
-    )
-    arrived = lax.all_to_all(send, "ctx", split_axis=0, concat_axis=0, tiled=True)
+    groups = 4
+    arrived = []
+    for group in range(groups):
+        send = attend(
+            slot, has, queries, cos_t, sin_t, k_ext, v_ext, doc_q, doc_k, ctx_size, head_dim,
+            group, groups,
+        )
+        arrived.append(lax.all_to_all(send, "ctx", split_axis=0, concat_axis=0, tiled=True))
 
     sources_match = owner_map == ctx_index
     my_sources = jnp.sum(
         jnp.where(sources_match, devices[:, None], 0), axis=0, dtype=jnp.int32
     )
-    finished = jnp.take(arrived, my_sources, axis=0)
+    finished = jnp.concatenate([jnp.take(a, my_sources, axis=0) for a in arrived], axis=-1)
     return finished.reshape(row_count, queries.shape[1])
 
 

time: 235 us -> 210 us (0.89)
  waiting for transfers between devices: 135 us -> 52.5 us
  Pallas kernels: 40.6 us -> 76.5 us
  starting transfers between devices: 21.2 us -> 37.3 us
  local copies, waits for them, and re-layouts: 12.3 us -> 17.6 us
    all_to_all x1 -> x4, waiting for transfers between devices: 131 us -> 51 us  [local(): lax.all_to_all(send, 'ctx', split_axis=0, concat_axis=0, tiled=True)]
    pallas_call x1 -> x4, Pallas kernels: 40.6 us -> 76.5 us  [attend(): pl.pallas_call(kernel, grid_spec=grid_spec, out_shape=jax.ShapeDtypeStruc...]
    all_to_all x1 -> x4, starting transfers between devices: 8.98 us -> 25.1 us  [local(): lax.all_to_all(send, 'ctx', split_axis=0, concat_axis=0, tiled=True)]
    sin x0 -> x1, other arithmetic: none -> 6.01 us  [rotation_tables(): sine = jnp.sin(angles)]
    another operation x3 -> x2, other arithmetic: 6.24 us -> 0.27 us
    neg x1 -> x0, other arithmetic: 5.34 us -> none  [rotation_tables(): -sine]
    convert_element_type x1, other arithmetic: 0.01 us -> 3.08 us  [local(): (k_f * cos_ext + jnp.roll(k_f, head_dim // 2, axis=1) * sin_ext).astype(j...]
    all_to_all x1, waiting for transfers between devices: 4.03 us -> 1 us  [local(): kv = lax.all_to_all(kv, 'tp', split_axis=1, concat_axis=0, tiled=True)]
  transfers between devices with their start and end apart: 3 -> 6, of which waited for: 2 -> 6; matrix products, arithmetic and copies ran while one was open for 7% -> 11% of each run, Pallas kernels for 0% -> 28%
where the time goes in v2:
time: 210 us; the launch traced here: 208 us
  Pallas kernels  76.5 us (36%)
  waiting for transfers between devices  52.5 us (25%)
  starting transfers between devices  37.3 us (18%)
  other arithmetic  23.9 us (11%)
  local copies, waits for them, and re-layouts  17.6 us (8%)
    pallas_call x4, Pallas kernels, attend(): pl.pallas_call(kernel, grid_spec=grid_spec, out_shape=jax.ShapeDtypeStruc...  76.5 us
    all_to_all x4, waiting for transfers between devices, local(): lax.all_to_all(send, 'ctx', split_axis=0, concat_axis=0, tiled=True)  51 us
    all_to_all x4, starting transfers between devices, local(): lax.all_to_all(send, 'ctx', split_axis=0, concat_axis=0, tiled=True)  25.1 us
    gather x4, local copies, waits for them, and re-layouts, local(): jnp.take(a, my_sources, axis=0)  8.2 us
    all_to_all x1, starting transfers between devices, local(): kv = lax.all_to_all(kv, 'tp', split_axis=1, concat_axis=0, tiled=True)  6.32 us
    sin x1, other arithmetic, rotation_tables(): sine = jnp.sin(angles)  6.01 us
    ppermute x1, starting transfers between devices, passed_along(): return lax.ppermute(shard, axis, pairs)  5.89 us
  transfers between devices with their start and end apart: 6, of which 6 were waited for; matrix products, arithmetic and copies ran while one was open for 11% of the time, Pallas kernels for 28%

profile of v2, /device:TPU:1, one launch (start us, length us, event | category | flops | bytes accessed | tf_op | source)
XLA Modules:
  0.0 208.0 jit_solution(12889429688029981973)
XLA Ops:
  0.0 1.2 copy.15
  1.4 1.1 copy.13
  2.5 1.5 all_to_all.26
  4.0 6.3 %all-to-all-start = ((bf16[256,8,256]{2,0,1:T(8,128)(2,1)}), bf16[256,8,256]{2,0,1:T(8,128)(2,1)}, u32[]{:S(2)}, u32[]{:S(2)}) async-start(bf16[256,8,256]{2,0,1:T(8,128)(2,1)} %all_to_all.26), calls=%async_computation | async-start | bytes 2097152 | tf_op jit(solution)/shard_map/all_to_all | solution.py:162
  10.8 2.0 fusion.1
  12.8 6.0 %multiply_sine_fusion = (f32[2560,64]{1,0:T(8,128)S(1)}, f32[2560,64]{1,0:T(8,128)S(1)}, f32[2560,64]{1,0:T(8,128)}) fusion(f32[64]{0:T(128)S(1)} %multiply_divide_fusion, f32[2560]{0:T(1024)S(1)} %get-tuple-element.29), kind=kLoop, calls=%fused_computation.5 | loop fusion | flops 327680 | bytes 1976576 | tf_op jit(solution)/shard_map/sin | solution.py:37
  18.8 2.2 %reduce_sum.53 = s32[10,256,1]{2,1,0:T(8,128)} reshape(s32[2560]{0:T(1024)S(1)} %get-tuple-element.6) | data formatting | bytes 20480 | tf_op jit(solution)/shard_map/reduce_sum | solution.py:23
  21.2 3.0 %fusion.5.cos_ref = f32[2048,128]{1,0:T(8,128)} fusion(f32[2560,64]{1,0:T(8,128)} %get-tuple-element.16), kind=kLoop, calls=%fused_computation.22 | loop fusion | flops 262144 | bytes 1703936 | tf_op jit(solution)/shard_map/concatenate | solution.py:39
  24.2 1.1 slice_select_fusion.dq_ref
  25.3 1.0 all-to-all-done
  26.3 1.0 slice.83
  27.3 5.9 %collective-permute-start = (bf16[512,256]{1,0:T(8,128)(2,1)S(1)}, bf16[512,256]{1,0:T(8,128)(2,1)S(1)}, u32[]{:S(2)}, u32[]{:S(2)}) collective-permute-start(bf16[512,256]{1,0:T(8,128)(2,1)S(1)} %bitcast.20), channel_id=1, source_target_pairs={{0,8},{8,16},{16,24},{24,32},{32,40},{40,48},{48,56},{56,64},{64,7... | collective-permute-start | bytes 786440 | tf_op jit(solution)/shard_map/ppermute | solution.py:17
  34.5 1.4 fusion.4.sin_ref
  36.5 2.2 %pad_maximum_fusion.2 = (bf16[2560,128]{1,0:T(8,128)(2,1)}, f32[2560,128]{1,0:T(8,128)S(1)}) fusion(bf16[2048,256]{1,0:T(8,128)(2,1)} %bitcast.3, bf16[512,256]{1,0:T(8,128)(2,1)S(1)} %collective-permute-done), kind=kLoop, calls=%fused_computation.35 | loop fusion | flops 2621440 | bytes 3276800 | tf_op jit(solution)/shard_map/concatenate | solution.py:164
  40.0 3.1 %fusion.3.k_ref = bf16[2560,128]{1,0:T(8,128)(2,1)} fusion(f32[2560,64]{1,0:T(8,128)S(1)} %get-tuple-element.13, f32[2560,64]{1,0:T(8,128)S(1)} %get-tuple-element.12, f32[2560,64]{1,0:T(8,128)S(1)} %copy-done, f32[2560,64]{1,0:T(8,128)S(1)} %get-tuple-element.14, f32[2560,64]{1,0:T(8,128)S(1)} %get-tuple-element.15, bf16[2048,256]{1,0:T(8,128)(2,1)} %bitcast.3, ...), kind=kLoop, calls=%fused_computation.13 | loop fusion | flops 3604480 | bytes 5242880 | tf_op jit(solution)/shard_map/convert_element_type | solution.py:176
  43.0 19.1 %shard_map.67 = bf16[16,256,256]{2,1,0:T(8,128)(2,1)} custom-call(s32[16]{0:T(128)} %get-tuple-element.9.slot_ref, s32[16]{0:T(128)} %get-tuple-element.8.has_ref, bf16[2048,1024]{1,0:T(8,128)(2,1)} %q_ref.7, f32[2048,128]{1,0:T(8,128)} %fusion.5.cos_ref, f32[2048,128]{1,0:T(8,128)} %fusion.4.sin_ref, bf16[2560,128]{1,0:T(8,128)(2,1)} %fusion.3.k_ref, ...), custom_call_target="tpu_custom_call" | custom-call | flops 1610612736 | bytes 4456448 | tf_op jit(solution)/shard_map/pallas_call | solution.py:128
  62.2 7.7 %all-to-all-start.4 = ((bf16[16,256,256]{2,1,0:T(8,128)(2,1)}), bf16[16,256,256]{2,1,0:T(8,128)(2,1)S(1)}, u32[]{:S(2)}, u32[]{:S(2)}) async-start(bf16[16,256,256]{2,1,0:T(8,128)(2,1)} %shard_map.67), calls=%async_computation.4 | async-start | bytes 4194304 | tf_op jit(solution)/shard_map/all_to_all | solution.py:200
  69.9 19.1 %shard_map.66 = bf16[16,256,256]{2,1,0:T(8,128)(2,1)} custom-call(s32[16]{0:T(128)} %get-tuple-element.9.slot_ref, s32[16]{0:T(128)} %get-tuple-element.8.has_ref, bf16[2048,1024]{1,0:T(8,128)(2,1)} %q_ref.7, f32[2048,128]{1,0:T(8,128)} %fusion.5.cos_ref, f32[2048,128]{1,0:T(8,128)} %fusion.4.sin_ref, bf16[2560,128]{1,0:T(8,128)(2,1)} %fusion.3.k_ref, ...), custom_call_target="tpu_custom_call" | custom-call | flops 1610612736 | bytes 4456448 | tf_op jit(solution)/shard_map/pallas_call | solution.py:128
  89.0 9.2 %all-to-all-done.4 = bf16[16,256,256]{2,1,0:T(8,128)(2,1)S(1)} async-done(((bf16[16,256,256]{2,1,0:T(8,128)(2,1)}), bf16[16,256,256]{2,1,0:T(8,128)(2,1)S(1)}, u32[]{:S(2)}, u32[]{:S(2)}) %all-to-all-start.4) | async-done | bytes 2097184 | tf_op jit(solution)/shard_map/all_to_all | solution.py:200
  98.2 5.8 %all-to-all-start.3 = ((bf16[16,256,256]{2,1,0:T(8,128)(2,1)}), bf16[16,256,256]{2,1,0:T(8,128)(2,1)}, u32[]{:S(2)}, u32[]{:S(2)}) async-start(bf16[16,256,256]{2,1,0:T(8,128)(2,1)} %shard_map.66), calls=%async_computation.3 | async-start | bytes 4194304 | tf_op jit(solution)/shard_map/all_to_all | solution.py:200
  104.0 19.1 %shard_map.64 = bf16[16,256,256]{2,1,0:T(8,128)(2,1)} custom-call(s32[16]{0:T(128)} %get-tuple-element.9.slot_ref, s32[16]{0:T(128)} %get-tuple-element.8.has_ref, bf16[2048,1024]{1,0:T(8,128)(2,1)} %q_ref.7, f32[2048,128]{1,0:T(8,128)} %fusion.5.cos_ref, f32[2048,128]{1,0:T(8,128)} %fusion.4.sin_ref, bf16[2560,128]{1,0:T(8,128)(2,1)} %fusion.3.k_ref, ...), custom_call_target="tpu_custom_call" | custom-call | flops 1610612736 | bytes 4456448 | tf_op jit(solution)/shard_map/pallas_call | solution.py:128
  123.1 9.3 %all-to-all-done.3 = bf16[16,256,256]{2,1,0:T(8,128)(2,1)} async-done(((bf16[16,256,256]{2,1,0:T(8,128)(2,1)}), bf16[16,256,256]{2,1,0:T(8,128)(2,1)}, u32[]{:S(2)}, u32[]{:S(2)}) %all-to-all-start.3) | async-done | bytes 2097184 | tf_op jit(solution)/shard_map/all_to_all | solution.py:200
  132.4 5.8 %all-to-all-start.1 = ((bf16[16,256,256]{2,1,0:T(8,128)(2,1)}), bf16[16,256,256]{2,1,0:T(8,128)(2,1)}, u32[]{:S(2)}, u32[]{:S(2)}) async-start(bf16[16,256,256]{2,1,0:T(8,128)(2,1)} %shard_map.64), calls=%async_computation.1 | async-start | bytes 4194304 | tf_op jit(solution)/shard_map/all_to_all | solution.py:200
  138.2 19.1 %shard_map.65 = bf16[16,256,256]{2,1,0:T(8,128)(2,1)} custom-call(s32[16]{0:T(128)} %get-tuple-element.9.slot_ref, s32[16]{0:T(128)} %get-tuple-element.8.has_ref, bf16[2048,1024]{1,0:T(8,128)(2,1)} %q_ref.7, f32[2048,128]{1,0:T(8,128)} %fusion.5.cos_ref, f32[2048,128]{1,0:T(8,128)} %fusion.4.sin_ref, bf16[2560,128]{1,0:T(8,128)(2,1)} %fusion.3.k_ref, ...), custom_call_target="tpu_custom_call" | custom-call | flops 1610612736 | bytes 4456448 | tf_op jit(solution)/shard_map/pallas_call | solution.py:128
  157.4 9.3 %all-to-all-done.1 = bf16[16,256,256]{2,1,0:T(8,128)(2,1)} async-done(((bf16[16,256,256]{2,1,0:T(8,128)(2,1)}), bf16[16,256,256]{2,1,0:T(8,128)(2,1)}, u32[]{:S(2)}, u32[]{:S(2)}) %all-to-all-start.1) | async-done | bytes 2097184 | tf_op jit(solution)/shard_map/all_to_all | solution.py:200
  166.7 5.8 %all-to-all-start.2 = ((bf16[16,256,256]{2,1,0:T(8,128)(2,1)}), bf16[16,256,256]{2,1,0:T(8,128)(2,1)}, u32[]{:S(2)}, u32[]{:S(2)}) async-start(bf16[16,256,256]{2,1,0:T(8,128)(2,1)} %shard_map.65), calls=%async_computation.2 | async-start | bytes 4194304 | tf_op jit(solution)/shard_map/all_to_all | solution.py:200
  173.2 2.2 %gather_fusion.2 = bf16[8,256,256]{2,1,0:T(8,128)(2,1)S(1)} fusion(bf16[16,256,256]{2,1,0:T(8,128)(2,1)} %all-to-all-done.3, s32[1024]{0:T(1024)S(1)} %pad_clamp_fusion), kind=kCustom, calls=%fused_computation.2.clone | custom fusion | bytes 2097184 | tf_op jit(solution)/shard_map/jit(_take)/gather | solution.py:206
  175.4 2.2 %gather_fusion = bf16[8,256,256]{2,1,0:T(8,128)(2,1)S(1)} fusion(bf16[16,256,256]{2,1,0:T(8,128)(2,1)} %all-to-all-done.1, s32[1024]{0:T(1024)S(1)} %pad_clamp_fusion), kind=kCustom, calls=%fused_computation.clone | custom fusion | bytes 2097184 | tf_op jit(solution)/shard_map/jit(_take)/gather | solution.py:206
  177.7 23.2 %all-to-all-done.2 = bf16[16,256,256]{2,1,0:T(8,128)(2,1)} async-done(((bf16[16,256,256]{2,1,0:T(8,128)(2,1)}), bf16[16,256,256]{2,1,0:T(8,128)(2,1)}, u32[]{:S(2)}, u32[]{:S(2)}) %all-to-all-start.2) | async-done | bytes 2097184 | tf_op jit(solution)/shard_map/all_to_all | solution.py:200
  200.9 3.2 %gather_fusion.1 = bf16[8,256,256]{2,1,0:T(8,128)(2,1)} fusion(bf16[16,256,256]{2,1,0:T(8,128)(2,1)} %all-to-all-done.2, s32[1024]{0:T(1024)S(1)} %pad_clamp_fusion), kind=kCustom, calls=%fused_computation.1.clone | custom fusion | bytes 2097184 | tf_op jit(solution)/shard_map/jit(_take)/gather | solution.py:206
  204.1 1.7 broadcast_select_fusion.3
  205.7 2.3 %pad_maximum_fusion = bf16[8,256,1024]{2,1,0:T(8,128)(2,1)} fusion(bf16[8,256,256]{2,1,0:T(8,128)(2,1)S(1)} %get-tuple-element.28, bf16[8,256,256]{2,1,0:T(8,128)(2,1)S(1)} %get-tuple-element.27, bf16[8,256,256]{2,1,0:T(8,128)(2,1)S(1)} %get-tuple-element.26, bf16[8,256,256]{2,1,0:T(8,128)(2,1)S(1)} %get-tuple-element.25), kind=kLoop, calls=%fused_computation.4 | loop fusion | flops 16777216 | bytes 8388608 | tf_op jit(solution)/shard_map/concatenate | solution.py:206
  (40 shorter events, 4.7 us)
Async XLA Ops:
  0.0 1.2 copy-start.2
  4.0 6.3 %copy-start.5 = (f32[64]{0:T(128)S(1)}, f32[64]{0:T(128)}, u32[]{:S(2)}) copy-start(f32[64]{0:T(128)} %param.11) | copy-start | bytes 772
  4.0 6.4 %copy-start.4 = (s32[128]{0:T(128)S(1)}, s32[128]{0:T(128)}, u32[]{:S(2)}) copy-start(s32[128]{0:T(128)} %param.12) | copy-start | bytes 1540
  4.0 22.3 %all-to-all-start = ((bf16[256,8,256]{2,0,1:T(8,128)(2,1)}), bf16[256,8,256]{2,0,1:T(8,128)(2,1)}, u32[]{:S(2)}, u32[]{:S(2)}) async-start(bf16[256,8,256]{2,0,1:T(8,128)(2,1)} %all_to_all.26), calls=%async_computation | async-start | bytes 2097152 | tf_op jit(solution)/shard_map/all_to_all | solution.py:162
  18.8 2.2 %copy-start.3 = (s32[16,8]{0,1:T(8,128)S(1)}, s32[16,8]{0,1:T(8,128)}, u32[]{:S(2)}) copy-start(s32[16,8]{0,1:T(8,128)} %param.13) | copy-start | bytes 1540
  21.0 3.2 %copy-start.1 = (s32[10,256,1]{2,1,0:T(8,128)S(1)}, s32[10,256,1]{2,1,0:T(8,128)}, u32[]{:S(2)}) copy-start(s32[10,256,1]{2,1,0:T(8,128)} %reduce_sum.53) | copy-start | bytes 30724
  27.3 9.2 %collective-permute-start = (bf16[512,256]{1,0:T(8,128)(2,1)S(1)}, bf16[512,256]{1,0:T(8,128)(2,1)S(1)}, u32[]{:S(2)}, u32[]{:S(2)}) collective-permute-start(bf16[512,256]{1,0:T(8,128)(2,1)S(1)} %bitcast.20), channel_id=1, source_target_pairs={{0,8},{8,16},{16,24},{24,32},{32,40},{40,48},{48,56},{56,64},{64,7... | collective-permute-start | bytes 786440 | tf_op jit(solution)/shard_map/ppermute | solution.py:17
  38.6 1.3 copy-start
  62.2 36.0 %all-to-all-start.4 = ((bf16[16,256,256]{2,1,0:T(8,128)(2,1)}), bf16[16,256,256]{2,1,0:T(8,128)(2,1)S(1)}, u32[]{:S(2)}, u32[]{:S(2)}) async-start(bf16[16,256,256]{2,1,0:T(8,128)(2,1)} %shard_map.67), calls=%async_computation.4 | async-start | bytes 4194304 | tf_op jit(solution)/shard_map/all_to_all | solution.py:200
  98.2 34.2 %all-to-all-start.3 = ((bf16[16,256,256]{2,1,0:T(8,128)(2,1)}), bf16[16,256,256]{2,1,0:T(8,128)(2,1)}, u32[]{:S(2)}, u32[]{:S(2)}) async-start(bf16[16,256,256]{2,1,0:T(8,128)(2,1)} %shard_map.66), calls=%async_computation.3 | async-start | bytes 4194304 | tf_op jit(solution)/shard_map/all_to_all | solution.py:200
  132.4 34.2 %all-to-all-start.1 = ((bf16[16,256,256]{2,1,0:T(8,128)(2,1)}), bf16[16,256,256]{2,1,0:T(8,128)(2,1)}, u32[]{:S(2)}, u32[]{:S(2)}) async-start(bf16[16,256,256]{2,1,0:T(8,128)(2,1)} %shard_map.64), calls=%async_computation.1 | async-start | bytes 4194304 | tf_op jit(solution)/shard_map/all_to_all | solution.py:200
  166.7 34.2 %all-to-all-start.2 = ((bf16[16,256,256]{2,1,0:T(8,128)(2,1)}), bf16[16,256,256]{2,1,0:T(8,128)(2,1)}, u32[]{:S(2)}, u32[]{:S(2)}) async-start(bf16[16,256,256]{2,1,0:T(8,128)(2,1)} %shard_map.65), calls=%async_computation.2 | async-start | bytes 4194304 | tf_op jit(solution)/shard_map/all_to_all | solution.py:200

commit v3 on v2

--- a/solution.py
+++ b/solution.py
@@ -31,14 +31,14 @@
     return 1.0 / (factors * jnp.power(jnp.float32(THETA), exponent))
 
 
-def rotation_tables(offsets, inverse):
-    angles = offsets.astype(jnp.float32)[:, None] * inverse[None, :]
+def rotation_tables(offsets, inverse, distinct):
+    angles = jnp.arange(distinct, dtype=jnp.int32).astype(jnp.float32)[:, None] * inverse[None, :]
     cosine = jnp.cos(angles)
     sine = jnp.sin(angles)
-    return (
-        jnp.concatenate([cosine, cosine], axis=1),
-        jnp.concatenate([-sine, sine], axis=1),
-    )
+    table = jnp.concatenate([cosine, cosine, -sine, sine], axis=1)
+    rows = jnp.take(table, jnp.clip(offsets, 0, distinct - 1), axis=0, mode="clip")
+    half = 2 * inverse.shape[0]
+    return rows[:, :half], rows[:, half:]
 
 
 def rotate(vectors, offsets, inverse):
@@ -57,10 +57,9 @@
     )
 
 
-def attend_kernel(
-    slot_ref, has_ref, q_ref, cos_ref, sin_ref, k_ref, v_ref, dq_ref, dk_ref, o_ref,
-    *, heads, head_dim, block_rows, span, scale,
-):
+def attend_kernel(slot_ref, has_ref, *refs, heads, head_dim, block_rows, span, scale):
+    q_refs = refs[:heads]
+    cos_ref, sin_ref, k_ref, v_ref, dq_ref, dk_ref, o_ref = refs[heads:]
     d = pl.program_id(0)
 
     @pl.when(has_ref[d] == 0)
@@ -82,7 +81,7 @@
         sin = sin_ref[...]
         for h in range(heads):
             cols = slice(h * head_dim, (h + 1) * head_dim)
-            qh = q_ref[:, cols].astype(jnp.float32)
+            qh = q_refs[h][...].astype(jnp.float32)
             qr = (qh * cos + pltpu.roll(qh, head_dim // 2, 1) * sin).astype(jnp.bfloat16)
             s = lax.dot_general(
                 qr, k, (((1,), (1,)), ((), ())), preferred_element_type=jnp.float32
@@ -95,13 +94,12 @@
             o_ref[0, :, cols] = (o / l).astype(o_ref.dtype)
 
 
-def attend(slot, has, q, cos_t, sin_t, k_ext, v_ext, doc_q, doc_k, n_dest, head_dim, group, groups):
+def attend(slot, has, q, cos_t, sin_t, k_ext, v_ext, doc_q, doc_k, n_dest, head_dim, first, heads):
     rows, all_width = q.shape
-    width = all_width // groups
+    width = heads * head_dim
     per_dev, block_rows, _ = doc_q.shape
     span = doc_k.shape[2]
     ext_rows = k_ext.shape[0]
-    heads = width // head_dim
     kernel = functools.partial(
         attend_kernel,
         heads=heads,
@@ -115,7 +113,10 @@
         num_scalar_prefetch=2,
         grid=(n_dest,),
         in_specs=[
-            pl.BlockSpec((block_rows, width), lambda d, s, h: (s[d], group)),
+            pl.BlockSpec((block_rows, head_dim), functools.partial(
+                lambda d, s, h, col: (s[d], col), col=first + head))
+            for head in range(heads)
+        ] + [
             pl.BlockSpec((block_rows, head_dim), lambda d, s, h: (s[d], 0)),
             pl.BlockSpec((block_rows, head_dim), lambda d, s, h: (s[d], 0)),
             pl.BlockSpec((ext_rows, head_dim), lambda d, s, h: (0, 0)),
@@ -135,7 +136,7 @@
             bytes_accessed=rows * width * 2 + n_dest * block_rows * width * 2
             + 2 * ext_rows * head_dim * 2,
         ),
-    )(slot, has, q, cos_t, sin_t, k_ext, v_ext, doc_q, doc_k)
+    )(slot, has, *([q] * heads), cos_t, sin_t, k_ext, v_ext, doc_q, doc_k)
 
 
 def local(queries, keys, values, rope_factors, doc_lengths, owner_map):
@@ -171,7 +172,7 @@
     doc_ext, off_ext = doc_tables(doc_lengths, pos_ext)
     doc_ext = jnp.where(pos_ext >= 0, doc_ext, -1)
     inverse = inverse_freqs(rope_factors, head_dim)
-    cos_ext, sin_ext = rotation_tables(off_ext, inverse)
+    cos_ext, sin_ext = rotation_tables(off_ext, inverse, tail_rows)
     k_f = k_raw.astype(jnp.float32)
     k_ext = (k_f * cos_ext + jnp.roll(k_f, head_dim // 2, axis=1) * sin_ext).astype(jnp.bfloat16)
     cos_t = cos_ext[tail_rows:]
@@ -190,20 +191,25 @@
         jnp.where(match, jnp.arange(per_dev, dtype=jnp.int32)[None, :], 0), axis=1, dtype=jnp.int32
     )
 
-    groups = 4
+    q_heads = queries.shape[1] // head_dim
+    sizes = [1, 2, 2, 2, 1] if q_heads == 8 else [q_heads]
     arrived = []
-    for group in range(groups):
+    first = 0
+    for heads in sizes:
         send = attend(
             slot, has, queries, cos_t, sin_t, k_ext, v_ext, doc_q, doc_k, ctx_size, head_dim,
-            group, groups,
+            first, heads,
         )
         arrived.append(lax.all_to_all(send, "ctx", split_axis=0, concat_axis=0, tiled=True))
+        first += heads
 
     sources_match = owner_map == ctx_index
     my_sources = jnp.sum(
         jnp.where(sources_match, devices[:, None], 0), axis=0, dtype=jnp.int32
     )
-    finished = jnp.concatenate([jnp.take(a, my_sources, axis=0) for a in arrived], axis=-1)
+    finished = jnp.concatenate(
+        [jnp.take(a, my_sources, axis=0, mode="clip") for a in arrived], axis=-1
+    )
     return finished.reshape(row_count, queries.shape[1])
 
 

time: 210 us -> 218 us (1.038)
  other arithmetic: 23.9 us -> 10.8 us
  local copies, waits for them, and re-layouts: 17.6 us -> 30.1 us
  starting transfers between devices: 37.3 us -> 46.9 us
  waiting for transfers between devices: 52.5 us -> 44 us
  Pallas kernels: 76.5 us -> 84.5 us
    all_to_all x4 -> x5, starting transfers between devices: 25.1 us -> 34.7 us  [local(): lax.all_to_all(send, 'ctx', split_axis=0, concat_axis=0, tiled=True)]
    all_to_all x4 -> x5, waiting for transfers between devices: 51 us -> 41.6 us  [local(): lax.all_to_all(send, 'ctx', split_axis=0, concat_axis=0, tiled=True)]
    pallas_call x4 -> x5, Pallas kernels: 76.5 us -> 84.5 us  [attend(): pl.pallas_call(kernel, grid_spec=grid_spec, out_shape=jax.ShapeDtypeStruc...]
    concatenate x3 -> x1, other arithmetic: 6.69 us -> 0.05 us  [rotation_tables(): table = jnp.concatenate([cosine, cosine, -sine, sine], axis=1)]
    sin x1 -> x0, other arithmetic: 6.01 us -> none  [rotation_tables(): sine = jnp.sin(angles)]
    gather x4 -> x6, local copies, waits for them, and re-layouts: 8.2 us -> 14.1 us  [the longest x5 8.31 us: local(): jnp.take(a, my_sources, axis=0, mode='clip')]
    unnamed x14 -> x18, local copies, waits for them, and re-layouts: 2.2 us -> 6.36 us
  transfers between devices with their start and end apart: 6 -> 7, of which waited for: 6 -> 6; matrix products, arithmetic and copies ran while one was open for 11% -> 12% of each run, Pallas kernels for 28% -> 32%
where the time goes in v3:
time: 218 us; the launch traced here: 217 us
  Pallas kernels  84.5 us (39%)
  starting transfers between devices  46.9 us (22%)
  waiting for transfers between devices  44 us (20%)
  local copies, waits for them, and re-layouts  30.1 us (14%)
  other arithmetic  10.8 us (5%)
    pallas_call x5, Pallas kernels, attend(): pl.pallas_call(kernel, grid_spec=grid_spec, out_shape=jax.ShapeDtypeStruc...  84.5 us
    all_to_all x5, waiting for transfers between devices, local(): lax.all_to_all(send, 'ctx', split_axis=0, concat_axis=0, tiled=True)  41.6 us
    all_to_all x5, starting transfers between devices, local(): lax.all_to_all(send, 'ctx', split_axis=0, concat_axis=0, tiled=True)  34.7 us
    gather x5, local copies, waits for them, and re-layouts, local(): jnp.take(a, my_sources, axis=0, mode='clip')  8.31 us
    unnamed x18, local copies, waits for them, and re-layouts  6.36 us
    all_to_all x1, starting transfers between devices, local(): kv = lax.all_to_all(kv, 'tp', split_axis=1, concat_axis=0, tiled=True)  6.32 us
    ppermute x1, starting transfers between devices, passed_along(): return lax.ppermute(shard, axis, pairs)  5.89 us
    gather x1, local copies, waits for them, and re-layouts, rotation_tables(): jnp.take(table, jnp.clip(offsets, 0, distinct - 1), axis=0, mode='clip')  5.75 us
  transfers between devices with their start and end apart: 7, of which 6 were waited for; matrix products, arithmetic and copies ran while one was open for 12% of the time, Pallas kernels for 32%

profile of v3, /device:TPU:1, one launch (start us, length us, event | category | flops | bytes accessed | tf_op | source)
XLA Modules:
  0.0 216.7 jit_solution(14247142451373799244)
XLA Ops:
  0.0 1.2 copy.19
  1.4 1.1 copy.17
  2.5 1.5 all_to_all.29
  4.0 6.3 %all-to-all-start = ((bf16[256,8,256]{2,0,1:T(8,128)(2,1)}), bf16[256,8,256]{2,0,1:T(8,128)(2,1)}, u32[]{:S(2)}, u32[]{:S(2)}) async-start(bf16[256,8,256]{2,0,1:T(8,128)(2,1)} %all_to_all.29), calls=%async_computation | async-start | bytes 2097152 | tf_op jit(solution)/shard_map/all_to_all | solution.py:163
  10.8 2.0 fusion.1
  13.4 2.2 %reduce_sum.56 = s32[10,256,1]{2,1,0:T(8,128)} reshape(s32[2560]{0:T(1024)S(1)} %get-tuple-element.5) | data formatting | bytes 20480 | tf_op jit(solution)/shard_map/reduce_sum | solution.py:23
  16.8 5.8 %gather_fusion = f32[2560,256]{1,0:T(8,128)S(1)} fusion(f32[512,256]{1,0:T(8,128)S(1)} %copy.16, s32[3072]{0:T(1024)S(1)} %pad_clamp_fusion), kind=kCustom, calls=%fused_computation | custom fusion | bytes 5253120 | tf_op jit(solution)/shard_map/jit(_take)/gather | solution.py:39
  23.2 1.5 fusion.9
  24.7 1.6 all-to-all-done
  27.3 5.9 %collective-permute-start = (bf16[512,256]{1,0:T(8,128)(2,1)S(1)}, bf16[512,256]{1,0:T(8,128)(2,1)S(1)}, u32[]{:S(2)}, u32[]{:S(2)}) collective-permute-start(bf16[512,256]{1,0:T(8,128)(2,1)S(1)} %bitcast.20), channel_id=1, source_target_pairs={{0,8},{8,16},{16,24},{24,32},{32,40},{40,48},{48,56},{56,64},{64,7... | collective-permute-start | bytes 786440 | tf_op jit(solution)/shard_map/ppermute | solution.py:17
  33.2 2.4 %slice_select_fusion.refs_5_.refs_6_ = s32[8,256,1]{2,1,0:T(8,128)} fusion(s32[10,256,1]{2,1,0:T(8,128)} %reduce_sum.56, s32[]{:T(128)S(6)} %sub.13), kind=kLoop, calls=%fused_computation.16 | loop fusion | flops 12288 | bytes 16388 | tf_op jit(solution)/shard_map/jit(_where)/select_n | solution.py:173
  36.5 2.2 %pad_maximum_fusion.1 = (bf16[2560,128]{1,0:T(8,128)(2,1)}, f32[2560,128]{1,0:T(8,128)S(1)}) fusion(bf16[2048,256]{1,0:T(8,128)(2,1)} %bitcast.3, bf16[512,256]{1,0:T(8,128)(2,1)S(1)} %collective-permute-done), kind=kLoop, calls=%fused_computation.24 | loop fusion | flops 2621440 | bytes 3276800 | tf_op jit(solution)/shard_map/concatenate | solution.py:165
  39.1 2.5 %fusion.3.refs_3_.refs_4_ = bf16[2560,128]{1,0:T(8,128)(2,1)} fusion(f32[2560,256]{1,0:T(8,128)S(1)} %gather_fusion, f32[2560,64]{1,0:T(8,128)S(1)} %get-tuple-element.14, f32[2560,64]{1,0:T(8,128)S(1)} %get-tuple-element.13, bf16[2048,256]{1,0:T(8,128)(2,1)} %bitcast.3, bf16[512,256]{1,0:T(8,128)(2,1)S(1)} %collective-permute-done), kind=kLoop, calls=%fused_computation.12 | loop fusion | flops 2949120 | bytes 5898240 | tf_op jit(solution)/shard_map/convert_element_type | solution.py:177
  41.5 14.8 %shard_map.68 = bf16[16,256,128]{2,1,0:T(8,128)(2,1)} custom-call(s32[16]{0:T(128)} %get-tuple-element.8.slot_ref, s32[16]{0:T(128)} %get-tuple-element.7.has_ref, bf16[2048,1024]{1,0:T(8,128)(2,1)} %refs_0_.9, f32[2048,128]{1,0:T(8,128)} %get-tuple-element.10.refs_1_.refs_2_, f32[2048,128]{1,0:T(8,128)} %get-tuple-element.9.refs_2_.refs_3_, ...), custom_call_target="tpu_custom_call" | custom-call | flops 805306368 | bytes 2883584 | tf_op jit(solution)/shard_map/pallas_call | solution.py:129
  56.4 9.0 %all-to-all-start.5 = ((bf16[16,256,128]{2,1,0:T(8,128)(2,1)}), bf16[16,256,128]{2,1,0:T(8,128)(2,1)S(1)}, u32[]{:S(2)}, u32[]{:S(2)}) async-start(bf16[16,256,128]{2,1,0:T(8,128)(2,1)} %shard_map.68), calls=%async_computation.5 | async-start | bytes 2097152 | tf_op jit(solution)/shard_map/all_to_all | solution.py:203
  65.4 14.8 %shard_map.64 = bf16[16,256,128]{2,1,0:T(8,128)(2,1)} custom-call(s32[16]{0:T(128)} %get-tuple-element.8.slot_ref, s32[16]{0:T(128)} %get-tuple-element.7.has_ref, bf16[2048,1024]{1,0:T(8,128)(2,1)} %refs_0_.9, f32[2048,128]{1,0:T(8,128)} %get-tuple-element.10.refs_1_.refs_2_, f32[2048,128]{1,0:T(8,128)} %get-tuple-element.9.refs_2_.refs_3_, ...), custom_call_target="tpu_custom_call" | custom-call | flops 805306368 | bytes 2883584 | tf_op jit(solution)/shard_map/pallas_call | solution.py:129
  80.2 2.2 all-to-all-done.5
  82.3 5.8 %all-to-all-start.1 = ((bf16[16,256,128]{2,1,0:T(8,128)(2,1)}), bf16[16,256,128]{2,1,0:T(8,128)(2,1)S(1)}, u32[]{:S(2)}, u32[]{:S(2)}) async-start(bf16[16,256,128]{2,1,0:T(8,128)(2,1)} %shard_map.64), calls=%async_computation.1 | async-start | bytes 2097152 | tf_op jit(solution)/shard_map/all_to_all | solution.py:203
  88.2 18.3 %shard_map.65 = bf16[16,256,256]{2,1,0:T(8,128)(2,1)} custom-call(s32[16]{0:T(128)} %get-tuple-element.8.slot_ref, s32[16]{0:T(128)} %get-tuple-element.7.has_ref, bf16[2048,1024]{1,0:T(8,128)(2,1)} %refs_0_.9, bf16[2048,1024]{1,0:T(8,128)(2,1)} %refs_0_.9, f32[2048,128]{1,0:T(8,128)} %get-tuple-element.10.refs_1_.refs_2_, ...), custom_call_target="tpu_custom_call" | custom-call | flops 1610612736 | bytes 4456448 | tf_op jit(solution)/shard_map/pallas_call | solution.py:129
  107.5 8.3 %all-to-all-start.2 = ((bf16[16,256,256]{2,1,0:T(8,128)(2,1)}), bf16[16,256,256]{2,1,0:T(8,128)(2,1)S(1)}, u32[]{:S(2)}, u32[]{:S(2)}) async-start(bf16[16,256,256]{2,1,0:T(8,128)(2,1)} %shard_map.65), calls=%async_computation.2 | async-start | bytes 4194304 | tf_op jit(solution)/shard_map/all_to_all | solution.py:203
  115.7 18.3 %shard_map.66 = bf16[16,256,256]{2,1,0:T(8,128)(2,1)} custom-call(s32[16]{0:T(128)} %get-tuple-element.8.slot_ref, s32[16]{0:T(128)} %get-tuple-element.7.has_ref, bf16[2048,1024]{1,0:T(8,128)(2,1)} %refs_0_.9, bf16[2048,1024]{1,0:T(8,128)(2,1)} %refs_0_.9, f32[2048,128]{1,0:T(8,128)} %get-tuple-element.10.refs_1_.refs_2_, ...), custom_call_target="tpu_custom_call" | custom-call | flops 1610612736 | bytes 4456448 | tf_op jit(solution)/shard_map/pallas_call | solution.py:129
  134.0 10.0 %all-to-all-done.2 = bf16[16,256,256]{2,1,0:T(8,128)(2,1)S(1)} async-done(((bf16[16,256,256]{2,1,0:T(8,128)(2,1)}), bf16[16,256,256]{2,1,0:T(8,128)(2,1)S(1)}, u32[]{:S(2)}, u32[]{:S(2)}) %all-to-all-start.2) | async-done | bytes 2097184 | tf_op jit(solution)/shard_map/all_to_all | solution.py:203
  144.0 5.8 %all-to-all-start.3 = ((bf16[16,256,256]{2,1,0:T(8,128)(2,1)}), bf16[16,256,256]{2,1,0:T(8,128)(2,1)}, u32[]{:S(2)}, u32[]{:S(2)}) async-start(bf16[16,256,256]{2,1,0:T(8,128)(2,1)} %shard_map.66), calls=%async_computation.3 | async-start | bytes 4194304 | tf_op jit(solution)/shard_map/all_to_all | solution.py:203
  149.8 18.3 %shard_map.67 = bf16[16,256,256]{2,1,0:T(8,128)(2,1)} custom-call(s32[16]{0:T(128)} %get-tuple-element.8.slot_ref, s32[16]{0:T(128)} %get-tuple-element.7.has_ref, bf16[2048,1024]{1,0:T(8,128)(2,1)} %refs_0_.9, bf16[2048,1024]{1,0:T(8,128)(2,1)} %refs_0_.9, f32[2048,128]{1,0:T(8,128)} %get-tuple-element.10.refs_1_.refs_2_, ...), custom_call_target="tpu_custom_call" | custom-call | flops 1610612736 | bytes 4456448 | tf_op jit(solution)/shard_map/pallas_call | solution.py:129
  168.1 10.1 %all-to-all-done.3 = bf16[16,256,256]{2,1,0:T(8,128)(2,1)} async-done(((bf16[16,256,256]{2,1,0:T(8,128)(2,1)}), bf16[16,256,256]{2,1,0:T(8,128)(2,1)}, u32[]{:S(2)}, u32[]{:S(2)}) %all-to-all-start.3) | async-done | bytes 2097184 | tf_op jit(solution)/shard_map/all_to_all | solution.py:203
  178.3 5.8 %all-to-all-start.4 = ((bf16[16,256,256]{2,1,0:T(8,128)(2,1)}), bf16[16,256,256]{2,1,0:T(8,128)(2,1)}, u32[]{:S(2)}, u32[]{:S(2)}) async-start(bf16[16,256,256]{2,1,0:T(8,128)(2,1)} %shard_map.67), calls=%async_computation.4 | async-start | bytes 4194304 | tf_op jit(solution)/shard_map/all_to_all | solution.py:203
  184.2 1.4 gather_fusion.5
  185.6 1.9 gather_fusion.1
  189.0 2.2 %gather_fusion.3 = bf16[8,256,256]{2,1,0:T(8,128)(2,1)S(1)} fusion(bf16[16,256,256]{2,1,0:T(8,128)(2,1)} %all-to-all-done.3, s32[1024]{0:T(1024)S(1)} %pad_clamp_fusion.1), kind=kCustom, calls=%fused_computation.3 | custom fusion | bytes 2097184 | tf_op jit(solution)/shard_map/jit(_take)/gather | solution.py:211
  191.2 1.0 constant_dynamic-update-slice_fusion.3
  193.3 19.2 %all-to-all-done.4 = bf16[16,256,256]{2,1,0:T(8,128)(2,1)} async-done(((bf16[16,256,256]{2,1,0:T(8,128)(2,1)}), bf16[16,256,256]{2,1,0:T(8,128)(2,1)}, u32[]{:S(2)}, u32[]{:S(2)}) %all-to-all-start.4) | async-done | bytes 2097184 | tf_op jit(solution)/shard_map/all_to_all | solution.py:203
  212.5 2.2 %gather_fusion.4 = bf16[8,256,256]{2,1,0:T(8,128)(2,1)S(1)} fusion(bf16[16,256,256]{2,1,0:T(8,128)(2,1)} %all-to-all-done.4, s32[1024]{0:T(1024)S(1)} %pad_clamp_fusion.1), kind=kCustom, calls=%fused_computation.4 | custom fusion | bytes 2097184 | tf_op jit(solution)/shard_map/jit(_take)/gather | solution.py:211
  (50 shorter events, 10.8 us)
Async XLA Ops:
  0.0 1.2 copy-start.2
  4.0 6.3 %copy-start.5 = (f32[64]{0:T(128)S(1)}, f32[64]{0:T(128)}, u32[]{:S(2)}) copy-start(f32[64]{0:T(128)} %param.9) | copy-start | bytes 772
  4.0 6.4 %copy-start.4 = (s32[128]{0:T(128)S(1)}, s32[128]{0:T(128)}, u32[]{:S(2)}) copy-start(s32[128]{0:T(128)} %param.10) | copy-start | bytes 1540
  4.0 22.3 %all-to-all-start = ((bf16[256,8,256]{2,0,1:T(8,128)(2,1)}), bf16[256,8,256]{2,0,1:T(8,128)(2,1)}, u32[]{:S(2)}, u32[]{:S(2)}) async-start(bf16[256,8,256]{2,0,1:T(8,128)(2,1)} %all_to_all.29), calls=%async_computation | async-start | bytes 2097152 | tf_op jit(solution)/shard_map/all_to_all | solution.py:163
  15.6 1.0 copy-start.3
  27.3 9.2 %collective-permute-start = (bf16[512,256]{1,0:T(8,128)(2,1)S(1)}, bf16[512,256]{1,0:T(8,128)(2,1)S(1)}, u32[]{:S(2)}, u32[]{:S(2)}) collective-permute-start(bf16[512,256]{1,0:T(8,128)(2,1)S(1)} %bitcast.20), channel_id=1, source_target_pairs={{0,8},{8,16},{16,24},{24,32},{32,40},{40,48},{48,56},{56,64},{64,7... | collective-permute-start | bytes 786440 | tf_op jit(solution)/shard_map/ppermute | solution.py:17
  56.4 26.0 %all-to-all-start.5 = ((bf16[16,256,128]{2,1,0:T(8,128)(2,1)}), bf16[16,256,128]{2,1,0:T(8,128)(2,1)S(1)}, u32[]{:S(2)}, u32[]{:S(2)}) async-start(bf16[16,256,128]{2,1,0:T(8,128)(2,1)} %shard_map.68), calls=%async_computation.5 | async-start | bytes 2097152 | tf_op jit(solution)/shard_map/all_to_all | solution.py:203
  82.3 24.2 %all-to-all-start.1 = ((bf16[16,256,128]{2,1,0:T(8,128)(2,1)}), bf16[16,256,128]{2,1,0:T(8,128)(2,1)S(1)}, u32[]{:S(2)}, u32[]{:S(2)}) async-start(bf16[16,256,128]{2,1,0:T(8,128)(2,1)} %shard_map.64), calls=%async_computation.1 | async-start | bytes 2097152 | tf_op jit(solution)/shard_map/all_to_all | solution.py:203
  106.5 1.0 copy-start
  107.5 36.6 %all-to-all-start.2 = ((bf16[16,256,256]{2,1,0:T(8,128)(2,1)}), bf16[16,256,256]{2,1,0:T(8,128)(2,1)S(1)}, u32[]{:S(2)}, u32[]{:S(2)}) async-start(bf16[16,256,256]{2,1,0:T(8,128)(2,1)} %shard_map.65), calls=%async_computation.2 | async-start | bytes 4194304 | tf_op jit(solution)/shard_map/all_to_all | solution.py:203
  144.0 34.2 %all-to-all-start.3 = ((bf16[16,256,256]{2,1,0:T(8,128)(2,1)}), bf16[16,256,256]{2,1,0:T(8,128)(2,1)}, u32[]{:S(2)}, u32[]{:S(2)}) async-start(bf16[16,256,256]{2,1,0:T(8,128)(2,1)} %shard_map.66), calls=%async_computation.3 | async-start | bytes 4194304 | tf_op jit(solution)/shard_map/all_to_all | solution.py:203
  178.3 34.2 %all-to-all-start.4 = ((bf16[16,256,256]{2,1,0:T(8,128)(2,1)}), bf16[16,256,256]{2,1,0:T(8,128)(2,1)}, u32[]{:S(2)}, u32[]{:S(2)}) async-start(bf16[16,256,256]{2,1,0:T(8,128)(2,1)} %shard_map.67), calls=%async_computation.4 | async-start | bytes 4194304 | tf_op jit(solution)/shard_map/all_to_all | solution.py:203
  214.7 1.2 copy-start.1

commit v4 on v3

--- a/solution.py
+++ b/solution.py
@@ -57,26 +57,19 @@
     )
 
 
-def attend_kernel(slot_ref, has_ref, *refs, heads, head_dim, block_rows, span, scale):
+def attend_kernel(dest_ref, *refs, heads, head_dim, block_rows, span, scale):
     q_refs = refs[:heads]
-    cos_ref, sin_ref, k_ref, v_ref, dq_ref, dk_ref, o_ref = refs[heads:]
-    d = pl.program_id(0)
-
-    @pl.when(has_ref[d] == 0)
-    def _():
-        o_ref[...] = jnp.zeros_like(o_ref)
-
-    @pl.when(has_ref[d] != 0)
-    def _():
-        start = pl.multiple_of(slot_ref[d] * block_rows, block_rows)
+    cos_ref, sin_ref, k_ref, v_ref, lo_ref, o_ref = refs[heads:]
+    r = pl.program_id(0)
+    if True:
+        start = pl.multiple_of(r * block_rows, block_rows)
         k = k_ref[pl.ds(start, span), :]
         v = v_ref[pl.ds(start, span), :]
-        doc_q = dq_ref[0]
-        doc_k = dk_ref[0]
         tail = span - block_rows
-        row = lax.broadcasted_iota(jnp.int32, (block_rows, span), 0)
+        lo = lo_ref[0]
+        hi = lax.broadcasted_iota(jnp.int32, (block_rows, 1), 0) + tail
         col = lax.broadcasted_iota(jnp.int32, (block_rows, span), 1)
-        visible = (doc_q == doc_k) & (col <= row + tail)
+        visible = (col >= lo) & (col <= hi)
         cos = cos_ref[...]
         sin = sin_ref[...]
         for h in range(heads):
@@ -94,12 +87,12 @@
             o_ref[0, :, cols] = (o / l).astype(o_ref.dtype)
 
 
-def attend(slot, has, q, cos_t, sin_t, k_ext, v_ext, doc_q, doc_k, n_dest, head_dim, first, heads):
+def attend(dest, q, cos_t, sin_t, k_ext, v_ext, lo, n_dest, head_dim, first, heads):
     rows, all_width = q.shape
     width = heads * head_dim
-    per_dev, block_rows, _ = doc_q.shape
-    span = doc_k.shape[2]
+    per_dev, block_rows, _ = lo.shape
     ext_rows = k_ext.shape[0]
+    span = ext_rows - rows + block_rows
     kernel = functools.partial(
         attend_kernel,
         heads=heads,
@@ -110,21 +103,20 @@
     )
     flops = 4 * per_dev * heads * block_rows * span * head_dim
     grid_spec = pltpu.PrefetchScalarGridSpec(
-        num_scalar_prefetch=2,
-        grid=(n_dest,),
+        num_scalar_prefetch=1,
+        grid=(per_dev,),
         in_specs=[
             pl.BlockSpec((block_rows, head_dim), functools.partial(
-                lambda d, s, h, col: (s[d], col), col=first + head))
+                lambda r, dst, col: (r, col), col=first + head))
             for head in range(heads)
         ] + [
-            pl.BlockSpec((block_rows, head_dim), lambda d, s, h: (s[d], 0)),
-            pl.BlockSpec((block_rows, head_dim), lambda d, s, h: (s[d], 0)),
-            pl.BlockSpec((ext_rows, head_dim), lambda d, s, h: (0, 0)),
-            pl.BlockSpec((ext_rows, head_dim), lambda d, s, h: (0, 0)),
-            pl.BlockSpec((1, block_rows, 1), lambda d, s, h: (s[d], 0, 0)),
-            pl.BlockSpec((1, 1, span), lambda d, s, h: (s[d], 0, 0)),
+            pl.BlockSpec((block_rows, head_dim), lambda r, dst: (r, 0)),
+            pl.BlockSpec((block_rows, head_dim), lambda r, dst: (r, 0)),
+            pl.BlockSpec((ext_rows, head_dim), lambda r, dst: (0, 0)),
+            pl.BlockSpec((ext_rows, head_dim), lambda r, dst: (0, 0)),
+            pl.BlockSpec((1, block_rows, 1), lambda r, dst: (r, 0, 0)),
         ],
-        out_specs=pl.BlockSpec((1, block_rows, width), lambda d, s, h: (d, 0, 0)),
+        out_specs=pl.BlockSpec((1, block_rows, width), lambda r, dst: (dst[r], 0, 0)),
     )
     return pl.pallas_call(
         kernel,
@@ -133,10 +125,10 @@
         cost_estimate=pl.CostEstimate(
             flops=flops,
             transcendentals=per_dev * heads * block_rows * span,
-            bytes_accessed=rows * width * 2 + n_dest * block_rows * width * 2
+            bytes_accessed=2 * rows * width * 2
             + 2 * ext_rows * head_dim * 2,
         ),
-    )(slot, has, *([q] * heads), cos_t, sin_t, k_ext, v_ext, doc_q, doc_k)
+    )(dest, *([q] * heads), cos_t, sin_t, k_ext, v_ext, lo)
 
 
 def local(queries, keys, values, rope_factors, doc_lengths, owner_map):
@@ -178,27 +170,19 @@
     cos_t = cos_ext[tail_rows:]
     sin_t = sin_ext[tail_rows:]
 
-    doc_q = doc_ext[tail_rows:].reshape(per_dev, block_rows, 1)
-    doc_k = jnp.stack(
-        [doc_ext[slot * block_rows : slot * block_rows + span] for slot in range(per_dev)]
-    ).reshape(per_dev, 1, span)
+    lo = (tail_rows + jnp.arange(row_count, dtype=jnp.int32) % block_rows - off_ext[tail_rows:])
+    lo = lo.reshape(per_dev, block_rows, 1)
 
     devices = jnp.arange(ctx_size, dtype=jnp.int32)
     owner_row = lax.dynamic_index_in_dim(owner_map, ctx_index, 0, keepdims=False)
-    match = owner_row[None, :] == devices[:, None]
-    has = jnp.sum(match.astype(jnp.int32), axis=1, dtype=jnp.int32)
-    slot = jnp.sum(
-        jnp.where(match, jnp.arange(per_dev, dtype=jnp.int32)[None, :], 0), axis=1, dtype=jnp.int32
-    )
 
     q_heads = queries.shape[1] // head_dim
-    sizes = [1, 2, 2, 2, 1] if q_heads == 8 else [q_heads]
+    sizes = [2, 2, 2, 2] if q_heads == 8 else [q_heads]
     arrived = []
     first = 0
     for heads in sizes:
         send = attend(
-            slot, has, queries, cos_t, sin_t, k_ext, v_ext, doc_q, doc_k, ctx_size, head_dim,
-            first, heads,
+            owner_row, queries, cos_t, sin_t, k_ext, v_ext, lo, ctx_size, head_dim, first, heads
         )
         arrived.append(lax.all_to_all(send, "ctx", split_axis=0, concat_axis=0, tiled=True))
         first += heads

time: 218 us -> 201 us (0.922)
  waiting for transfers between devices: 44 us -> 77 us
  Pallas kernels: 84.5 us -> 51.6 us
  starting transfers between devices: 46.9 us -> 37.6 us
  local copies, waits for them, and re-layouts: 30.1 us -> 23.1 us
    pallas_call x5 -> x4, Pallas kernels: 84.5 us -> 51.6 us  [attend(): pl.pallas_call(kernel, grid_spec=grid_spec, out_shape=jax.ShapeDtypeStruc...]
    all_to_all x5 -> x4, waiting for transfers between devices: 41.6 us -> 69.7 us  [local(): lax.all_to_all(send, 'ctx', split_axis=0, concat_axis=0, tiled=True)]
    all_to_all x5 -> x4, starting transfers between devices: 34.7 us -> 25.4 us  [local(): lax.all_to_all(send, 'ctx', split_axis=0, concat_axis=0, tiled=True)]
    all_to_all x1, waiting for transfers between devices: 1.61 us -> 7.27 us  [local(): kv = lax.all_to_all(kv, 'tp', split_axis=1, concat_axis=0, tiled=True)]
    unnamed x18 -> x10, local copies, waits for them, and re-layouts: 6.36 us -> 1.3 us
    concatenate x0 -> x1, other arithmetic: none -> 3.35 us  [local(): jnp.concatenate([jnp.take(a, my_sources, axis=0, mode='clip') for a in ar...]
    select_n x2 -> x0, other arithmetic: 2.45 us -> none  [local(): doc_ext = jnp.where(pos_ext >= 0, doc_ext, -1)]
    reduce_sum x1, local copies, waits for them, and re-layouts: 2.2 us -> 0.01 us  [doc_tables(): jnp.sum(jnp.where(before, lengths[None, :], 0), axis=1, dtype=jnp.int32)]
  transfers between devices with their start and end apart: 7 -> 6, of which waited for: 6 -> 5; matrix products, arithmetic and copies ran while one was open for 12% -> 9% of each run, Pallas kernels for 32% -> 19%
where the time goes in v4:
time: 201 us; the launch traced here: 200 us
  waiting for transfers between devices  77 us (38%)
  Pallas kernels  51.6 us (26%)
  starting transfers between devices  37.6 us (19%)
  local copies, waits for them, and re-layouts  23.1 us (11%)
  other arithmetic  10.8 us (5%)
    all_to_all x4, waiting for transfers between devices, local(): lax.all_to_all(send, 'ctx', split_axis=0, concat_axis=0, tiled=True)  69.7 us
    pallas_call x4, Pallas kernels, attend(): pl.pallas_call(kernel, grid_spec=grid_spec, out_shape=jax.ShapeDtypeStruc...  51.6 us
    all_to_all x4, starting transfers between devices, local(): lax.all_to_all(send, 'ctx', split_axis=0, concat_axis=0, tiled=True)  25.4 us
    gather x4, local copies, waits for them, and re-layouts, local(): jnp.take(a, my_sources, axis=0, mode='clip')  8.2 us
    all_to_all x1, waiting for transfers between devices, local(): kv = lax.all_to_all(kv, 'tp', split_axis=1, concat_axis=0, tiled=True)  7.27 us
    all_to_all x1, starting transfers between devices, local(): kv = lax.all_to_all(kv, 'tp', split_axis=1, concat_axis=0, tiled=True)  6.32 us
    ppermute x1, starting transfers between devices, passed_along(): return lax.ppermute(shard, axis, pairs)  5.89 us
    gather x1, local copies, waits for them, and re-layouts, rotation_tables(): jnp.take(table, jnp.clip(offsets, 0, distinct - 1), axis=0, mode='clip')  5.75 us
  transfers between devices with their start and end apart: 6, of which 5 were waited for; matrix products, arithmetic and copies ran while one was open for 9% of the time, Pallas kernels for 19%

profile of v4, /device:TPU:1, one launch (start us, length us, event | category | flops | bytes accessed | tf_op | source)
XLA Modules:
  0.0 200.3 jit_solution(15313594331807048677)
XLA Ops:
  0.0 1.2 copy.28
  1.4 1.1 copy.23
  2.5 1.5 all_to_all.26
  4.0 6.3 %all-to-all-start = ((bf16[256,8,256]{2,0,1:T(8,128)(2,1)}), bf16[256,8,256]{2,0,1:T(8,128)(2,1)}, u32[]{:S(2)}, u32[]{:S(2)}) async-start(bf16[256,8,256]{2,0,1:T(8,128)(2,1)} %all_to_all.26), calls=%async_computation | async-start | bytes 2097152 | tf_op jit(solution)/shard_map/all_to_all | solution.py:155
  10.8 0.5 multiply_cosine_fusion
  11.6 1.6 select_reduce_fusion
  13.3 5.8 %gather_fusion = f32[2560,256]{1,0:T(8,128)S(1)} fusion(f32[512,256]{1,0:T(8,128)S(1)} %copy.22, s32[3072]{0:T(1024)S(1)} %pad_clamp_fusion), kind=kCustom, calls=%fused_computation | custom fusion | bytes 5253120 | tf_op jit(solution)/shard_map/jit(_take)/gather | solution.py:39
  19.0 7.3 %all-to-all-done = bf16[256,8,256]{2,0,1:T(8,128)(2,1)} async-done(((bf16[256,8,256]{2,0,1:T(8,128)(2,1)}), bf16[256,8,256]{2,0,1:T(8,128)(2,1)}, u32[]{:S(2)}, u32[]{:S(2)}) %all-to-all-start) | async-done | bytes 1048608 | tf_op jit(solution)/shard_map/all_to_all | solution.py:155
  26.3 1.0 slice.63
  27.3 5.9 %collective-permute-start = (bf16[512,256]{1,0:T(8,128)(2,1)S(1)}, bf16[512,256]{1,0:T(8,128)(2,1)S(1)}, u32[]{:S(2)}, u32[]{:S(2)}) collective-permute-start(bf16[512,256]{1,0:T(8,128)(2,1)S(1)} %bitcast.22), channel_id=1, source_target_pairs={{0,8},{8,16},{16,24},{24,32},{32,40},{40,48},{48,56},{56,64},{64,7... | collective-permute-start | bytes 786440 | tf_op jit(solution)/shard_map/ppermute | solution.py:17
  33.2 1.5 fusion.10
  34.7 1.4 copy.24.refs_6_
  36.1 0.7 dynamic-slice_reduce_fusion.dest_ref
  36.8 2.2 %pad_maximum_fusion.2 = (bf16[2560,128]{1,0:T(8,128)(2,1)}, f32[2560,128]{1,0:T(8,128)S(1)}) fusion(bf16[2048,256]{1,0:T(8,128)(2,1)} %bitcast.3, bf16[512,256]{1,0:T(8,128)(2,1)S(1)} %collective-permute-done), kind=kLoop, calls=%fused_computation.16 | loop fusion | flops 2621440 | bytes 3276800 | tf_op jit(solution)/shard_map/concatenate | solution.py:157
  39.4 2.5 %fusion.1.refs_4_ = bf16[2560,128]{1,0:T(8,128)(2,1)} fusion(f32[2560,256]{1,0:T(8,128)S(1)} %gather_fusion, f32[2560,64]{1,0:T(8,128)S(1)} %get-tuple-element.10, f32[2560,64]{1,0:T(8,128)S(1)} %get-tuple-element.9, bf16[2048,256]{1,0:T(8,128)(2,1)} %bitcast.3, bf16[512,256]{1,0:T(8,128)(2,1)S(1)} %collective-permute-done), kind=kLoop, calls=%fused_computation.8 | loop fusion | flops 2949120 | bytes 5898240 | tf_op jit(solution)/shard_map/convert_element_type | solution.py:169
  41.9 12.9 %shard_map.67 = bf16[16,256,256]{2,1,0:T(8,128)(2,1)} custom-call(s32[8]{0:T(128)} %dynamic-slice_reduce_fusion.dest_ref, bf16[2048,1024]{1,0:T(8,128)(2,1)} %refs_1_.7, bf16[2048,1024]{1,0:T(8,128)(2,1)} %refs_1_.7, f32[2048,128]{1,0:T(8,128)} %get-tuple-element.6.refs_2_, f32[2048,128]{1,0:T(8,128)} %get-tuple-element.5.refs_3_, ...), custom_call_target="tpu_custom_call" | custom-call | flops 1610612736 | bytes 3407872 | tf_op jit(solution)/shard_map/pallas_call | solution.py:121
  54.8 7.9 %all-to-all-start.4 = ((bf16[16,256,256]{2,1,0:T(8,128)(2,1)}), bf16[16,256,256]{2,1,0:T(8,128)(2,1)S(1)}, u32[]{:S(2)}, u32[]{:S(2)}) async-start(bf16[16,256,256]{2,1,0:T(8,128)(2,1)} %shard_map.67), calls=%async_computation.4 | async-start | bytes 4194304 | tf_op jit(solution)/shard_map/all_to_all | solution.py:187
  62.7 12.9 %shard_map.66 = bf16[16,256,256]{2,1,0:T(8,128)(2,1)} custom-call(s32[8]{0:T(128)} %dynamic-slice_reduce_fusion.dest_ref, bf16[2048,1024]{1,0:T(8,128)(2,1)} %refs_1_.7, bf16[2048,1024]{1,0:T(8,128)(2,1)} %refs_1_.7, f32[2048,128]{1,0:T(8,128)} %get-tuple-element.6.refs_2_, f32[2048,128]{1,0:T(8,128)} %get-tuple-element.5.refs_3_, ...), custom_call_target="tpu_custom_call" | custom-call | flops 1610612736 | bytes 3407872 | tf_op jit(solution)/shard_map/pallas_call | solution.py:121
  75.6 15.4 %all-to-all-done.4 = bf16[16,256,256]{2,1,0:T(8,128)(2,1)S(1)} async-done(((bf16[16,256,256]{2,1,0:T(8,128)(2,1)}), bf16[16,256,256]{2,1,0:T(8,128)(2,1)S(1)}, u32[]{:S(2)}, u32[]{:S(2)}) %all-to-all-start.4) | async-done | bytes 2097184 | tf_op jit(solution)/shard_map/all_to_all | solution.py:187
  91.0 5.8 %all-to-all-start.3 = ((bf16[16,256,256]{2,1,0:T(8,128)(2,1)}), bf16[16,256,256]{2,1,0:T(8,128)(2,1)}, u32[]{:S(2)}, u32[]{:S(2)}) async-start(bf16[16,256,256]{2,1,0:T(8,128)(2,1)} %shard_map.66), calls=%async_computation.3 | async-start | bytes 4194304 | tf_op jit(solution)/shard_map/all_to_all | solution.py:187
  96.9 12.9 %shard_map.64 = bf16[16,256,256]{2,1,0:T(8,128)(2,1)} custom-call(s32[8]{0:T(128)} %dynamic-slice_reduce_fusion.dest_ref, bf16[2048,1024]{1,0:T(8,128)(2,1)} %refs_1_.7, bf16[2048,1024]{1,0:T(8,128)(2,1)} %refs_1_.7, f32[2048,128]{1,0:T(8,128)} %get-tuple-element.6.refs_2_, f32[2048,128]{1,0:T(8,128)} %get-tuple-element.5.refs_3_, ...), custom_call_target="tpu_custom_call" | custom-call | flops 1610612736 | bytes 3407872 | tf_op jit(solution)/shard_map/pallas_call | solution.py:121
  109.7 15.5 %all-to-all-done.3 = bf16[16,256,256]{2,1,0:T(8,128)(2,1)} async-done(((bf16[16,256,256]{2,1,0:T(8,128)(2,1)}), bf16[16,256,256]{2,1,0:T(8,128)(2,1)}, u32[]{:S(2)}, u32[]{:S(2)}) %all-to-all-start.3) | async-done | bytes 2097184 | tf_op jit(solution)/shard_map/all_to_all | solution.py:187
  125.3 5.8 %all-to-all-start.1 = ((bf16[16,256,256]{2,1,0:T(8,128)(2,1)}), bf16[16,256,256]{2,1,0:T(8,128)(2,1)}, u32[]{:S(2)}, u32[]{:S(2)}) async-start(bf16[16,256,256]{2,1,0:T(8,128)(2,1)} %shard_map.64), calls=%async_computation.1 | async-start | bytes 4194304 | tf_op jit(solution)/shard_map/all_to_all | solution.py:187
  131.1 12.9 %shard_map.65 = bf16[16,256,256]{2,1,0:T(8,128)(2,1)} custom-call(s32[8]{0:T(128)} %dynamic-slice_reduce_fusion.dest_ref, bf16[2048,1024]{1,0:T(8,128)(2,1)} %refs_1_.7, bf16[2048,1024]{1,0:T(8,128)(2,1)} %refs_1_.7, f32[2048,128]{1,0:T(8,128)} %get-tuple-element.6.refs_2_, f32[2048,128]{1,0:T(8,128)} %get-tuple-element.5.refs_3_, ...), custom_call_target="tpu_custom_call" | custom-call | flops 1610612736 | bytes 3407872 | tf_op jit(solution)/shard_map/pallas_call | solution.py:121
  144.0 15.5 %all-to-all-done.1 = bf16[16,256,256]{2,1,0:T(8,128)(2,1)} async-done(((bf16[16,256,256]{2,1,0:T(8,128)(2,1)}), bf16[16,256,256]{2,1,0:T(8,128)(2,1)}, u32[]{:S(2)}, u32[]{:S(2)}) %all-to-all-start.1) | async-done | bytes 2097184 | tf_op jit(solution)/shard_map/all_to_all | solution.py:187
  159.5 5.8 %all-to-all-start.2 = ((bf16[16,256,256]{2,1,0:T(8,128)(2,1)}), bf16[16,256,256]{2,1,0:T(8,128)(2,1)}, u32[]{:S(2)}, u32[]{:S(2)}) async-start(bf16[16,256,256]{2,1,0:T(8,128)(2,1)} %shard_map.65), calls=%async_computation.2 | async-start | bytes 4194304 | tf_op jit(solution)/shard_map/all_to_all | solution.py:187
  165.4 0.6 gather_fusion.4
  166.1 2.2 %gather_fusion.3 = bf16[8,256,256]{2,1,0:T(8,128)(2,1)S(1)} fusion(bf16[16,256,256]{2,1,0:T(8,128)(2,1)} %all-to-all-done.3, s32[1024]{0:T(1024)S(1)} %pad_clamp_fusion.1), kind=kCustom, calls=%fused_computation.3 | custom fusion | bytes 2097184 | tf_op jit(solution)/shard_map/jit(_take)/gather | solution.py:195
  168.3 2.2 %gather_fusion.1 = bf16[8,256,256]{2,1,0:T(8,128)(2,1)S(1)} fusion(bf16[16,256,256]{2,1,0:T(8,128)(2,1)} %all-to-all-done.1, s32[1024]{0:T(1024)S(1)} %pad_clamp_fusion.1), kind=kCustom, calls=%fused_computation.1 | custom fusion | bytes 2097184 | tf_op jit(solution)/shard_map/jit(_take)/gather | solution.py:195
  170.5 23.2 %all-to-all-done.2 = bf16[16,256,256]{2,1,0:T(8,128)(2,1)} async-done(((bf16[16,256,256]{2,1,0:T(8,128)(2,1)}), bf16[16,256,256]{2,1,0:T(8,128)(2,1)}, u32[]{:S(2)}, u32[]{:S(2)}) %all-to-all-start.2) | async-done | bytes 2097184 | tf_op jit(solution)/shard_map/all_to_all | solution.py:187
  193.7 3.2 %gather_fusion.2 = bf16[8,256,256]{2,1,0:T(8,128)(2,1)} fusion(bf16[16,256,256]{2,1,0:T(8,128)(2,1)} %all-to-all-done.2, s32[1024]{0:T(1024)S(1)} %pad_clamp_fusion.1), kind=kCustom, calls=%fused_computation.2 | custom fusion | bytes 2097184 | tf_op jit(solution)/shard_map/jit(_take)/gather | solution.py:195
  196.9 3.4 %pad_maximum_fusion = bf16[8,256,1024]{2,1,0:T(8,128)(2,1)} fusion(bf16[8,256,256]{2,1,0:T(8,128)(2,1)S(1)} %gather_fusion.4, bf16[8,256,256]{2,1,0:T(8,128)(2,1)S(1)} %gather_fusion.3, bf16[8,256,256]{2,1,0:T(8,128)(2,1)} %gather_fusion.2, bf16[8,256,256]{2,1,0:T(8,128)(2,1)S(1)} %gather_fusion.1), kind=kLoop, calls=%fused_computation.5 | loop fusion | flops 16777216 | bytes 8388608 | tf_op jit(solution)/shard_map/concatenate | solution.py:194
  (26 shorter events, 1.5 us)
Async XLA Ops:
  0.0 1.2 copy-start
  4.0 6.3 %copy-start.2 = (s32[128]{0:T(128)S(1)}, s32[128]{0:T(128)}, u32[]{:S(2)}) copy-start(s32[128]{0:T(128)} %param.10) | copy-start | bytes 1540
  4.0 6.7 %copy-start.3 = (f32[64]{0:T(128)S(1)}, f32[64]{0:T(128)}, u32[]{:S(2)}) copy-start(f32[64]{0:T(128)} %param.9) | copy-start | bytes 772
  4.0 22.3 %all-to-all-start = ((bf16[256,8,256]{2,0,1:T(8,128)(2,1)}), bf16[256,8,256]{2,0,1:T(8,128)(2,1)}, u32[]{:S(2)}, u32[]{:S(2)}) async-start(bf16[256,8,256]{2,0,1:T(8,128)(2,1)} %all_to_all.26), calls=%async_computation | async-start | bytes 2097152 | tf_op jit(solution)/shard_map/all_to_all | solution.py:155
  27.3 8.8 %copy-start.1 = (s32[16,8]{0,1:T(8,128)S(1)}, s32[16,8]{0,1:T(8,128)}, u32[]{:S(2)}) copy-start(s32[16,8]{0,1:T(8,128)} %param.11) | copy-start | bytes 1540
  27.3 9.5 %collective-permute-start = (bf16[512,256]{1,0:T(8,128)(2,1)S(1)}, bf16[512,256]{1,0:T(8,128)(2,1)S(1)}, u32[]{:S(2)}, u32[]{:S(2)}) collective-permute-start(bf16[512,256]{1,0:T(8,128)(2,1)S(1)} %bitcast.22), channel_id=1, source_target_pairs={{0,8},{8,16},{16,24},{24,32},{32,40},{40,48},{48,56},{56,64},{64,7... | collective-permute-start | bytes 786440 | tf_op jit(solution)/shard_map/ppermute | solution.py:17
  54.8 36.3 %all-to-all-start.4 = ((bf16[16,256,256]{2,1,0:T(8,128)(2,1)}), bf16[16,256,256]{2,1,0:T(8,128)(2,1)S(1)}, u32[]{:S(2)}, u32[]{:S(2)}) async-start(bf16[16,256,256]{2,1,0:T(8,128)(2,1)} %shard_map.67), calls=%async_computation.4 | async-start | bytes 4194304 | tf_op jit(solution)/shard_map/all_to_all | solution.py:187
  91.0 34.2 %all-to-all-start.3 = ((bf16[16,256,256]{2,1,0:T(8,128)(2,1)}), bf16[16,256,256]{2,1,0:T(8,128)(2,1)}, u32[]{:S(2)}, u32[]{:S(2)}) async-start(bf16[16,256,256]{2,1,0:T(8,128)(2,1)} %shard_map.66), calls=%async_computation.3 | async-start | bytes 4194304 | tf_op jit(solution)/shard_map/all_to_all | solution.py:187
  125.3 34.2 %all-to-all-start.1 = ((bf16[16,256,256]{2,1,0:T(8,128)(2,1)}), bf16[16,256,256]{2,1,0:T(8,128)(2,1)}, u32[]{:S(2)}, u32[]{:S(2)}) async-start(bf16[16,256,256]{2,1,0:T(8,128)(2,1)} %shard_map.64), calls=%async_computation.1 | async-start | bytes 4194304 | tf_op jit(solution)/shard_map/all_to_all | solution.py:187
  159.5 34.2 %all-to-all-start.2 = ((bf16[16,256,256]{2,1,0:T(8,128)(2,1)}), bf16[16,256,256]{2,1,0:T(8,128)(2,1)}, u32[]{:S(2)}, u32[]{:S(2)}) async-start(bf16[16,256,256]{2,1,0:T(8,128)(2,1)} %shard_map.65), calls=%async_computation.2 | async-start | bytes 4194304 | tf_op jit(solution)/shard_map/all_to_all | solution.py:187

commit v5 on v4

--- a/solution.py
+++ b/solution.py
@@ -61,8 +61,8 @@
     q_refs = refs[:heads]
     cos_ref, sin_ref, k_ref, v_ref, lo_ref, o_ref = refs[heads:]
     r = pl.program_id(0)
+    start = pl.multiple_of(r * block_rows, block_rows)
     if True:
-        start = pl.multiple_of(r * block_rows, block_rows)
         k = k_ref[pl.ds(start, span), :]
         v = v_ref[pl.ds(start, span), :]
         tail = span - block_rows
@@ -191,9 +191,13 @@
     my_sources = jnp.sum(
         jnp.where(sources_match, devices[:, None], 0), axis=0, dtype=jnp.int32
     )
-    finished = jnp.concatenate(
-        [jnp.take(a, my_sources, axis=0, mode="clip") for a in arrived], axis=-1
-    )
+    finished = jnp.zeros((per_dev, block_rows, queries.shape[1]), queries.dtype)
+    first = 0
+    for heads, a in zip(sizes, arrived):
+        finished = lax.dynamic_update_slice(
+            finished, jnp.take(a, my_sources, axis=0, mode="clip"), (0, 0, first * head_dim)
+        )
+        first += heads
     return finished.reshape(row_count, queries.shape[1])
 
 

time: 201 us -> 198 us (0.985)
  local copies, waits for them, and re-layouts: 23.1 us -> 27.9 us
  waiting for transfers between devices: 77 us -> 72.3 us
  other arithmetic: 10.8 us -> 7.39 us
    dynamic_update_slice x0 -> x4, local copies, waits for them, and re-layouts: none -> 5.69 us  [local(): lax.dynamic_update_slice(finished, jnp.take(a, my_sources, axis=0, mode='...]
    all_to_all x4, waiting for transfers between devices: 69.7 us -> 65.1 us  [local(): lax.all_to_all(send, 'ctx', split_axis=0, concat_axis=0, tiled=True)]
    concatenate x1 -> x0, other arithmetic: 3.35 us -> none  [local(): jnp.concatenate([jnp.take(a, my_sources, axis=0, mode='clip') for a in ar...]
  transfers between devices with their start and end apart: 6 -> 6, of which waited for: 5 -> 5; matrix products, arithmetic and copies ran while one was open for 9% -> 11% of each run, Pallas kernels for 19% -> 20%
where the time goes in v5:
time: 198 us; the launch traced here: 197 us
  waiting for transfers between devices  72.3 us (37%)
  Pallas kernels  51.6 us (26%)
  starting transfers between devices  37.5 us (19%)
  local copies, waits for them, and re-layouts  27.9 us (14%)
  other arithmetic  7.39 us (4%)
    all_to_all x4, waiting for transfers between devices, local(): lax.all_to_all(send, 'ctx', split_axis=0, concat_axis=0, tiled=True)  65.1 us
    pallas_call x4, Pallas kernels, attend(): pl.pallas_call(kernel, grid_spec=grid_spec, out_shape=jax.ShapeDtypeStruc...  51.6 us
    all_to_all x4, starting transfers between devices, local(): lax.all_to_all(send, 'ctx', split_axis=0, concat_axis=0, tiled=True)  25.3 us
    all_to_all x1, waiting for transfers between devices, local(): kv = lax.all_to_all(kv, 'tp', split_axis=1, concat_axis=0, tiled=True)  7.27 us
    gather x4, local copies, waits for them, and re-layouts, local(): jnp.take(a, my_sources, axis=0, mode='clip')  7.22 us
    all_to_all x1, starting transfers between devices, local(): kv = lax.all_to_all(kv, 'tp', split_axis=1, concat_axis=0, tiled=True)  6.32 us
    ppermute x1, starting transfers between devices, passed_along(): return lax.ppermute(shard, axis, pairs)  5.89 us
    gather x1, local copies, waits for them, and re-layouts, rotation_tables(): jnp.take(table, jnp.clip(offsets, 0, distinct - 1), axis=0, mode='clip')  5.75 us
  transfers between devices with their start and end apart: 6, of which 5 were waited for; matrix products, arithmetic and copies ran while one was open for 11% of the time, Pallas kernels for 20%

profile of v5, /device:TPU:1, one launch (start us, length us, event | category | flops | bytes accessed | tf_op | source)
XLA Modules:
  0.0 196.9 jit_solution(18266972833171217874)
XLA Ops:
  0.0 1.2 copy.28
  1.4 1.1 copy.23
  2.5 1.5 all_to_all.26
  4.0 6.3 %all-to-all-start = ((bf16[256,8,256]{2,0,1:T(8,128)(2,1)}), bf16[256,8,256]{2,0,1:T(8,128)(2,1)}, u32[]{:S(2)}, u32[]{:S(2)}) async-start(bf16[256,8,256]{2,0,1:T(8,128)(2,1)} %all_to_all.26), calls=%async_computation | async-start | bytes 2097152 | tf_op jit(solution)/shard_map/all_to_all | solution.py:155
  11.6 1.6 select_reduce_fusion
  13.3 5.8 %gather_fusion = f32[2560,256]{1,0:T(8,128)S(1)} fusion(f32[512,256]{1,0:T(8,128)S(1)} %copy.22, s32[3072]{0:T(1024)S(1)} %pad_clamp_fusion), kind=kCustom, calls=%fused_computation | custom fusion | bytes 5253120 | tf_op jit(solution)/shard_map/jit(_take)/gather | solution.py:39
  19.0 7.3 %all-to-all-done = bf16[256,8,256]{2,0,1:T(8,128)(2,1)} async-done(((bf16[256,8,256]{2,0,1:T(8,128)(2,1)}), bf16[256,8,256]{2,0,1:T(8,128)(2,1)}, u32[]{:S(2)}, u32[]{:S(2)}) %all-to-all-start) | async-done | bytes 1048608 | tf_op jit(solution)/shard_map/all_to_all | solution.py:155
  26.3 1.0 slice.63
  27.3 5.9 %collective-permute-start = (bf16[512,256]{1,0:T(8,128)(2,1)S(1)}, bf16[512,256]{1,0:T(8,128)(2,1)S(1)}, u32[]{:S(2)}, u32[]{:S(2)}) collective-permute-start(bf16[512,256]{1,0:T(8,128)(2,1)S(1)} %bitcast.22), channel_id=1, source_target_pairs={{0,8},{8,16},{16,24},{24,32},{32,40},{40,48},{48,56},{56,64},{64,7... | collective-permute-start | bytes 786440 | tf_op jit(solution)/shard_map/ppermute | solution.py:17
  33.2 1.5 fusion.10
  34.7 1.4 copy.24.refs_6_
  36.8 2.2 %pad_maximum_fusion.1 = (bf16[2560,128]{1,0:T(8,128)(2,1)}, f32[2560,128]{1,0:T(8,128)S(1)}) fusion(bf16[2048,256]{1,0:T(8,128)(2,1)} %bitcast.3, bf16[512,256]{1,0:T(8,128)(2,1)S(1)} %collective-permute-done), kind=kLoop, calls=%fused_computation.15 | loop fusion | flops 2621440 | bytes 3276800 | tf_op jit(solution)/shard_map/concatenate | solution.py:157
  39.4 2.5 %fusion.1.refs_4_ = bf16[2560,128]{1,0:T(8,128)(2,1)} fusion(f32[2560,256]{1,0:T(8,128)S(1)} %gather_fusion, f32[2560,64]{1,0:T(8,128)S(1)} %get-tuple-element.10, f32[2560,64]{1,0:T(8,128)S(1)} %get-tuple-element.9, bf16[2048,256]{1,0:T(8,128)(2,1)} %bitcast.3, bf16[512,256]{1,0:T(8,128)(2,1)S(1)} %collective-permute-done), kind=kLoop, calls=%fused_computation.7 | loop fusion | flops 2949120 | bytes 5898240 | tf_op jit(solution)/shard_map/convert_element_type | solution.py:169
  41.9 12.9 %shard_map.66 = bf16[16,256,256]{2,1,0:T(8,128)(2,1)} custom-call(s32[8]{0:T(128)} %dynamic-slice_reduce_fusion.dest_ref, bf16[2048,1024]{1,0:T(8,128)(2,1)} %refs_1_.7, bf16[2048,1024]{1,0:T(8,128)(2,1)} %refs_1_.7, f32[2048,128]{1,0:T(8,128)} %get-tuple-element.6.refs_2_, f32[2048,128]{1,0:T(8,128)} %get-tuple-element.5.refs_3_, ...), custom_call_target="tpu_custom_call" | custom-call | flops 1610612736 | bytes 3407872 | tf_op jit(solution)/shard_map/pallas_call | solution.py:121
  54.8 7.9 %all-to-all-start.3 = ((bf16[16,256,256]{2,1,0:T(8,128)(2,1)}), bf16[16,256,256]{2,1,0:T(8,128)(2,1)S(1)}, u32[]{:S(2)}, u32[]{:S(2)}) async-start(bf16[16,256,256]{2,1,0:T(8,128)(2,1)} %shard_map.66), calls=%async_computation.3 | async-start | bytes 4194304 | tf_op jit(solution)/shard_map/all_to_all | solution.py:187
  62.7 12.9 %shard_map.64 = bf16[16,256,256]{2,1,0:T(8,128)(2,1)} custom-call(s32[8]{0:T(128)} %dynamic-slice_reduce_fusion.dest_ref, bf16[2048,1024]{1,0:T(8,128)(2,1)} %refs_1_.7, bf16[2048,1024]{1,0:T(8,128)(2,1)} %refs_1_.7, f32[2048,128]{1,0:T(8,128)} %get-tuple-element.6.refs_2_, f32[2048,128]{1,0:T(8,128)} %get-tuple-element.5.refs_3_, ...), custom_call_target="tpu_custom_call" | custom-call | flops 1610612736 | bytes 3407872 | tf_op jit(solution)/shard_map/pallas_call | solution.py:121
  75.6 15.4 %all-to-all-done.3 = bf16[16,256,256]{2,1,0:T(8,128)(2,1)S(1)} async-done(((bf16[16,256,256]{2,1,0:T(8,128)(2,1)}), bf16[16,256,256]{2,1,0:T(8,128)(2,1)S(1)}, u32[]{:S(2)}, u32[]{:S(2)}) %all-to-all-start.3) | async-done | bytes 2097184 | tf_op jit(solution)/shard_map/all_to_all | solution.py:187
  91.0 5.8 %all-to-all-start.1 = ((bf16[16,256,256]{2,1,0:T(8,128)(2,1)}), bf16[16,256,256]{2,1,0:T(8,128)(2,1)}, u32[]{:S(2)}, u32[]{:S(2)}) async-start(bf16[16,256,256]{2,1,0:T(8,128)(2,1)} %shard_map.64), calls=%async_computation.1 | async-start | bytes 4194304 | tf_op jit(solution)/shard_map/all_to_all | solution.py:187
  96.8 12.9 %shard_map.65 = bf16[16,256,256]{2,1,0:T(8,128)(2,1)} custom-call(s32[8]{0:T(128)} %dynamic-slice_reduce_fusion.dest_ref, bf16[2048,1024]{1,0:T(8,128)(2,1)} %refs_1_.7, bf16[2048,1024]{1,0:T(8,128)(2,1)} %refs_1_.7, f32[2048,128]{1,0:T(8,128)} %get-tuple-element.6.refs_2_, f32[2048,128]{1,0:T(8,128)} %get-tuple-element.5.refs_3_, ...), custom_call_target="tpu_custom_call" | custom-call | flops 1610612736 | bytes 3407872 | tf_op jit(solution)/shard_map/pallas_call | solution.py:121
  109.7 15.5 %all-to-all-done.1 = bf16[16,256,256]{2,1,0:T(8,128)(2,1)} async-done(((bf16[16,256,256]{2,1,0:T(8,128)(2,1)}), bf16[16,256,256]{2,1,0:T(8,128)(2,1)}, u32[]{:S(2)}, u32[]{:S(2)}) %all-to-all-start.1) | async-done | bytes 2097184 | tf_op jit(solution)/shard_map/all_to_all | solution.py:187
  125.2 5.8 %all-to-all-start.2 = ((bf16[16,256,256]{2,1,0:T(8,128)(2,1)}), bf16[16,256,256]{2,1,0:T(8,128)(2,1)}, u32[]{:S(2)}, u32[]{:S(2)}) async-start(bf16[16,256,256]{2,1,0:T(8,128)(2,1)} %shard_map.65), calls=%async_computation.2 | async-start | bytes 4194304 | tf_op jit(solution)/shard_map/all_to_all | solution.py:187
  131.0 12.9 %shard_map.67 = bf16[16,256,256]{2,1,0:T(8,128)(2,1)} custom-call(s32[8]{0:T(128)} %dynamic-slice_reduce_fusion.dest_ref, bf16[2048,1024]{1,0:T(8,128)(2,1)} %refs_1_.7, bf16[2048,1024]{1,0:T(8,128)(2,1)} %refs_1_.7, f32[2048,128]{1,0:T(8,128)} %get-tuple-element.6.refs_2_, f32[2048,128]{1,0:T(8,128)} %get-tuple-element.5.refs_3_, ...), custom_call_target="tpu_custom_call" | custom-call | flops 1610612736 | bytes 3407872 | tf_op jit(solution)/shard_map/pallas_call | solution.py:121
  143.9 15.5 %all-to-all-done.2 = bf16[16,256,256]{2,1,0:T(8,128)(2,1)} async-done(((bf16[16,256,256]{2,1,0:T(8,128)(2,1)}), bf16[16,256,256]{2,1,0:T(8,128)(2,1)}, u32[]{:S(2)}, u32[]{:S(2)}) %all-to-all-start.2) | async-done | bytes 2097184 | tf_op jit(solution)/shard_map/all_to_all | solution.py:187
  159.4 5.8 %all-to-all-start.4 = ((bf16[16,256,256]{2,1,0:T(8,128)(2,1)}), bf16[16,256,256]{2,1,0:T(8,128)(2,1)}, u32[]{:S(2)}, u32[]{:S(2)}) async-start(bf16[16,256,256]{2,1,0:T(8,128)(2,1)} %shard_map.67), calls=%async_computation.4 | async-start | bytes 4194304 | tf_op jit(solution)/shard_map/all_to_all | solution.py:187
  165.4 2.2 %gather_fusion.1 = bf16[8,256,256]{2,1,0:T(8,128)(2,1)S(1)} fusion(bf16[16,256,256]{2,1,0:T(8,128)(2,1)} %all-to-all-done.1, s32[1024]{0:T(1024)S(1)} %pad_clamp_fusion.1), kind=kCustom, calls=%fused_computation.1 | custom fusion | bytes 2097184 | tf_op jit(solution)/shard_map/jit(_take)/gather | solution.py:198
  167.6 2.6 %dynamic_update_slice.12 = bf16[8,256,1024]{2,1,0:T(8,128)(2,1)} pad(bf16[8,256,256]{2,1,0:T(8,128)(2,1)S(1)} %gather_fusion.1, bf16[]{:T(256)} %constant.49.clone.1), padding=0_0x0_0x0_768 | pad | bytes 5242882 | tf_op jit(solution)/shard_map/dynamic_update_slice | solution.py:197
  170.8 2.2 %gather_fusion.2 = bf16[8,256,256]{2,1,0:T(8,128)(2,1)S(1)} fusion(bf16[16,256,256]{2,1,0:T(8,128)(2,1)} %all-to-all-done.2, s32[1024]{0:T(1024)S(1)} %pad_clamp_fusion.1), kind=kCustom, calls=%fused_computation.2 | custom fusion | bytes 2097184 | tf_op jit(solution)/shard_map/jit(_take)/gather | solution.py:198
  173.0 1.0 constant_dynamic-update-slice_fusion.1
  174.0 1.0 constant_dynamic-update-slice_fusion
  175.1 18.6 %all-to-all-done.4 = bf16[16,256,256]{2,1,0:T(8,128)(2,1)} async-done(((bf16[16,256,256]{2,1,0:T(8,128)(2,1)}), bf16[16,256,256]{2,1,0:T(8,128)(2,1)}, u32[]{:S(2)}, u32[]{:S(2)}) %all-to-all-start.4) | async-done | bytes 2097184 | tf_op jit(solution)/shard_map/all_to_all | solution.py:187
  193.7 2.2 %gather_fusion.4 = bf16[8,256,256]{2,1,0:T(8,128)(2,1)S(1)} fusion(bf16[16,256,256]{2,1,0:T(8,128)(2,1)} %all-to-all-done.4, s32[1024]{0:T(1024)S(1)} %pad_clamp_fusion.1), kind=kCustom, calls=%fused_computation.4 | custom fusion | bytes 2097184 | tf_op jit(solution)/shard_map/jit(_take)/gather | solution.py:198
  195.9 1.0 constant_dynamic-update-slice_fusion.2
  (29 shorter events, 3.4 us)
Async XLA Ops:
  0.0 1.2 copy-start
  4.0 6.3 %copy-start.2 = (s32[128]{0:T(128)S(1)}, s32[128]{0:T(128)}, u32[]{:S(2)}) copy-start(s32[128]{0:T(128)} %param.10) | copy-start | bytes 1540
  4.0 6.7 %copy-start.3 = (f32[64]{0:T(128)S(1)}, f32[64]{0:T(128)}, u32[]{:S(2)}) copy-start(f32[64]{0:T(128)} %param.9) | copy-start | bytes 772
  4.0 22.3 %all-to-all-start = ((bf16[256,8,256]{2,0,1:T(8,128)(2,1)}), bf16[256,8,256]{2,0,1:T(8,128)(2,1)}, u32[]{:S(2)}, u32[]{:S(2)}) async-start(bf16[256,8,256]{2,0,1:T(8,128)(2,1)} %all_to_all.26), calls=%async_computation | async-start | bytes 2097152 | tf_op jit(solution)/shard_map/all_to_all | solution.py:155
  27.3 8.8 %copy-start.1 = (s32[16,8]{0,1:T(8,128)S(1)}, s32[16,8]{0,1:T(8,128)}, u32[]{:S(2)}) copy-start(s32[16,8]{0,1:T(8,128)} %param.11) | copy-start | bytes 1540
  27.3 9.6 %collective-permute-start = (bf16[512,256]{1,0:T(8,128)(2,1)S(1)}, bf16[512,256]{1,0:T(8,128)(2,1)S(1)}, u32[]{:S(2)}, u32[]{:S(2)}) collective-permute-start(bf16[512,256]{1,0:T(8,128)(2,1)S(1)} %bitcast.22), channel_id=1, source_target_pairs={{0,8},{8,16},{16,24},{24,32},{32,40},{40,48},{48,56},{56,64},{64,7... | collective-permute-start | bytes 786440 | tf_op jit(solution)/shard_map/ppermute | solution.py:17
  54.8 36.2 %all-to-all-start.3 = ((bf16[16,256,256]{2,1,0:T(8,128)(2,1)}), bf16[16,256,256]{2,1,0:T(8,128)(2,1)S(1)}, u32[]{:S(2)}, u32[]{:S(2)}) async-start(bf16[16,256,256]{2,1,0:T(8,128)(2,1)} %shard_map.66), calls=%async_computation.3 | async-start | bytes 4194304 | tf_op jit(solution)/shard_map/all_to_all | solution.py:187
  91.0 34.2 %all-to-all-start.1 = ((bf16[16,256,256]{2,1,0:T(8,128)(2,1)}), bf16[16,256,256]{2,1,0:T(8,128)(2,1)}, u32[]{:S(2)}, u32[]{:S(2)}) async-start(bf16[16,256,256]{2,1,0:T(8,128)(2,1)} %shard_map.64), calls=%async_computation.1 | async-start | bytes 4194304 | tf_op jit(solution)/shard_map/all_to_all | solution.py:187
  125.2 34.2 %all-to-all-start.2 = ((bf16[16,256,256]{2,1,0:T(8,128)(2,1)}), bf16[16,256,256]{2,1,0:T(8,128)(2,1)}, u32[]{:S(2)}, u32[]{:S(2)}) async-start(bf16[16,256,256]{2,1,0:T(8,128)(2,1)} %shard_map.65), calls=%async_computation.2 | async-start | bytes 4194304 | tf_op jit(solution)/shard_map/all_to_all | solution.py:187
  159.4 34.2 %all-to-all-start.4 = ((bf16[16,256,256]{2,1,0:T(8,128)(2,1)}), bf16[16,256,256]{2,1,0:T(8,128)(2,1)}, u32[]{:S(2)}, u32[]{:S(2)}) async-start(bf16[16,256,256]{2,1,0:T(8,128)(2,1)} %shard_map.67), calls=%async_computation.4 | async-start | bytes 4194304 | tf_op jit(solution)/shard_map/all_to_all | solution.py:187

commit v6 on v5

--- a/solution.py
+++ b/solution.py
@@ -177,7 +177,7 @@
     owner_row = lax.dynamic_index_in_dim(owner_map, ctx_index, 0, keepdims=False)
 
     q_heads = queries.shape[1] // head_dim
-    sizes = [2, 2, 2, 2] if q_heads == 8 else [q_heads]
+    sizes = [2, 3, 3] if q_heads == 8 else [q_heads]
     arrived = []
     first = 0
     for heads in sizes:

time: 198 us -> 194 us (0.980)
  Pallas kernels: 51.6 us -> 45.4 us
  local copies, waits for them, and re-layouts: 27.9 us -> 32.1 us
    pallas_call x4 -> x3, Pallas kernels: 51.6 us -> 45.4 us  [attend(): pl.pallas_call(kernel, grid_spec=grid_spec, out_shape=jax.ShapeDtypeStruc...]
    dynamic_update_slice x4 -> x3, local copies, waits for them, and re-layouts: 5.69 us -> 7.81 us  [local(): lax.dynamic_update_slice(finished, jnp.take(a, my_sources, axis=0, mode='...]
    all_to_all x4 -> x3, starting transfers between devices: 25.3 us -> 23.5 us  [local(): lax.all_to_all(send, 'ctx', split_axis=0, concat_axis=0, tiled=True)]
    all_to_all x4 -> x3, waiting for transfers between devices: 65.1 us -> 63.3 us  [local(): lax.all_to_all(send, 'ctx', split_axis=0, concat_axis=0, tiled=True)]
    gather x4 -> x3, local copies, waits for them, and re-layouts: 7.22 us -> 7.96 us  [local(): jnp.take(a, my_sources, axis=0, mode='clip')]
  transfers between devices with their start and end apart: 6 -> 5, of which waited for: 5 -> 4; matrix products, arithmetic and copies ran while one was open for 11% -> 13% of each run, Pallas kernels for 20% -> 17%
where the time goes in v6:
time: 194 us; the launch traced here: 192 us
  waiting for transfers between devices  70.6 us (36%)
  Pallas kernels  45.4 us (23%)
  starting transfers between devices  35.8 us (18%)
  local copies, waits for them, and re-layouts  32.1 us (17%)
  other arithmetic  7.51 us (4%)
    all_to_all x3, waiting for transfers between devices, local(): lax.all_to_all(send, 'ctx', split_axis=0, concat_axis=0, tiled=True)  63.3 us
    pallas_call x3, Pallas kernels, attend(): pl.pallas_call(kernel, grid_spec=grid_spec, out_shape=jax.ShapeDtypeStruc...  45.4 us
    all_to_all x3, starting transfers between devices, local(): lax.all_to_all(send, 'ctx', split_axis=0, concat_axis=0, tiled=True)  23.5 us
    gather x3, local copies, waits for them, and re-layouts, local(): jnp.take(a, my_sources, axis=0, mode='clip')  7.96 us
    dynamic_update_slice x3, local copies, waits for them, and re-layouts, local(): lax.dynamic_update_slice(finished, jnp.take(a, my_sources, axis=0, mode='...  7.81 us
    all_to_all x1, waiting for transfers between devices, local(): kv = lax.all_to_all(kv, 'tp', split_axis=1, concat_axis=0, tiled=True)  7.27 us
    all_to_all x1, starting transfers between devices, local(): kv = lax.all_to_all(kv, 'tp', split_axis=1, concat_axis=0, tiled=True)  6.32 us
    ppermute x1, starting transfers between devices, passed_along(): return lax.ppermute(shard, axis, pairs)  5.89 us
  transfers between devices with their start and end apart: 5, of which 4 were waited for; matrix products, arithmetic and copies ran while one was open for 13% of the time, Pallas kernels for 17%

profile of v6, /device:TPU:1, one launch (start us, length us, event | category | flops | bytes accessed | tf_op | source)
XLA Modules:
  0.0 191.5 jit_solution(2297284838849597395)
XLA Ops:
  0.0 1.2 copy.25
  1.4 1.1 copy.21
  2.5 1.5 all_to_all.23
  4.0 6.3 %all-to-all-start = ((bf16[256,8,256]{2,0,1:T(8,128)(2,1)}), bf16[256,8,256]{2,0,1:T(8,128)(2,1)}, u32[]{:S(2)}, u32[]{:S(2)}) async-start(bf16[256,8,256]{2,0,1:T(8,128)(2,1)} %all_to_all.23), calls=%async_computation | async-start | bytes 2097152 | tf_op jit(solution)/shard_map/all_to_all | solution.py:155
  10.8 0.5 multiply_cosine_fusion
  11.6 1.6 select_reduce_fusion
  13.3 5.8 %gather_fusion = f32[2560,256]{1,0:T(8,128)S(1)} fusion(f32[512,256]{1,0:T(8,128)S(1)} %copy.20, s32[3072]{0:T(1024)S(1)} %pad_clamp_fusion), kind=kCustom, calls=%fused_computation | custom fusion | bytes 5253120 | tf_op jit(solution)/shard_map/jit(_take)/gather | solution.py:39
  19.0 7.3 %all-to-all-done = bf16[256,8,256]{2,0,1:T(8,128)(2,1)} async-done(((bf16[256,8,256]{2,0,1:T(8,128)(2,1)}), bf16[256,8,256]{2,0,1:T(8,128)(2,1)}, u32[]{:S(2)}, u32[]{:S(2)}) %all-to-all-start) | async-done | bytes 1048608 | tf_op jit(solution)/shard_map/all_to_all | solution.py:155
  26.3 1.0 slice.61
  27.3 5.9 %collective-permute-start = (bf16[512,256]{1,0:T(8,128)(2,1)S(1)}, bf16[512,256]{1,0:T(8,128)(2,1)S(1)}, u32[]{:S(2)}, u32[]{:S(2)}) collective-permute-start(bf16[512,256]{1,0:T(8,128)(2,1)S(1)} %bitcast.22), channel_id=1, source_target_pairs={{0,8},{8,16},{16,24},{24,32},{32,40},{40,48},{48,56},{56,64},{64,7... | collective-permute-start | bytes 786440 | tf_op jit(solution)/shard_map/ppermute | solution.py:17
  33.2 1.5 fusion.10
  34.7 1.4 copy.22.refs_6_.refs_7_
  36.1 0.7 dynamic-slice_reduce_fusion.dest_ref
  36.8 2.2 %pad_maximum_fusion.1 = (bf16[2560,128]{1,0:T(8,128)(2,1)}, f32[2560,128]{1,0:T(8,128)S(1)}) fusion(bf16[2048,256]{1,0:T(8,128)(2,1)} %bitcast.3, bf16[512,256]{1,0:T(8,128)(2,1)S(1)} %collective-permute-done), kind=kLoop, calls=%fused_computation.14 | loop fusion | flops 2621440 | bytes 3276800 | tf_op jit(solution)/shard_map/concatenate | solution.py:157
  39.1 0.4 fusion.11
  39.5 2.5 %fusion.1.refs_4_.refs_5_ = bf16[2560,128]{1,0:T(8,128)(2,1)} fusion(f32[2560,256]{1,0:T(8,128)S(1)} %gather_fusion, f32[2560,64]{1,0:T(8,128)S(1)} %get-tuple-element.10, f32[2560,64]{1,0:T(8,128)S(1)} %get-tuple-element.9, bf16[2048,256]{1,0:T(8,128)(2,1)} %bitcast.3, bf16[512,256]{1,0:T(8,128)(2,1)S(1)} %collective-permute-done), kind=kLoop, calls=%fused_computation.6 | loop fusion | flops 2949120 | bytes 5898240 | tf_op jit(solution)/shard_map/convert_element_type | solution.py:169
  42.0 12.9 %shard_map.64 = bf16[16,256,256]{2,1,0:T(8,128)(2,1)} custom-call(s32[8]{0:T(128)} %dynamic-slice_reduce_fusion.dest_ref, bf16[2048,1024]{1,0:T(8,128)(2,1)} %refs_2_.3, bf16[2048,1024]{1,0:T(8,128)(2,1)} %refs_2_.3, f32[2048,128]{1,0:T(8,128)} %get-tuple-element.6.refs_2_.refs_3_, f32[2048,128]{1,0:T(8,128)} %get-tuple-element.5.refs_3_.refs_4_, ...), custom_call_target="tpu_custom_call" | custom-call | flops 1610612736 | bytes 3407872 | tf_op jit(solution)/shard_map/pallas_call | solution.py:121
  54.9 7.9 %all-to-all-start.1 = ((bf16[16,256,256]{2,1,0:T(8,128)(2,1)}), bf16[16,256,256]{2,1,0:T(8,128)(2,1)S(1)}, u32[]{:S(2)}, u32[]{:S(2)}) async-start(bf16[16,256,256]{2,1,0:T(8,128)(2,1)} %shard_map.64), calls=%async_computation.1 | async-start | bytes 4194304 | tf_op jit(solution)/shard_map/all_to_all | solution.py:187
  62.8 16.3 %shard_map.65 = bf16[16,256,384]{2,1,0:T(8,128)(2,1)} custom-call(s32[8]{0:T(128)} %dynamic-slice_reduce_fusion.dest_ref, bf16[2048,1024]{1,0:T(8,128)(2,1)} %refs_2_.3, bf16[2048,1024]{1,0:T(8,128)(2,1)} %refs_2_.3, bf16[2048,1024]{1,0:T(8,128)(2,1)} %refs_2_.3, f32[2048,128]{1,0:T(8,128)} %get-tuple-element.6.refs_2_.refs_3_, ...), custom_call_target="tpu_custom_call" | custom-call | flops 2415919104 | bytes 4456448 | tf_op jit(solution)/shard_map/pallas_call | solution.py:121
  79.1 12.1 %all-to-all-done.1 = bf16[16,256,256]{2,1,0:T(8,128)(2,1)S(1)} async-done(((bf16[16,256,256]{2,1,0:T(8,128)(2,1)}), bf16[16,256,256]{2,1,0:T(8,128)(2,1)S(1)}, u32[]{:S(2)}, u32[]{:S(2)}) %all-to-all-start.1) | async-done | bytes 2097184 | tf_op jit(solution)/shard_map/all_to_all | solution.py:187
  91.1 1.3 copy-done
  92.5 5.8 %all-to-all-start.2 = ((bf16[16,256,384]{2,1,0:T(8,128)(2,1)}), bf16[16,256,384]{2,1,0:T(8,128)(2,1)S(1)}, u32[]{:S(2)}, u32[]{:S(2)}) async-start(bf16[16,256,384]{2,1,0:T(8,128)(2,1)} %shard_map.65), calls=%async_computation.2 | async-start | bytes 6291456 | tf_op jit(solution)/shard_map/all_to_all | solution.py:187
  98.3 16.3 %shard_map.66 = bf16[16,256,384]{2,1,0:T(8,128)(2,1)} custom-call(s32[8]{0:T(128)} %dynamic-slice_reduce_fusion.dest_ref, bf16[2048,1024]{1,0:T(8,128)(2,1)} %refs_2_.3, bf16[2048,1024]{1,0:T(8,128)(2,1)} %refs_2_.3, bf16[2048,1024]{1,0:T(8,128)(2,1)} %refs_2_.3, f32[2048,128]{1,0:T(8,128)} %get-tuple-element.6.refs_2_.refs_3_, ...), custom_call_target="tpu_custom_call" | custom-call | flops 2415919104 | bytes 4456448 | tf_op jit(solution)/shard_map/pallas_call | solution.py:121
  114.5 23.3 %all-to-all-done.2 = bf16[16,256,384]{2,1,0:T(8,128)(2,1)S(1)} async-done(((bf16[16,256,384]{2,1,0:T(8,128)(2,1)}), bf16[16,256,384]{2,1,0:T(8,128)(2,1)S(1)}, u32[]{:S(2)}, u32[]{:S(2)}) %all-to-all-start.2) | async-done | bytes 3145760 | tf_op jit(solution)/shard_map/all_to_all | solution.py:187
  137.9 9.8 %all-to-all-start.3 = ((bf16[16,256,384]{2,1,0:T(8,128)(2,1)}), bf16[16,256,384]{2,1,0:T(8,128)(2,1)}, u32[]{:S(2)}, u32[]{:S(2)}) async-start(bf16[16,256,384]{2,1,0:T(8,128)(2,1)} %shard_map.66), calls=%async_computation.3 | async-start | bytes 6291456 | tf_op jit(solution)/shard_map/all_to_all | solution.py:187
  147.8 3.3 %gather_fusion.1 = bf16[8,256,256]{2,1,0:T(8,128)(2,1)} fusion(bf16[16,256,256]{2,1,0:T(8,128)(2,1)} %copy-done, s32[1024]{0:T(1024)S(1)} %pad_clamp_fusion.1), kind=kCustom, calls=%fused_computation.1 | custom fusion | bytes 2097184 | tf_op jit(solution)/shard_map/jit(_take)/gather | solution.py:198
  151.1 3.8 %dynamic_update_slice.9 = bf16[8,256,1024]{2,1,0:T(8,128)(2,1)} pad(bf16[8,256,256]{2,1,0:T(8,128)(2,1)} %gather_fusion.1, bf16[]{:T(256)} %constant.49.clone.1), padding=0_0x0_0x0_768 | pad | bytes 5242882 | tf_op jit(solution)/shard_map/dynamic_update_slice | solution.py:197
  154.9 1.9 gather_fusion.2
  156.8 2.7 %constant_dynamic-update-slice_fusion = bf16[8,256,1024]{2,1,0:T(8,128)(2,1)} fusion(bf16[8,256,1024]{2,1,0:T(8,128)(2,1)} %dynamic_update_slice.9, bf16[8,256,384]{2,1,0:T(8,128)(2,1)} %gather_fusion.2), kind=kLoop, calls=%fused_computation.37 | loop fusion | bytes 3145728 | tf_op jit(solution)/shard_map/dynamic_update_slice | solution.py:197
  159.5 27.9 %all-to-all-done.3 = bf16[16,256,384]{2,1,0:T(8,128)(2,1)} async-done(((bf16[16,256,384]{2,1,0:T(8,128)(2,1)}), bf16[16,256,384]{2,1,0:T(8,128)(2,1)}, u32[]{:S(2)}, u32[]{:S(2)}) %all-to-all-start.3) | async-done | bytes 3145760 | tf_op jit(solution)/shard_map/all_to_all | solution.py:187
  187.4 2.8 %gather_fusion.3 = bf16[8,256,384]{2,1,0:T(8,128)(2,1)S(1)} fusion(bf16[16,256,384]{2,1,0:T(8,128)(2,1)} %all-to-all-done.3, s32[1024]{0:T(1024)S(1)} %pad_clamp_fusion.1), kind=kCustom, calls=%fused_computation.3 | custom fusion | bytes 3145760 | tf_op jit(solution)/shard_map/jit(_take)/gather | solution.py:198
  190.2 1.3 constant_dynamic-update-slice_fusion.1
  (26 shorter events, 1.1 us)
Async XLA Ops:
  0.0 1.2 copy-start.1
  4.0 6.3 %copy-start.3 = (s32[128]{0:T(128)S(1)}, s32[128]{0:T(128)}, u32[]{:S(2)}) copy-start(s32[128]{0:T(128)} %param.10) | copy-start | bytes 1540
  4.0 6.7 %copy-start.4 = (f32[64]{0:T(128)S(1)}, f32[64]{0:T(128)}, u32[]{:S(2)}) copy-start(f32[64]{0:T(128)} %param.9) | copy-start | bytes 772
  4.0 22.3 %all-to-all-start = ((bf16[256,8,256]{2,0,1:T(8,128)(2,1)}), bf16[256,8,256]{2,0,1:T(8,128)(2,1)}, u32[]{:S(2)}, u32[]{:S(2)}) async-start(bf16[256,8,256]{2,0,1:T(8,128)(2,1)} %all_to_all.23), calls=%async_computation | async-start | bytes 2097152 | tf_op jit(solution)/shard_map/all_to_all | solution.py:155
  27.3 8.8 %copy-start.2 = (s32[16,8]{0,1:T(8,128)S(1)}, s32[16,8]{0,1:T(8,128)}, u32[]{:S(2)}) copy-start(s32[16,8]{0,1:T(8,128)} %param.11) | copy-start | bytes 1540
  27.3 9.6 %collective-permute-start = (bf16[512,256]{1,0:T(8,128)(2,1)S(1)}, bf16[512,256]{1,0:T(8,128)(2,1)S(1)}, u32[]{:S(2)}, u32[]{:S(2)}) collective-permute-start(bf16[512,256]{1,0:T(8,128)(2,1)S(1)} %bitcast.22), channel_id=1, source_target_pairs={{0,8},{8,16},{16,24},{24,32},{32,40},{40,48},{48,56},{56,64},{64,7... | collective-permute-start | bytes 786440 | tf_op jit(solution)/shard_map/ppermute | solution.py:17
  54.9 36.2 %all-to-all-start.1 = ((bf16[16,256,256]{2,1,0:T(8,128)(2,1)}), bf16[16,256,256]{2,1,0:T(8,128)(2,1)S(1)}, u32[]{:S(2)}, u32[]{:S(2)}) async-start(bf16[16,256,256]{2,1,0:T(8,128)(2,1)} %shard_map.64), calls=%async_computation.1 | async-start | bytes 4194304 | tf_op jit(solution)/shard_map/all_to_all | solution.py:187
  91.1 1.3 copy-start
  92.5 45.4 %all-to-all-start.2 = ((bf16[16,256,384]{2,1,0:T(8,128)(2,1)}), bf16[16,256,384]{2,1,0:T(8,128)(2,1)S(1)}, u32[]{:S(2)}, u32[]{:S(2)}) async-start(bf16[16,256,384]{2,1,0:T(8,128)(2,1)} %shard_map.65), calls=%async_computation.2 | async-start | bytes 6291456 | tf_op jit(solution)/shard_map/all_to_all | solution.py:187
  137.9 49.5 %all-to-all-start.3 = ((bf16[16,256,384]{2,1,0:T(8,128)(2,1)}), bf16[16,256,384]{2,1,0:T(8,128)(2,1)}, u32[]{:S(2)}, u32[]{:S(2)}) async-start(bf16[16,256,384]{2,1,0:T(8,128)(2,1)} %shard_map.66), calls=%async_computation.3 | async-start | bytes 6291456 | tf_op jit(solution)/shard_map/all_to_all | solution.py:187

commit v7 on v6

--- a/solution.py
+++ b/solution.py
@@ -177,7 +177,7 @@
     owner_row = lax.dynamic_index_in_dim(owner_map, ctx_index, 0, keepdims=False)
 
     q_heads = queries.shape[1] // head_dim
-    sizes = [2, 3, 3] if q_heads == 8 else [q_heads]
+    sizes = [2, 6] if q_heads == 8 else [q_heads]
     arrived = []
     first = 0
     for heads in sizes:

time: 194 us -> 202 us (1.041)
  waiting for transfers between devices: 70.6 us -> 102 us
  local copies, waits for them, and re-layouts: 32.1 us -> 20.2 us
  starting transfers between devices: 35.8 us -> 25.9 us
  Pallas kernels: 45.4 us -> 39.8 us
  other arithmetic: 7.51 us -> 11.2 us
    all_to_all x3 -> x2, waiting for transfers between devices: 63.3 us -> 94.9 us  [local(): lax.all_to_all(send, 'ctx', split_axis=0, concat_axis=0, tiled=True)]
    all_to_all x3 -> x2, starting transfers between devices: 23.5 us -> 13.7 us  [local(): lax.all_to_all(send, 'ctx', split_axis=0, concat_axis=0, tiled=True)]
    dynamic_update_slice x3 -> x0, local copies, waits for them, and re-layouts: 7.81 us -> none  [local(): lax.dynamic_update_slice(finished, jnp.take(a, my_sources, axis=0, mode='...]
    pallas_call x3 -> x2, Pallas kernels: 45.4 us -> 39.8 us  [attend(): pl.pallas_call(kernel, grid_spec=grid_spec, out_shape=jax.ShapeDtypeStruc...]
    dynamic_update_slice x0 -> x1, other arithmetic: none -> 3.79 us  [local(): lax.dynamic_update_slice(finished, jnp.take(a, my_sources, axis=0, mode='...]
    gather x3 -> x2, local copies, waits for them, and re-layouts: 7.96 us -> 5.2 us  [local(): jnp.take(a, my_sources, axis=0, mode='clip')]
  transfers between devices with their start and end apart: 5 -> 4, of which waited for: 4 -> 3; matrix products, arithmetic and copies ran while one was open for 13% -> 7% of each run, Pallas kernels for 17% -> 13%
where the time goes in v7:
time: 202 us; the launch traced here: 199 us
  waiting for transfers between devices  102 us (50%)
  Pallas kernels  39.8 us (20%)
  starting transfers between devices  25.9 us (13%)
  local copies, waits for them, and re-layouts  20.2 us (10%)
  other arithmetic  11.2 us (6%)
    all_to_all x2, waiting for transfers between devices, local(): lax.all_to_all(send, 'ctx', split_axis=0, concat_axis=0, tiled=True)  94.9 us
    pallas_call x2, Pallas kernels, attend(): pl.pallas_call(kernel, grid_spec=grid_spec, out_shape=jax.ShapeDtypeStruc...  39.8 us
    all_to_all x2, starting transfers between devices, local(): lax.all_to_all(send, 'ctx', split_axis=0, concat_axis=0, tiled=True)  13.7 us
    all_to_all x1, waiting for transfers between devices, local(): kv = lax.all_to_all(kv, 'tp', split_axis=1, concat_axis=0, tiled=True)  7.27 us
    all_to_all x1, starting transfers between devices, local(): kv = lax.all_to_all(kv, 'tp', split_axis=1, concat_axis=0, tiled=True)  6.32 us
    ppermute x1, starting transfers between devices, passed_along(): return lax.ppermute(shard, axis, pairs)  5.89 us
    gather x1, local copies, waits for them, and re-layouts, rotation_tables(): jnp.take(table, jnp.clip(offsets, 0, distinct - 1), axis=0, mode='clip')  5.75 us
    gather x2, local copies, waits for them, and re-layouts, local(): jnp.take(a, my_sources, axis=0, mode='clip')  5.2 us
  transfers between devices with their start and end apart: 4, of which 3 were waited for; matrix products, arithmetic and copies ran while one was open for 7% of the time, Pallas kernels for 13%

profile of v7, /device:TPU:1, one launch (start us, length us, event | category | flops | bytes accessed | tf_op | source)
XLA Modules:
  0.0 199.4 jit_solution(8818350867199358551)
XLA Ops:
  0.0 1.2 copy.22
  1.2 0.1 copy.23
  1.3 0.1 pad_maximum_fusion.1
  1.4 1.1 copy.19
  2.5 1.5 all_to_all.20
  4.0 6.3 %all-to-all-start = ((bf16[256,8,256]{2,0,1:T(8,128)(2,1)}), bf16[256,8,256]{2,0,1:T(8,128)(2,1)}, u32[]{:S(2)}, u32[]{:S(2)}) async-start(bf16[256,8,256]{2,0,1:T(8,128)(2,1)} %all_to_all.20), calls=%async_computation | async-start | bytes 2097152 | tf_op jit(solution)/shard_map/all_to_all | solution.py:155
  10.3 0.1 copy.17
  10.5 0.2 reduce-window.8
  10.6 0.1 reduce.1
  10.8 0.5 multiply_cosine_fusion
  11.4 0.2 copy.18
  11.6 1.6 select_reduce_fusion
  13.3 5.8 %gather_fusion = f32[2560,256]{1,0:T(8,128)S(1)} fusion(f32[512,256]{1,0:T(8,128)S(1)} %copy.18, s32[3072]{0:T(1024)S(1)} %pad_clamp_fusion), kind=kCustom, calls=%fused_computation | custom fusion | bytes 5253120 | tf_op jit(solution)/shard_map/jit(_take)/gather | solution.py:39
  19.0 7.3 %all-to-all-done = bf16[256,8,256]{2,0,1:T(8,128)(2,1)} async-done(((bf16[256,8,256]{2,0,1:T(8,128)(2,1)}), bf16[256,8,256]{2,0,1:T(8,128)(2,1)}, u32[]{:S(2)}, u32[]{:S(2)}) %all-to-all-start) | async-done | bytes 1048608 | tf_op jit(solution)/shard_map/all_to_all | solution.py:155
  26.3 1.0 slice.59
  27.3 5.9 %collective-permute-start = (bf16[512,256]{1,0:T(8,128)(2,1)S(1)}, bf16[512,256]{1,0:T(8,128)(2,1)S(1)}, u32[]{:S(2)}, u32[]{:S(2)}) collective-permute-start(bf16[512,256]{1,0:T(8,128)(2,1)S(1)} %bitcast.22), channel_id=1, source_target_pairs={{0,8},{8,16},{16,24},{24,32},{32,40},{40,48},{48,56},{56,64},{64,7... | collective-permute-start | bytes 786440 | tf_op jit(solution)/shard_map/ppermute | solution.py:17
  33.2 1.5 fusion.10
  34.7 1.4 copy.20.refs_6_.refs_10_
  36.1 0.7 dynamic-slice_reduce_fusion.dest_ref
  36.9 2.2 %pad_maximum_fusion.2 = (bf16[2560,128]{1,0:T(8,128)(2,1)}, f32[2560,128]{1,0:T(8,128)S(1)}) fusion(bf16[2048,256]{1,0:T(8,128)(2,1)} %bitcast.3, bf16[512,256]{1,0:T(8,128)(2,1)S(1)} %collective-permute-done), kind=kLoop, calls=%fused_computation.14 | loop fusion | flops 2621440 | bytes 3276800 | tf_op jit(solution)/shard_map/concatenate | solution.py:157
  39.0 0.4 fusion.11
  39.4 2.5 %fusion.1.refs_4_.refs_8_ = bf16[2560,128]{1,0:T(8,128)(2,1)} fusion(f32[2560,256]{1,0:T(8,128)S(1)} %gather_fusion, f32[2560,64]{1,0:T(8,128)S(1)} %get-tuple-element.10, f32[2560,64]{1,0:T(8,128)S(1)} %get-tuple-element.9, bf16[2048,256]{1,0:T(8,128)(2,1)} %bitcast.3, bf16[512,256]{1,0:T(8,128)(2,1)S(1)} %collective-permute-done), kind=kLoop, calls=%fused_computation.6 | loop fusion | flops 2949120 | bytes 5898240 | tf_op jit(solution)/shard_map/convert_element_type | solution.py:169
  41.9 12.9 %shard_map.64 = bf16[16,256,256]{2,1,0:T(8,128)(2,1)} custom-call(s32[8]{0:T(128)} %dynamic-slice_reduce_fusion.dest_ref, bf16[2048,1024]{1,0:T(8,128)(2,1)} %refs_5_.1, bf16[2048,1024]{1,0:T(8,128)(2,1)} %refs_5_.1, f32[2048,128]{1,0:T(8,128)} %get-tuple-element.6.refs_2_.refs_6_, f32[2048,128]{1,0:T(8,128)} %get-tuple-element.5.refs_3_.refs_7_, ...), custom_call_target="tpu_custom_call" | custom-call | flops 1610612736 | bytes 3407872 | tf_op jit(solution)/shard_map/pallas_call | solution.py:121
  54.8 7.9 %all-to-all-start.1 = ((bf16[16,256,256]{2,1,0:T(8,128)(2,1)}), bf16[16,256,256]{2,1,0:T(8,128)(2,1)S(1)}, u32[]{:S(2)}, u32[]{:S(2)}) async-start(bf16[16,256,256]{2,1,0:T(8,128)(2,1)} %shard_map.64), calls=%async_computation.1 | async-start | bytes 4194304 | tf_op jit(solution)/shard_map/all_to_all | solution.py:187
  62.7 26.9 %shard_map.65 = bf16[16,256,768]{2,1,0:T(8,128)(2,1)} custom-call(s32[8]{0:T(128)} %dynamic-slice_reduce_fusion.dest_ref, bf16[2048,1024]{1,0:T(8,128)(2,1)} %refs_5_.1, bf16[2048,1024]{1,0:T(8,128)(2,1)} %refs_5_.1, bf16[2048,1024]{1,0:T(8,128)(2,1)} %refs_5_.1, bf16[2048,1024]{1,0:T(8,128)(2,1)} %refs_5_.1, bf16[2048,1024]{1,0:T(8,128)(2,1)} %refs_5_.1, ...), custom_call_target="tpu_custom_call" | custom-call | flops 4831838208 | bytes 7602176 | tf_op jit(solution)/shard_map/pallas_call | solution.py:121
  89.6 1.4 all-to-all-done.1
  91.0 5.8 %all-to-all-start.2 = ((bf16[16,256,768]{2,1,0:T(8,128)(2,1)}), bf16[16,256,768]{2,1,0:T(8,128)(2,1)}, u32[]{:S(2)}, u32[]{:S(2)}) async-start(bf16[16,256,768]{2,1,0:T(8,128)(2,1)} %shard_map.65), calls=%async_computation.2 | async-start | bytes 12582912 | tf_op jit(solution)/shard_map/all_to_all | solution.py:187
  96.8 0.1 select_reduce_fusion.1
  97.0 1.7 gather_fusion.1
  98.6 93.4 %all-to-all-done.2 = bf16[16,256,768]{2,1,0:T(8,128)(2,1)} async-done(((bf16[16,256,768]{2,1,0:T(8,128)(2,1)}), bf16[16,256,768]{2,1,0:T(8,128)(2,1)}, u32[]{:S(2)}, u32[]{:S(2)}) %all-to-all-start.2) | async-done | bytes 6291488 | tf_op jit(solution)/shard_map/all_to_all | solution.py:187
  192.0 3.5 %gather_fusion.2 = bf16[8,256,768]{2,1,0:T(8,128)(2,1)S(1)} fusion(bf16[16,256,768]{2,1,0:T(8,128)(2,1)} %all-to-all-done.2, s32[1024]{0:T(1024)S(1)} %pad_clamp_fusion.1), kind=kCustom, calls=%fused_computation.2 | custom fusion | bytes 6291488 | tf_op jit(solution)/shard_map/jit(_take)/gather | solution.py:198
  195.6 3.8 %pad_maximum_fusion = bf16[8,256,1024]{2,1,0:T(8,128)(2,1)} fusion(bf16[8,256,768]{2,1,0:T(8,128)(2,1)S(1)} %gather_fusion.2, bf16[8,256,256]{2,1,0:T(8,128)(2,1)} %gather_fusion.1), kind=kLoop, calls=%fused_computation.3 | loop fusion | flops 8388608 | bytes 8388608 | tf_op jit(solution)/shard_map/dynamic_update_slice | solution.py:197
  (18 shorter events, 0.2 us)
Async XLA Ops:
  0.0 1.2 copy-start
  4.0 6.3 %copy-start.2 = (s32[128]{0:T(128)S(1)}, s32[128]{0:T(128)}, u32[]{:S(2)}) copy-start(s32[128]{0:T(128)} %param.10) | copy-start | bytes 1540
  4.0 6.7 %copy-start.3 = (f32[64]{0:T(128)S(1)}, f32[64]{0:T(128)}, u32[]{:S(2)}) copy-start(f32[64]{0:T(128)} %param.9) | copy-start | bytes 772
  4.0 22.3 %all-to-all-start = ((bf16[256,8,256]{2,0,1:T(8,128)(2,1)}), bf16[256,8,256]{2,0,1:T(8,128)(2,1)}, u32[]{:S(2)}, u32[]{:S(2)}) async-start(bf16[256,8,256]{2,0,1:T(8,128)(2,1)} %all_to_all.20), calls=%async_computation | async-start | bytes 2097152 | tf_op jit(solution)/shard_map/all_to_all | solution.py:155
  27.3 8.9 %copy-start.1 = (s32[16,8]{0,1:T(8,128)S(1)}, s32[16,8]{0,1:T(8,128)}, u32[]{:S(2)}) copy-start(s32[16,8]{0,1:T(8,128)} %param.11) | copy-start | bytes 1540
  27.3 9.6 %collective-permute-start = (bf16[512,256]{1,0:T(8,128)(2,1)S(1)}, bf16[512,256]{1,0:T(8,128)(2,1)S(1)}, u32[]{:S(2)}, u32[]{:S(2)}) collective-permute-start(bf16[512,256]{1,0:T(8,128)(2,1)S(1)} %bitcast.22), channel_id=1, source_target_pairs={{0,8},{8,16},{16,24},{24,32},{32,40},{40,48},{48,56},{56,64},{64,7... | collective-permute-start | bytes 786440 | tf_op jit(solution)/shard_map/ppermute | solution.py:17
  54.8 36.2 %all-to-all-start.1 = ((bf16[16,256,256]{2,1,0:T(8,128)(2,1)}), bf16[16,256,256]{2,1,0:T(8,128)(2,1)S(1)}, u32[]{:S(2)}, u32[]{:S(2)}) async-start(bf16[16,256,256]{2,1,0:T(8,128)(2,1)} %shard_map.64), calls=%async_computation.1 | async-start | bytes 4194304 | tf_op jit(solution)/shard_map/all_to_all | solution.py:187
  91.0 101.0 %all-to-all-start.2 = ((bf16[16,256,768]{2,1,0:T(8,128)(2,1)}), bf16[16,256,768]{2,1,0:T(8,128)(2,1)}, u32[]{:S(2)}, u32[]{:S(2)}) async-start(bf16[16,256,768]{2,1,0:T(8,128)(2,1)} %shard_map.65), calls=%async_computation.2 | async-start | bytes 12582912 | tf_op jit(solution)/shard_map/all_to_all | solution.py:187

commit v8 on v7

--- a/solution.py
+++ b/solution.py
@@ -177,7 +177,7 @@
     owner_row = lax.dynamic_index_in_dim(owner_map, ctx_index, 0, keepdims=False)
 
     q_heads = queries.shape[1] // head_dim
-    sizes = [2, 6] if q_heads == 8 else [q_heads]
+    sizes = [3, 3, 2] if q_heads == 8 else [q_heads]
     arrived = []
     first = 0
     for heads in sizes:

time: 202 us -> 195 us (0.965)
  waiting for transfers between devices: 102 us -> 73.1 us
  local copies, waits for them, and re-layouts: 20.2 us -> 30.6 us
  starting transfers between devices: 25.9 us -> 35.9 us
  Pallas kernels: 39.8 us -> 45.4 us
  other arithmetic: 11.2 us -> 7.5 us
    all_to_all x2 -> x3, waiting for transfers between devices: 94.9 us -> 65.8 us  [local(): lax.all_to_all(send, 'ctx', split_axis=0, concat_axis=0, tiled=True)]
    all_to_all x2 -> x3, starting transfers between devices: 13.7 us -> 23.6 us  [local(): lax.all_to_all(send, 'ctx', split_axis=0, concat_axis=0, tiled=True)]
    dynamic_update_slice x0 -> x3, local copies, waits for them, and re-layouts: none -> 6.34 us  [local(): lax.dynamic_update_slice(finished, jnp.take(a, my_sources, axis=0, mode='...]
    pallas_call x2 -> x3, Pallas kernels: 39.8 us -> 45.4 us  [attend(): pl.pallas_call(kernel, grid_spec=grid_spec, out_shape=jax.ShapeDtypeStruc...]
    dynamic_update_slice x1 -> x0, other arithmetic: 3.79 us -> none  [local(): lax.dynamic_update_slice(finished, jnp.take(a, my_sources, axis=0, mode='...]
    gather x2 -> x3, local copies, waits for them, and re-layouts: 5.2 us -> 7.95 us  [local(): jnp.take(a, my_sources, axis=0, mode='clip')]
  transfers between devices with their start and end apart: 4 -> 5, of which waited for: 3 -> 4; matrix products, arithmetic and copies ran while one was open for 7% -> 11% of each run, Pallas kernels for 13% -> 17%
where the time goes in v8:
time: 195 us; the launch traced here: 193 us
  waiting for transfers between devices  73.1 us (37%)
  Pallas kernels  45.4 us (23%)
  starting transfers between devices  35.9 us (18%)
  local copies, waits for them, and re-layouts  30.6 us (16%)
  other arithmetic  7.5 us (4%)
    all_to_all x3, waiting for transfers between devices, local(): lax.all_to_all(send, 'ctx', split_axis=0, concat_axis=0, tiled=True)  65.8 us
    pallas_call x3, Pallas kernels, attend(): pl.pallas_call(kernel, grid_spec=grid_spec, out_shape=jax.ShapeDtypeStruc...  45.4 us
    all_to_all x3, starting transfers between devices, local(): lax.all_to_all(send, 'ctx', split_axis=0, concat_axis=0, tiled=True)  23.6 us
    gather x3, local copies, waits for them, and re-layouts, local(): jnp.take(a, my_sources, axis=0, mode='clip')  7.95 us
    all_to_all x1, waiting for transfers between devices, local(): kv = lax.all_to_all(kv, 'tp', split_axis=1, concat_axis=0, tiled=True)  7.27 us
    dynamic_update_slice x3, local copies, waits for them, and re-layouts, local(): lax.dynamic_update_slice(finished, jnp.take(a, my_sources, axis=0, mode='...  6.34 us
    all_to_all x1, starting transfers between devices, local(): kv = lax.all_to_all(kv, 'tp', split_axis=1, concat_axis=0, tiled=True)  6.32 us
    ppermute x1, starting transfers between devices, passed_along(): return lax.ppermute(shard, axis, pairs)  5.89 us
  transfers between devices with their start and end apart: 5, of which 4 were waited for; matrix products, arithmetic and copies ran while one was open for 11% of the time, Pallas kernels for 17%

profile of v8, /device:TPU:1, one launch (start us, length us, event | category | flops | bytes accessed | tf_op | source)
XLA Modules:
  0.0 192.7 jit_solution(6376149365217316045)
XLA Ops:
  0.0 1.2 copy.25
  1.4 1.1 copy.21
  2.5 1.5 all_to_all.23
  4.0 6.3 %all-to-all-start = ((bf16[256,8,256]{2,0,1:T(8,128)(2,1)}), bf16[256,8,256]{2,0,1:T(8,128)(2,1)}, u32[]{:S(2)}, u32[]{:S(2)}) async-start(bf16[256,8,256]{2,0,1:T(8,128)(2,1)} %all_to_all.23), calls=%async_computation | async-start | bytes 2097152 | tf_op jit(solution)/shard_map/all_to_all | solution.py:155
  10.8 0.5 multiply_cosine_fusion
  11.6 1.6 select_reduce_fusion
  13.3 5.8 %gather_fusion = f32[2560,256]{1,0:T(8,128)S(1)} fusion(f32[512,256]{1,0:T(8,128)S(1)} %copy.20, s32[3072]{0:T(1024)S(1)} %pad_clamp_fusion), kind=kCustom, calls=%fused_computation | custom fusion | bytes 5253120 | tf_op jit(solution)/shard_map/jit(_take)/gather | solution.py:39
  19.0 7.3 %all-to-all-done = bf16[256,8,256]{2,0,1:T(8,128)(2,1)} async-done(((bf16[256,8,256]{2,0,1:T(8,128)(2,1)}), bf16[256,8,256]{2,0,1:T(8,128)(2,1)}, u32[]{:S(2)}, u32[]{:S(2)}) %all-to-all-start) | async-done | bytes 1048608 | tf_op jit(solution)/shard_map/all_to_all | solution.py:155
  26.3 1.0 slice.61
  27.3 5.9 %collective-permute-start = (bf16[512,256]{1,0:T(8,128)(2,1)S(1)}, bf16[512,256]{1,0:T(8,128)(2,1)S(1)}, u32[]{:S(2)}, u32[]{:S(2)}) collective-permute-start(bf16[512,256]{1,0:T(8,128)(2,1)S(1)} %bitcast.22), channel_id=1, source_target_pairs={{0,8},{8,16},{16,24},{24,32},{32,40},{40,48},{48,56},{56,64},{64,7... | collective-permute-start | bytes 786440 | tf_op jit(solution)/shard_map/ppermute | solution.py:17
  33.2 1.5 fusion.10
  34.7 1.4 copy.22.refs_7_.refs_6_
  36.1 0.7 dynamic-slice_reduce_fusion.dest_ref
  36.7 2.2 %pad_maximum_fusion.1 = (bf16[2560,128]{1,0:T(8,128)(2,1)}, f32[2560,128]{1,0:T(8,128)S(1)}) fusion(bf16[2048,256]{1,0:T(8,128)(2,1)} %bitcast.3, bf16[512,256]{1,0:T(8,128)(2,1)S(1)} %collective-permute-done), kind=kLoop, calls=%fused_computation.14 | loop fusion | flops 2621440 | bytes 3276800 | tf_op jit(solution)/shard_map/concatenate | solution.py:157
  39.0 0.4 fusion.11
  39.4 2.5 %fusion.1.refs_5_.refs_4_ = bf16[2560,128]{1,0:T(8,128)(2,1)} fusion(f32[2560,256]{1,0:T(8,128)S(1)} %gather_fusion, f32[2560,64]{1,0:T(8,128)S(1)} %get-tuple-element.10, f32[2560,64]{1,0:T(8,128)S(1)} %get-tuple-element.9, bf16[2048,256]{1,0:T(8,128)(2,1)} %bitcast.3, bf16[512,256]{1,0:T(8,128)(2,1)S(1)} %collective-permute-done), kind=kLoop, calls=%fused_computation.6 | loop fusion | flops 2949120 | bytes 5898240 | tf_op jit(solution)/shard_map/convert_element_type | solution.py:169
  41.9 12.9 %shard_map.66 = bf16[16,256,256]{2,1,0:T(8,128)(2,1)} custom-call(s32[8]{0:T(128)} %dynamic-slice_reduce_fusion.dest_ref, bf16[2048,1024]{1,0:T(8,128)(2,1)} %refs_1_.5, bf16[2048,1024]{1,0:T(8,128)(2,1)} %refs_1_.5, f32[2048,128]{1,0:T(8,128)} %get-tuple-element.6.refs_3_.refs_2_, f32[2048,128]{1,0:T(8,128)} %get-tuple-element.5.refs_4_.refs_3_, ...), custom_call_target="tpu_custom_call" | custom-call | flops 1610612736 | bytes 3407872 | tf_op jit(solution)/shard_map/pallas_call | solution.py:121
  54.8 8.0 %all-to-all-start.3 = ((bf16[16,256,256]{2,1,0:T(8,128)(2,1)}), bf16[16,256,256]{2,1,0:T(8,128)(2,1)S(1)}, u32[]{:S(2)}, u32[]{:S(2)}) async-start(bf16[16,256,256]{2,1,0:T(8,128)(2,1)} %shard_map.66), calls=%async_computation.3 | async-start | bytes 4194304 | tf_op jit(solution)/shard_map/all_to_all | solution.py:187
  62.8 16.3 %shard_map.64 = bf16[16,256,384]{2,1,0:T(8,128)(2,1)} custom-call(s32[8]{0:T(128)} %dynamic-slice_reduce_fusion.dest_ref, bf16[2048,1024]{1,0:T(8,128)(2,1)} %refs_1_.5, bf16[2048,1024]{1,0:T(8,128)(2,1)} %refs_1_.5, bf16[2048,1024]{1,0:T(8,128)(2,1)} %refs_1_.5, f32[2048,128]{1,0:T(8,128)} %get-tuple-element.6.refs_3_.refs_2_, ...), custom_call_target="tpu_custom_call" | custom-call | flops 2415919104 | bytes 4456448 | tf_op jit(solution)/shard_map/pallas_call | solution.py:121
  79.0 12.1 %all-to-all-done.3 = bf16[16,256,256]{2,1,0:T(8,128)(2,1)S(1)} async-done(((bf16[16,256,256]{2,1,0:T(8,128)(2,1)}), bf16[16,256,256]{2,1,0:T(8,128)(2,1)S(1)}, u32[]{:S(2)}, u32[]{:S(2)}) %all-to-all-start.3) | async-done | bytes 2097184 | tf_op jit(solution)/shard_map/all_to_all | solution.py:187
  91.1 1.3 copy-done
  92.4 5.8 %all-to-all-start.1 = ((bf16[16,256,384]{2,1,0:T(8,128)(2,1)}), bf16[16,256,384]{2,1,0:T(8,128)(2,1)S(1)}, u32[]{:S(2)}, u32[]{:S(2)}) async-start(bf16[16,256,384]{2,1,0:T(8,128)(2,1)} %shard_map.64), calls=%async_computation.1 | async-start | bytes 6291456 | tf_op jit(solution)/shard_map/all_to_all | solution.py:187
  98.3 16.2 %shard_map.65 = bf16[16,256,384]{2,1,0:T(8,128)(2,1)} custom-call(s32[8]{0:T(128)} %dynamic-slice_reduce_fusion.dest_ref, bf16[2048,1024]{1,0:T(8,128)(2,1)} %refs_1_.5, bf16[2048,1024]{1,0:T(8,128)(2,1)} %refs_1_.5, bf16[2048,1024]{1,0:T(8,128)(2,1)} %refs_1_.5, f32[2048,128]{1,0:T(8,128)} %get-tuple-element.6.refs_3_.refs_2_, ...), custom_call_target="tpu_custom_call" | custom-call | flops 2415919104 | bytes 4456448 | tf_op jit(solution)/shard_map/pallas_call | solution.py:121
  114.5 23.3 %all-to-all-done.1 = bf16[16,256,384]{2,1,0:T(8,128)(2,1)S(1)} async-done(((bf16[16,256,384]{2,1,0:T(8,128)(2,1)}), bf16[16,256,384]{2,1,0:T(8,128)(2,1)S(1)}, u32[]{:S(2)}, u32[]{:S(2)}) %all-to-all-start.1) | async-done | bytes 3145760 | tf_op jit(solution)/shard_map/all_to_all | solution.py:187
  137.8 9.8 %all-to-all-start.2 = ((bf16[16,256,384]{2,1,0:T(8,128)(2,1)}), bf16[16,256,384]{2,1,0:T(8,128)(2,1)}, u32[]{:S(2)}, u32[]{:S(2)}) async-start(bf16[16,256,384]{2,1,0:T(8,128)(2,1)} %shard_map.65), calls=%async_computation.2 | async-start | bytes 6291456 | tf_op jit(solution)/shard_map/all_to_all | solution.py:187
  147.8 3.3 %gather_fusion.3 = bf16[8,256,256]{2,1,0:T(8,128)(2,1)} fusion(bf16[16,256,256]{2,1,0:T(8,128)(2,1)} %copy-done, s32[1024]{0:T(1024)S(1)} %pad_clamp_fusion.1), kind=kCustom, calls=%fused_computation.3 | custom fusion | bytes 2097184 | tf_op jit(solution)/shard_map/jit(_take)/gather | solution.py:198
  151.0 1.9 gather_fusion.1
  153.0 4.0 %dynamic_update_slice.9 = bf16[8,256,1024]{2,1,0:T(8,128)(2,1)} pad(bf16[8,256,384]{2,1,0:T(8,128)(2,1)} %gather_fusion.1, bf16[]{:T(256)} %constant.50.clone.1), padding=0_0x0_0x0_640 | pad | bytes 5767170 | tf_op jit(solution)/shard_map/dynamic_update_slice | solution.py:197
  156.9 30.4 %all-to-all-done.2 = bf16[16,256,384]{2,1,0:T(8,128)(2,1)} async-done(((bf16[16,256,384]{2,1,0:T(8,128)(2,1)}), bf16[16,256,384]{2,1,0:T(8,128)(2,1)}, u32[]{:S(2)}, u32[]{:S(2)}) %all-to-all-start.2) | async-done | bytes 3145760 | tf_op jit(solution)/shard_map/all_to_all | solution.py:187
  187.4 2.8 %gather_fusion.2 = bf16[8,256,384]{2,1,0:T(8,128)(2,1)S(1)} fusion(bf16[16,256,384]{2,1,0:T(8,128)(2,1)} %all-to-all-done.2, s32[1024]{0:T(1024)S(1)} %pad_clamp_fusion.1), kind=kCustom, calls=%fused_computation.2 | custom fusion | bytes 3145760 | tf_op jit(solution)/shard_map/jit(_take)/gather | solution.py:198
  190.2 1.3 constant_dynamic-update-slice_fusion
  191.6 1.0 constant_dynamic-update-slice_fusion.1
  (28 shorter events, 1.2 us)
Async XLA Ops:
  0.0 1.2 copy-start.2
  4.0 6.3 %copy-start.4 = (s32[128]{0:T(128)S(1)}, s32[128]{0:T(128)}, u32[]{:S(2)}) copy-start(s32[128]{0:T(128)} %param.10) | copy-start | bytes 1540
  4.0 6.7 %copy-start.5 = (f32[64]{0:T(128)S(1)}, f32[64]{0:T(128)}, u32[]{:S(2)}) copy-start(f32[64]{0:T(128)} %param.9) | copy-start | bytes 772
  4.0 22.3 %all-to-all-start = ((bf16[256,8,256]{2,0,1:T(8,128)(2,1)}), bf16[256,8,256]{2,0,1:T(8,128)(2,1)}, u32[]{:S(2)}, u32[]{:S(2)}) async-start(bf16[256,8,256]{2,0,1:T(8,128)(2,1)} %all_to_all.23), calls=%async_computation | async-start | bytes 2097152 | tf_op jit(solution)/shard_map/all_to_all | solution.py:155
  27.3 8.8 %copy-start.3 = (s32[16,8]{0,1:T(8,128)S(1)}, s32[16,8]{0,1:T(8,128)}, u32[]{:S(2)}) copy-start(s32[16,8]{0,1:T(8,128)} %param.11) | copy-start | bytes 1540
  27.3 9.5 %collective-permute-start = (bf16[512,256]{1,0:T(8,128)(2,1)S(1)}, bf16[512,256]{1,0:T(8,128)(2,1)S(1)}, u32[]{:S(2)}, u32[]{:S(2)}) collective-permute-start(bf16[512,256]{1,0:T(8,128)(2,1)S(1)} %bitcast.22), channel_id=1, source_target_pairs={{0,8},{8,16},{16,24},{24,32},{32,40},{40,48},{48,56},{56,64},{64,7... | collective-permute-start | bytes 786440 | tf_op jit(solution)/shard_map/ppermute | solution.py:17
  54.8 36.3 %all-to-all-start.3 = ((bf16[16,256,256]{2,1,0:T(8,128)(2,1)}), bf16[16,256,256]{2,1,0:T(8,128)(2,1)S(1)}, u32[]{:S(2)}, u32[]{:S(2)}) async-start(bf16[16,256,256]{2,1,0:T(8,128)(2,1)} %shard_map.66), calls=%async_computation.3 | async-start | bytes 4194304 | tf_op jit(solution)/shard_map/all_to_all | solution.py:187
  91.1 1.3 copy-start
  92.4 45.4 %all-to-all-start.1 = ((bf16[16,256,384]{2,1,0:T(8,128)(2,1)}), bf16[16,256,384]{2,1,0:T(8,128)(2,1)S(1)}, u32[]{:S(2)}, u32[]{:S(2)}) async-start(bf16[16,256,384]{2,1,0:T(8,128)(2,1)} %shard_map.64), calls=%async_computation.1 | async-start | bytes 6291456 | tf_op jit(solution)/shard_map/all_to_all | solution.py:187
  137.8 49.5 %all-to-all-start.2 = ((bf16[16,256,384]{2,1,0:T(8,128)(2,1)}), bf16[16,256,384]{2,1,0:T(8,128)(2,1)}, u32[]{:S(2)}, u32[]{:S(2)}) async-start(bf16[16,256,384]{2,1,0:T(8,128)(2,1)} %shard_map.65), calls=%async_computation.2 | async-start | bytes 6291456 | tf_op jit(solution)/shard_map/all_to_all | solution.py:187
  190.2 1.5 copy-start.1

commit v9 on v6

--- a/solution.py
+++ b/solution.py
@@ -145,17 +145,18 @@
     kv_local = kv_heads // tp_size
     shard_rows = keys.shape[0]
 
-    kv = jnp.stack(
+    kv_width = kv_local * head_dim
+    kv = jnp.concatenate(
         [
-            keys.reshape(shard_rows, tp_size, kv_local * head_dim),
-            values.reshape(shard_rows, tp_size, kv_local * head_dim),
+            keys.reshape(shard_rows, tp_size, kv_width).transpose(1, 0, 2),
+            values.reshape(shard_rows, tp_size, kv_width).transpose(1, 0, 2),
         ],
         axis=2,
-    ).reshape(shard_rows, tp_size * 2 * kv_local * head_dim)
-    kv = lax.all_to_all(kv, "tp", split_axis=1, concat_axis=0, tiled=True)
+    )
+    kv = lax.all_to_all(kv, "tp", split_axis=0, concat_axis=0, tiled=True)
+    kv = kv.reshape(row_count, 2 * kv_width)
     kv_tail = passed_along(kv[row_count - tail_rows :], "ctx", 1)
     kv_ext = jnp.concatenate([kv_tail, kv], axis=0)
-    kv_width = kv_local * head_dim
     k_raw = kv_ext[:, :kv_width]
     v_ext = kv_ext[:, kv_width:]
 

time: 194 us -> 190 us (0.979)
  local copies, waits for them, and re-layouts: 32.1 us -> 30.1 us
    all_to_all x3, waiting for transfers between devices: 63.3 us -> 65.6 us  [local(): lax.all_to_all(send, 'ctx', split_axis=0, concat_axis=0, tiled=True)]
where the time goes in v9:
time: 190 us; the launch traced here: 188 us
  waiting for transfers between devices  71.5 us (38%)
  Pallas kernels  45.4 us (24%)
  starting transfers between devices  34.2 us (18%)
  local copies, waits for them, and re-layouts  30.1 us (16%)
  other arithmetic  6.19 us (3%)
    all_to_all x3, waiting for transfers between devices, local(): lax.all_to_all(send, 'ctx', split_axis=0, concat_axis=0, tiled=True)  65.6 us
    pallas_call x3, Pallas kernels, attend(): pl.pallas_call(kernel, grid_spec=grid_spec, out_shape=jax.ShapeDtypeStruc...  45.4 us
    all_to_all x3, starting transfers between devices, local(): lax.all_to_all(send, 'ctx', split_axis=0, concat_axis=0, tiled=True)  22 us
    gather x3, local copies, waits for them, and re-layouts, local(): jnp.take(a, my_sources, axis=0, mode='clip')  7.14 us
    gather x1, local copies, waits for them, and re-layouts, rotation_tables(): jnp.take(table, jnp.clip(offsets, 0, distinct - 1), axis=0, mode='clip')  7.01 us
    dynamic_update_slice x3, local copies, waits for them, and re-layouts, local(): lax.dynamic_update_slice(finished, jnp.take(a, my_sources, axis=0, mode='...  6.43 us
    all_to_all x1, starting transfers between devices, local(): kv = lax.all_to_all(kv, 'tp', split_axis=0, concat_axis=0, tiled=True)  6.32 us
    all_to_all x1, waiting for transfers between devices, local(): kv = lax.all_to_all(kv, 'tp', split_axis=0, concat_axis=0, tiled=True)  5.91 us
  transfers between devices with their start and end apart: 5, of which 4 were waited for; matrix products, arithmetic and copies ran while one was open for 13% of the time, Pallas kernels for 17%

profile of v9, /device:TPU:1, one launch (start us, length us, event | category | flops | bytes accessed | tf_op | source)
XLA Modules:
  0.0 187.7 jit_solution(11517017203373167881)
XLA Ops:
  0.0 1.0 copy-done
  1.0 1.3 bitcast_bitcast_fusion
  2.3 1.1 pad_maximum_fusion
  3.4 6.3 %all-to-all-start = ((bf16[8,256,256]{2,1,0:T(8,128)(2,1)}), bf16[8,256,256]{2,1,0:T(8,128)(2,1)S(1)}, u32[]{:S(2)}, u32[]{:S(2)}) async-start(bf16[8,256,256]{2,1,0:T(8,128)(2,1)} %pad_maximum_fusion), calls=%async_computation | async-start | bytes 2097152 | tf_op jit(solution)/shard_map/all_to_all | solution.py:156
  10.2 0.5 multiply_cosine_fusion
  10.8 0.2 copy.23
  11.0 1.6 select_reduce_fusion
  12.7 7.0 %gather_fusion = f32[2560,256]{1,0:T(8,128)} fusion(f32[512,256]{1,0:T(8,128)S(1)} %copy.23, s32[3072]{0:T(1024)S(1)} %pad_clamp_fusion), kind=kCustom, calls=%fused_computation | custom fusion | bytes 5253120 | tf_op jit(solution)/shard_map/jit(_take)/gather | solution.py:39
  19.7 5.9 %all-to-all-done = bf16[8,256,256]{2,1,0:T(8,128)(2,1)S(1)} async-done(((bf16[8,256,256]{2,1,0:T(8,128)(2,1)}), bf16[8,256,256]{2,1,0:T(8,128)(2,1)S(1)}, u32[]{:S(2)}, u32[]{:S(2)}) %all-to-all-start) | async-done | bytes 1048608 | tf_op jit(solution)/shard_map/all_to_all | solution.py:156
  25.7 5.9 %collective-permute-start = (bf16[512,256]{1,0:T(8,128)(2,1)S(1)}, bf16[512,256]{1,0:T(8,128)(2,1)S(1)}, u32[]{:S(2)}, u32[]{:S(2)}) collective-permute-start(bf16[512,256]{1,0:T(8,128)(2,1)S(1)} %bitcast.22), channel_id=1, source_target_pairs={{0,8},{8,16},{16,24},{24,32},{32,40},{40,48},{48,56},{56,64},{64,7... | collective-permute-start | bytes 786440 | tf_op jit(solution)/shard_map/ppermute | solution.py:17
  31.6 3.0 %fusion.10 = (f32[2048,128]{1,0:T(8,128)}, f32[2048,128]{1,0:T(8,128)}) fusion(f32[2560,256]{1,0:T(8,128)} %gather_fusion), kind=kLoop, calls=%fused_computation.42 | loop fusion | bytes 4194304 | tf_op jit(solution)/shard_map/slice | solution.py:172
  34.6 1.4 copy.26.refs_6_.refs_7_
  36.0 0.7 dynamic-slice_reduce_fusion.dest_ref
  36.8 1.0 pad_maximum_fusion.1
  37.8 0.4 fusion.11
  38.2 1.3 copy-done.1
  39.5 1.4 fusion.1.refs_4_.refs_5_
  40.9 12.9 %shard_map.64 = bf16[16,256,256]{2,1,0:T(8,128)(2,1)} custom-call(s32[8]{0:T(128)} %dynamic-slice_reduce_fusion.dest_ref, bf16[2048,1024]{1,0:T(8,128)(2,1)} %refs_2_.3, bf16[2048,1024]{1,0:T(8,128)(2,1)} %refs_2_.3, f32[2048,128]{1,0:T(8,128)} %get-tuple-element.6.refs_2_.refs_3_, f32[2048,128]{1,0:T(8,128)} %get-tuple-element.5.refs_3_.refs_4_, ...), custom_call_target="tpu_custom_call" | custom-call | flops 1610612736 | bytes 3407872 | tf_op jit(solution)/shard_map/pallas_call | solution.py:121
  53.8 6.4 %all-to-all-start.1 = ((bf16[16,256,256]{2,1,0:T(8,128)(2,1)}), bf16[16,256,256]{2,1,0:T(8,128)(2,1)S(1)}, u32[]{:S(2)}, u32[]{:S(2)}) async-start(bf16[16,256,256]{2,1,0:T(8,128)(2,1)} %shard_map.64), calls=%async_computation.1 | async-start | bytes 4194304 | tf_op jit(solution)/shard_map/all_to_all | solution.py:188
  60.2 16.2 %shard_map.65 = bf16[16,256,384]{2,1,0:T(8,128)(2,1)} custom-call(s32[8]{0:T(128)} %dynamic-slice_reduce_fusion.dest_ref, bf16[2048,1024]{1,0:T(8,128)(2,1)} %refs_2_.3, bf16[2048,1024]{1,0:T(8,128)(2,1)} %refs_2_.3, bf16[2048,1024]{1,0:T(8,128)(2,1)} %refs_2_.3, f32[2048,128]{1,0:T(8,128)} %get-tuple-element.6.refs_2_.refs_3_, ...), custom_call_target="tpu_custom_call" | custom-call | flops 2415919104 | bytes 4456448 | tf_op jit(solution)/shard_map/pallas_call | solution.py:121
  76.5 12.1 %all-to-all-done.1 = bf16[16,256,256]{2,1,0:T(8,128)(2,1)S(1)} async-done(((bf16[16,256,256]{2,1,0:T(8,128)(2,1)}), bf16[16,256,256]{2,1,0:T(8,128)(2,1)S(1)}, u32[]{:S(2)}, u32[]{:S(2)}) %all-to-all-start.1) | async-done | bytes 2097184 | tf_op jit(solution)/shard_map/all_to_all | solution.py:188
  88.5 5.8 %all-to-all-start.2 = ((bf16[16,256,384]{2,1,0:T(8,128)(2,1)}), bf16[16,256,384]{2,1,0:T(8,128)(2,1)}, u32[]{:S(2)}, u32[]{:S(2)}) async-start(bf16[16,256,384]{2,1,0:T(8,128)(2,1)} %shard_map.65), calls=%async_computation.2 | async-start | bytes 6291456 | tf_op jit(solution)/shard_map/all_to_all | solution.py:188
  94.3 16.3 %shard_map.66 = bf16[16,256,384]{2,1,0:T(8,128)(2,1)} custom-call(s32[8]{0:T(128)} %dynamic-slice_reduce_fusion.dest_ref, bf16[2048,1024]{1,0:T(8,128)(2,1)} %refs_2_.3, bf16[2048,1024]{1,0:T(8,128)(2,1)} %refs_2_.3, bf16[2048,1024]{1,0:T(8,128)(2,1)} %refs_2_.3, f32[2048,128]{1,0:T(8,128)} %get-tuple-element.6.refs_2_.refs_3_, ...), custom_call_target="tpu_custom_call" | custom-call | flops 2415919104 | bytes 4456448 | tf_op jit(solution)/shard_map/pallas_call | solution.py:121
  110.6 23.4 %all-to-all-done.2 = bf16[16,256,384]{2,1,0:T(8,128)(2,1)} async-done(((bf16[16,256,384]{2,1,0:T(8,128)(2,1)}), bf16[16,256,384]{2,1,0:T(8,128)(2,1)}, u32[]{:S(2)}, u32[]{:S(2)}) %all-to-all-start.2) | async-done | bytes 3145760 | tf_op jit(solution)/shard_map/all_to_all | solution.py:188
  134.0 9.8 %all-to-all-start.3 = ((bf16[16,256,384]{2,1,0:T(8,128)(2,1)}), bf16[16,256,384]{2,1,0:T(8,128)(2,1)}, u32[]{:S(2)}, u32[]{:S(2)}) async-start(bf16[16,256,384]{2,1,0:T(8,128)(2,1)} %shard_map.66), calls=%async_computation.3 | async-start | bytes 6291456 | tf_op jit(solution)/shard_map/all_to_all | solution.py:188
  144.0 1.6 gather_fusion.1
  145.6 3.8 %dynamic_update_slice.9 = bf16[8,256,1024]{2,1,0:T(8,128)(2,1)} pad(bf16[8,256,256]{2,1,0:T(8,128)(2,1)} %gather_fusion.1, bf16[]{:T(256)} %constant.49.clone.1), padding=0_0x0_0x0_768 | pad | bytes 5242882 | tf_op jit(solution)/shard_map/dynamic_update_slice | solution.py:198
  149.3 2.8 %gather_fusion.2 = bf16[8,256,384]{2,1,0:T(8,128)(2,1)S(1)} fusion(bf16[16,256,384]{2,1,0:T(8,128)(2,1)} %all-to-all-done.2, s32[1024]{0:T(1024)S(1)} %pad_clamp_fusion.1), kind=kCustom, calls=%fused_computation.2 | custom fusion | bytes 3145760 | tf_op jit(solution)/shard_map/jit(_take)/gather | solution.py:199
  152.1 1.3 constant_dynamic-update-slice_fusion
  153.4 30.1 %all-to-all-done.3 = bf16[16,256,384]{2,1,0:T(8,128)(2,1)} async-done(((bf16[16,256,384]{2,1,0:T(8,128)(2,1)}), bf16[16,256,384]{2,1,0:T(8,128)(2,1)}, u32[]{:S(2)}, u32[]{:S(2)}) %all-to-all-start.3) | async-done | bytes 3145760 | tf_op jit(solution)/shard_map/all_to_all | solution.py:188
  183.6 2.8 %gather_fusion.3 = bf16[8,256,384]{2,1,0:T(8,128)(2,1)S(1)} fusion(bf16[16,256,384]{2,1,0:T(8,128)(2,1)} %all-to-all-done.3, s32[1024]{0:T(1024)S(1)} %pad_clamp_fusion.1), kind=kCustom, calls=%fused_computation.3 | custom fusion | bytes 3145760 | tf_op jit(solution)/shard_map/jit(_take)/gather | solution.py:199
  186.3 1.3 constant_dynamic-update-slice_fusion.1
  (23 shorter events, 0.7 us)
Async XLA Ops:
  0.0 1.0 copy-start
  3.4 6.3 %copy-start.3 = (s32[128]{0:T(128)S(1)}, s32[128]{0:T(128)}, u32[]{:S(2)}) copy-start(s32[128]{0:T(128)} %param.10) | copy-start | bytes 1540
  3.4 6.7 %copy-start.4 = (f32[64]{0:T(128)S(1)}, f32[64]{0:T(128)}, u32[]{:S(2)}) copy-start(f32[64]{0:T(128)} %param.9) | copy-start | bytes 772
  3.4 22.2 %all-to-all-start = ((bf16[8,256,256]{2,1,0:T(8,128)(2,1)}), bf16[8,256,256]{2,1,0:T(8,128)(2,1)S(1)}, u32[]{:S(2)}, u32[]{:S(2)}) async-start(bf16[8,256,256]{2,1,0:T(8,128)(2,1)} %pad_maximum_fusion), calls=%async_computation | async-start | bytes 2097152 | tf_op jit(solution)/shard_map/all_to_all | solution.py:156
  25.7 10.4 %copy-start.2 = (s32[16,8]{0,1:T(8,128)S(1)}, s32[16,8]{0,1:T(8,128)}, u32[]{:S(2)}) copy-start(s32[16,8]{0,1:T(8,128)} %param.11) | copy-start | bytes 1540
  25.7 11.1 %collective-permute-start = (bf16[512,256]{1,0:T(8,128)(2,1)S(1)}, bf16[512,256]{1,0:T(8,128)(2,1)S(1)}, u32[]{:S(2)}, u32[]{:S(2)}) collective-permute-start(bf16[512,256]{1,0:T(8,128)(2,1)S(1)} %bitcast.22), channel_id=1, source_target_pairs={{0,8},{8,16},{16,24},{24,32},{32,40},{40,48},{48,56},{56,64},{64,7... | collective-permute-start | bytes 786440 | tf_op jit(solution)/shard_map/ppermute | solution.py:17
  37.8 1.7 copy-start.1
  53.8 34.7 %all-to-all-start.1 = ((bf16[16,256,256]{2,1,0:T(8,128)(2,1)}), bf16[16,256,256]{2,1,0:T(8,128)(2,1)S(1)}, u32[]{:S(2)}, u32[]{:S(2)}) async-start(bf16[16,256,256]{2,1,0:T(8,128)(2,1)} %shard_map.64), calls=%async_computation.1 | async-start | bytes 4194304 | tf_op jit(solution)/shard_map/all_to_all | solution.py:188
  88.5 45.5 %all-to-all-start.2 = ((bf16[16,256,384]{2,1,0:T(8,128)(2,1)}), bf16[16,256,384]{2,1,0:T(8,128)(2,1)}, u32[]{:S(2)}, u32[]{:S(2)}) async-start(bf16[16,256,384]{2,1,0:T(8,128)(2,1)} %shard_map.65), calls=%async_computation.2 | async-start | bytes 6291456 | tf_op jit(solution)/shard_map/all_to_all | solution.py:188
  134.0 49.5 %all-to-all-start.3 = ((bf16[16,256,384]{2,1,0:T(8,128)(2,1)}), bf16[16,256,384]{2,1,0:T(8,128)(2,1)}, u32[]{:S(2)}, u32[]{:S(2)}) async-start(bf16[16,256,384]{2,1,0:T(8,128)(2,1)} %shard_map.66), calls=%async_computation.3 | async-start | bytes 6291456 | tf_op jit(solution)/shard_map/all_to_all | solution.py:188

commit v10 on v9

v10 whole, which is shorter than its diff:
```python
import functools
import math

import jax
import jax.numpy as jnp
from jax import lax
from jax.experimental import pallas as pl
from jax.experimental.pallas import tpu as pltpu
from jax.sharding import PartitionSpec as P

THETA = 500000.0


def passed_along(shard, axis, by):
    length = lax.axis_size(axis)
    pairs = [(i, i + by) for i in range(length) if 0 <= i + by < length]
    return lax.ppermute(shard, axis, pairs)


def doc_tables(lengths, positions):
    doc_ends = jnp.cumsum(lengths, dtype=jnp.int32)
    before = positions[:, None] >= doc_ends[None, :]
    doc_index = jnp.sum(before.astype(jnp.int32), axis=1, dtype=jnp.int32)
    doc_start = jnp.sum(jnp.where(before, lengths[None, :], 0), axis=1, dtype=jnp.int32)
    return (doc_index, positions - doc_start)


def inverse_freqs(factors, head_dim):
    half_dim = head_dim // 2
    exponent = jnp.arange(half_dim, dtype=jnp.float32) * (2.0 / head_dim)
    return 1.0 / (factors * jnp.power(jnp.float32(THETA), exponent))


def rotation_rows(offsets, inverse, distinct):
    angles = jnp.arange(distinct, dtype=jnp.int32).astype(jnp.float32)[:, None] * inverse[None, :]
    cosine = jnp.cos(angles)
    sine = jnp.sin(angles)
    table = jnp.concatenate([cosine, cosine, -sine, sine], axis=1)
    return jnp.take(table, jnp.clip(offsets, 0, distinct - 1), axis=0, mode="clip")


def rotate(vectors, offsets, inverse):
    half_dim = vectors.shape[-1] // 2
    angles = offsets.astype(jnp.float32)[:, None] * inverse[None, :]
    cosine = jnp.cos(angles)
    sine_part = jnp.sin(angles)
    first_half = vectors[..., :half_dim]
    second_half = vectors[..., half_dim:]
    return jnp.concatenate(
        [
            first_half * cosine - second_half * sine_part,
            second_half * cosine + first_half * sine_part,
        ],
        axis=-1,
    )


def attend_kernel(
    dest_ref, *refs, heads, head_dim, block_rows, span, scale, first_block, key_base, aliased
):
    q_refs = refs[:heads]
    cos_ref, sin_ref, k_ref, v_ref, lo_ref = refs[heads : heads + 5]
    o_ref = refs[-1]
    r = pl.program_id(0) + first_block
    start = pl.multiple_of(r * block_rows - key_base, block_rows)
    k = k_ref[pl.ds(start, span), :]
    v = v_ref[pl.ds(start, span), :]
    tail = span - block_rows
    lo = lo_ref[0]
    hi = lax.broadcasted_iota(jnp.int32, (block_rows, 1), 0) + tail
    col = lax.broadcasted_iota(jnp.int32, (block_rows, span), 1)
    visible = (col >= lo) & (col <= hi)
    cos = cos_ref[...]
    sin = sin_ref[...]
    for h in range(heads):
        cols = slice(h * head_dim, (h + 1) * head_dim)
        qh = q_refs[h][...].astype(jnp.float32)
        qr = (qh * cos + pltpu.roll(qh, head_dim // 2, 1) * sin).astype(jnp.bfloat16)
        s = lax.dot_general(
            qr, k, (((1,), (1,)), ((), ())), preferred_element_type=jnp.float32
        ) * scale
        s = jnp.where(visible, s, -1e30)
        m = jnp.max(s, axis=1, keepdims=True)
        p = jnp.exp(s - m)
        l = jnp.sum(p, axis=1, keepdims=True)
        o = jnp.dot(p.astype(jnp.bfloat16), v, preferred_element_type=jnp.float32)
        o_ref[0, :, cols] = (o / l).astype(o_ref.dtype)


def attend(
    dest, q, table, k_arr, v_arr, lo, n_dest, head_dim, first, heads,
    first_block, blocks, key_base, prev=None,
):
    rows, all_width = q.shape
    width = heads * head_dim
    per_dev, block_rows, _ = lo.shape
    tail_blocks = (table.shape[0] - rows) // block_rows
    span = (tail_blocks + 1) * block_rows
    k_rows = k_arr.shape[0]
    kernel = functools.partial(
        attend_kernel,
        heads=heads,
        head_dim=head_dim,
        block_rows=block_rows,
        span=span,
        scale=1.0 / math.sqrt(head_dim),
        first_block=first_block,
        key_base=key_base,
        aliased=prev is not None,
    )
    flops = 4 * blocks * heads * block_rows * span * head_dim
    in_specs = [
        pl.BlockSpec((block_rows, head_dim), functools.partial(
            lambda i, dst, col: (i + first_block, col), col=first + head))
        for head in range(heads)
    ] + [
        pl.BlockSpec((block_rows, head_dim), lambda i, dst: (i + first_block + tail_blocks, 0)),
        pl.BlockSpec((block_rows, head_dim), lambda i, dst: (i + first_block + tail_blocks, 1)),
        pl.BlockSpec((k_rows, head_dim), lambda i, dst: (0, 0)),
        pl.BlockSpec((k_rows, head_dim), lambda i, dst: (0, 0)),
        pl.BlockSpec((1, block_rows, 1), lambda i, dst: (i + first_block, 0, 0)),
    ]
    args = [dest] + [q] * heads + [table, table, k_arr, v_arr, lo]
    aliases = {}
    if prev is not None:
        in_specs.append(pl.BlockSpec(memory_space=pl.ANY))
        args.append(prev)
        aliases = {len(args) - 1: 0}
    grid_spec = pltpu.PrefetchScalarGridSpec(
        num_scalar_prefetch=1,
        grid=(blocks,),
        in_specs=in_specs,
        out_specs=pl.BlockSpec((1, block_rows, width), lambda i, dst: (dst[i + first_block], 0, 0)),
    )
    return pl.pallas_call(
        kernel,
        grid_spec=grid_spec,
        out_shape=jax.ShapeDtypeStruct((n_dest, block_rows, width), q.dtype),
        input_output_aliases=aliases,
        cost_estimate=pl.CostEstimate(
            flops=flops,
            transcendentals=blocks * heads * block_rows * span,
            bytes_accessed=2 * blocks * block_rows * width * 2 + 2 * k_rows * head_dim * 2,
        ),
    )(*args)


def local(queries, keys, values, rope_factors, doc_lengths, owner_map):
    ctx_size = lax.axis_size("ctx")
    ctx_index = lax.axis_index("ctx")
    tp_size = lax.axis_size("tp")
    row_count = queries.shape[0]
    per_dev = owner_map.shape[1]
    block_rows = row_count // per_dev
    tail_rows = row_count // 4
    span = tail_rows + block_rows
    head_dim = 2 * rope_factors.shape[0]
    kv_heads = keys.shape[1] // head_dim
    kv_local = kv_heads // tp_size
    shard_rows = keys.shape[0]

    kv_width = kv_local * head_dim
    kv = jnp.concatenate(
        [
            keys.reshape(shard_rows, tp_size, kv_width).transpose(1, 0, 2),
            values.reshape(shard_rows, tp_size, kv_width).transpose(1, 0, 2),
        ],
        axis=2,
    )
    kv = lax.all_to_all(kv, "tp", split_axis=0, concat_axis=0, tiled=True)
    kv = kv.reshape(row_count, 2 * kv_width)
    k_own_raw = kv[:, :kv_width]
    v_own = kv[:, kv_width:]
    kv_tail = passed_along(kv[row_count - tail_rows :], "ctx", 1)

    ext_rows = row_count + tail_rows
    pos_ext = ctx_index * row_count - tail_rows + jnp.arange(ext_rows, dtype=jnp.int32)
    unused_doc, off_ext = doc_tables(doc_lengths, pos_ext)
    inverse = inverse_freqs(rope_factors, head_dim)
    table = rotation_rows(off_ext, inverse, tail_rows)
    cos_ext = table[:, :head_dim]
    sin_ext = table[:, head_dim:]

    def rotated(raw, cosine, sine):
        raw = raw.astype(jnp.float32)
        return (raw * cosine + jnp.roll(raw, head_dim // 2, axis=1) * sine).astype(jnp.bfloat16)

    k_own = rotated(k_own_raw, cos_ext[tail_rows:], sin_ext[tail_rows:])
    k_tail = rotated(kv_tail[:, :kv_width], cos_ext[:tail_rows], sin_ext[:tail_rows])
    k_ext = jnp.concatenate([k_tail, k_own], axis=0)
    v_ext = jnp.concatenate([kv_tail[:, kv_width:], v_own], axis=0)

    lo = (tail_rows + jnp.arange(row_count, dtype=jnp.int32) % block_rows - off_ext[tail_rows:])
    lo = lo.reshape(per_dev, block_rows, 1)

    devices = jnp.arange(ctx_size, dtype=jnp.int32)
    owner_row = lax.dynamic_index_in_dim(owner_map, ctx_index, 0, keepdims=False)

    q_heads = queries.shape[1] // head_dim
    sizes = [2, 3, 3] if q_heads == 8 else [q_heads]
    tail_blocks = tail_rows // block_rows
    arrived = []
    first = 0
    for number, heads in enumerate(sizes):
        if number == 0:
            send = attend(
                owner_row, queries, table, k_own, v_own, lo, ctx_size, head_dim, first, heads,
                tail_blocks, per_dev - tail_blocks, tail_rows,
            )
            send = attend(
                owner_row, queries, table, k_ext, v_ext, lo, ctx_size, head_dim, first, heads,
                0, tail_blocks, 0, prev=send,
            )
        else:
            send = attend(
                owner_row, queries, table, k_ext, v_ext, lo, ctx_size, head_dim, first, heads,
                0, per_dev, 0,
            )
        arrived.append(lax.all_to_all(send, "ctx", split_axis=0, concat_axis=0, tiled=True))
        first += heads

    sources_match = owner_map == ctx_index
    my_sources = jnp.sum(
        jnp.where(sources_match, devices[:, None], 0), axis=0, dtype=jnp.int32
    )
    finished = jnp.zeros((per_dev, block_rows, queries.shape[1]), queries.dtype)
    first = 0
    for heads, a in zip(sizes, arrived):
        finished = lax.dynamic_update_slice(
            finished, jnp.take(a, my_sources, axis=0, mode="clip"), (0, 0, first * head_dim)
        )
        first += heads
    return finished.reshape(row_count, queries.shape[1])


def solution(mesh):
    in_specs = (P("ctx", "tp"), P(("ctx", "tp"), None), P(("ctx", "tp"), None), P(), P(), P())
    out_specs = P("ctx", "tp")
    return jax.shard_map(local, mesh=mesh, in_specs=in_specs, out_specs=out_specs, check_vma=False)
```

time: 190 us -> 188 us (0.989)
  local copies, waits for them, and re-layouts: 30.1 us -> 26 us
  Pallas kernels: 45.4 us -> 48.6 us
  other arithmetic: 6.19 us -> 9.03 us
  waiting for transfers between devices: 71.5 us -> 69.1 us
    pallas_call x3 -> x4, Pallas kernels: 45.4 us -> 48.6 us  [attend(): pl.pallas_call(kernel, grid_spec=grid_spec, out_shape=jax.ShapeDtypeStruc...]
    slice x2, local copies, waits for them, and re-layouts: 3.42 us -> 0.46 us  [rotated(): jnp.roll(raw, head_dim // 2, axis=1) * sine]
    all_to_all x1, waiting for transfers between devices: 5.91 us -> 3.64 us  [local(): kv = lax.all_to_all(kv, 'tp', split_axis=0, concat_axis=0, tiled=True)]
  transfers between devices with their start and end apart: 5 -> 5, of which waited for: 4 -> 4; matrix products, arithmetic and copies ran while one was open for 13% -> 12% of each run, Pallas kernels for 17% -> 23%
where the time goes in v10:
time: 188 us; the launch traced here: 185 us
  waiting for transfers between devices  69.1 us (37%)
  Pallas kernels  48.6 us (26%)
  starting transfers between devices  32.6 us (17%)
  local copies, waits for them, and re-layouts  26 us (14%)
  other arithmetic  9.03 us (5%)
    all_to_all x3, waiting for transfers between devices, local(): lax.all_to_all(send, 'ctx', split_axis=0, concat_axis=0, tiled=True)  65.4 us
    pallas_call x4, Pallas kernels, attend(): pl.pallas_call(kernel, grid_spec=grid_spec, out_shape=jax.ShapeDtypeStruc...  48.6 us
    all_to_all x3, starting transfers between devices, local(): lax.all_to_all(send, 'ctx', split_axis=0, concat_axis=0, tiled=True)  20.3 us
    gather x3, local copies, waits for them, and re-layouts, local(): jnp.take(a, my_sources, axis=0, mode='clip')  7.12 us
    gather x1, local copies, waits for them, and re-layouts, rotation_rows(): jnp.take(table, jnp.clip(offsets, 0, distinct - 1), axis=0, mode='clip')  7.07 us
    dynamic_update_slice x3, local copies, waits for them, and re-layouts, local(): lax.dynamic_update_slice(finished, jnp.take(a, my_sources, axis=0, mode='...  6.43 us
    all_to_all x1, starting transfers between devices, local(): kv = lax.all_to_all(kv, 'tp', split_axis=0, concat_axis=0, tiled=True)  6.19 us
    ppermute x1, starting transfers between devices, passed_along(): return lax.ppermute(shard, axis, pairs)  6.02 us
  transfers between devices with their start and end apart: 5, of which 4 were waited for; matrix products, arithmetic and copies ran while one was open for 12% of the time, Pallas kernels for 23%

profile of v10, /device:TPU:1, one launch (start us, length us, event | category | flops | bytes accessed | tf_op | source)
XLA Modules:
  0.0 185.4 jit_solution(1169195471394262450)
XLA Ops:
  0.0 1.0 copy-done
  1.0 1.3 bitcast_bitcast_fusion
  2.4 1.1 pad_maximum_fusion
  3.5 6.2 %all-to-all-start = ((bf16[8,256,256]{2,1,0:T(8,128)(2,1)}), bf16[8,256,256]{2,1,0:T(8,128)(2,1)S(1)}, u32[]{:S(2)}, u32[]{:S(2)}) async-start(bf16[8,256,256]{2,1,0:T(8,128)(2,1)} %pad_maximum_fusion), calls=%async_computation | async-start | bytes 2097152 | tf_op jit(solution)/shard_map/all_to_all | solution.py:170
  10.1 0.5 multiply_cosine_fusion
  10.9 1.6 select_reduce_fusion
  12.6 1.4 copy.30.refs_6_.refs_7_
  14.0 7.1 %gather_fusion = f32[2560,256]{1,0:T(8,128)} fusion(f32[512,256]{1,0:T(8,128)S(1)} %copy.26, s32[3072]{0:T(1024)S(1)} %pad_clamp_fusion), kind=kCustom, calls=%fused_computation | custom fusion | bytes 5253120 | tf_op jit(solution)/shard_map/jit(_take)/gather | solution.py:39
  21.1 0.8 dynamic-slice_reduce_fusion.dest_ref
  21.9 3.6 %all-to-all-done = bf16[8,256,256]{2,1,0:T(8,128)(2,1)S(1)} async-done(((bf16[8,256,256]{2,1,0:T(8,128)(2,1)}), bf16[8,256,256]{2,1,0:T(8,128)(2,1)S(1)}, u32[]{:S(2)}, u32[]{:S(2)}) %all-to-all-start) | async-done | bytes 1048608 | tf_op jit(solution)/shard_map/all_to_all | solution.py:170
  25.5 0.9 fusion.10
  26.8 6.0 %collective-permute-start = (bf16[512,256]{1,0:T(8,128)(2,1)S(1)}, bf16[512,256]{1,0:T(8,128)(2,1)S(1)}, u32[]{:S(2)}, u32[]{:S(2)}) collective-permute-start(bf16[512,256]{1,0:T(8,128)(2,1)S(1)} %bitcast.22), channel_id=1, source_target_pairs={{0,8},{8,16},{16,24},{24,32},{32,40},{40,48},{48,56},{56,64},{64,7... | collective-permute-start | bytes 786440 | tf_op jit(solution)/shard_map/ppermute | solution.py:17
  32.8 1.2 fusion.1.refs_4_
  34.1 10.4 %shard_map.64.refs_7_ = bf16[16,256,256]{2,1,0:T(8,128)(2,1)} custom-call(s32[8]{0:T(128)} %dynamic-slice_reduce_fusion.dest_ref, bf16[2048,1024]{1,0:T(8,128)(2,1)} %refs_2_.3, bf16[2048,1024]{1,0:T(8,128)(2,1)} %refs_2_.3, f32[2560,256]{1,0:T(8,128)} %gather_fusion, f32[2560,256]{1,0:T(8,128)} %gather_fusion, bf16[2048,128]{1,0:T(8,128)(2,1)} %fusion.1.refs_4_, ...), custom_call_target="tpu_custom_call" | custom-call | flops 1207959552 | bytes 2621440 | tf_op jit(solution)/shard_map/pallas_call | solution.py:135
  44.7 1.3 fusion.3
  46.0 0.9 pad_maximum_fusion.1.refs_4_.refs_5_
  46.9 0.9 pad_maximum_fusion.2.refs_5_.refs_6_
  47.8 5.4 %shard_map.65 = bf16[16,256,256]{2,1,0:T(8,128)(2,1)} custom-call(s32[8]{0:T(128)} %dynamic-slice_reduce_fusion.dest_ref, bf16[2048,1024]{1,0:T(8,128)(2,1)} %refs_2_.3, bf16[2048,1024]{1,0:T(8,128)(2,1)} %refs_2_.3, f32[2560,256]{1,0:T(8,128)} %gather_fusion, f32[2560,256]{1,0:T(8,128)} %gather_fusion, ...), custom_call_target="tpu_custom_call", output_to_operand_aliasing={{}: (8, {})} | custom-call | flops 402653184 | bytes 1835008 | tf_op jit(solution)/shard_map/pallas_call | solution.py:135
  53.2 4.7 %all-to-all-start.1 = ((bf16[16,256,256]{2,1,0:T(8,128)(2,1)}), bf16[16,256,256]{2,1,0:T(8,128)(2,1)S(1)}, u32[]{:S(2)}, u32[]{:S(2)}) async-start(bf16[16,256,256]{2,1,0:T(8,128)(2,1)} %shard_map.65), calls=%async_computation.1 | async-start | bytes 4194304 | tf_op jit(solution)/shard_map/all_to_all | solution.py:219
  57.9 16.4 %shard_map.66 = bf16[16,256,384]{2,1,0:T(8,128)(2,1)} custom-call(s32[8]{0:T(128)} %dynamic-slice_reduce_fusion.dest_ref, bf16[2048,1024]{1,0:T(8,128)(2,1)} %refs_2_.3, bf16[2048,1024]{1,0:T(8,128)(2,1)} %refs_2_.3, bf16[2048,1024]{1,0:T(8,128)(2,1)} %refs_2_.3, f32[2560,256]{1,0:T(8,128)} %gather_fusion, f32[2560,256]{1,0:T(8,128)} %gather_fusion, ...), custom_call_target="tpu_custom_call" | custom-call | flops 2415919104 | bytes 4456448 | tf_op jit(solution)/shard_map/pallas_call | solution.py:135
  74.3 11.9 %all-to-all-done.1 = bf16[16,256,256]{2,1,0:T(8,128)(2,1)S(1)} async-done(((bf16[16,256,256]{2,1,0:T(8,128)(2,1)}), bf16[16,256,256]{2,1,0:T(8,128)(2,1)S(1)}, u32[]{:S(2)}, u32[]{:S(2)}) %all-to-all-start.1) | async-done | bytes 2097184 | tf_op jit(solution)/shard_map/all_to_all | solution.py:219
  86.2 5.8 %all-to-all-start.2 = ((bf16[16,256,384]{2,1,0:T(8,128)(2,1)}), bf16[16,256,384]{2,1,0:T(8,128)(2,1)}, u32[]{:S(2)}, u32[]{:S(2)}) async-start(bf16[16,256,384]{2,1,0:T(8,128)(2,1)} %shard_map.66), calls=%async_computation.2 | async-start | bytes 6291456 | tf_op jit(solution)/shard_map/all_to_all | solution.py:219
  92.1 16.4 %shard_map.67 = bf16[16,256,384]{2,1,0:T(8,128)(2,1)} custom-call(s32[8]{0:T(128)} %dynamic-slice_reduce_fusion.dest_ref, bf16[2048,1024]{1,0:T(8,128)(2,1)} %refs_2_.3, bf16[2048,1024]{1,0:T(8,128)(2,1)} %refs_2_.3, bf16[2048,1024]{1,0:T(8,128)(2,1)} %refs_2_.3, f32[2560,256]{1,0:T(8,128)} %gather_fusion, f32[2560,256]{1,0:T(8,128)} %gather_fusion, ...), custom_call_target="tpu_custom_call" | custom-call | flops 2415919104 | bytes 4456448 | tf_op jit(solution)/shard_map/pallas_call | solution.py:135
  108.4 23.3 %all-to-all-done.2 = bf16[16,256,384]{2,1,0:T(8,128)(2,1)} async-done(((bf16[16,256,384]{2,1,0:T(8,128)(2,1)}), bf16[16,256,384]{2,1,0:T(8,128)(2,1)}, u32[]{:S(2)}, u32[]{:S(2)}) %all-to-all-start.2) | async-done | bytes 3145760 | tf_op jit(solution)/shard_map/all_to_all | solution.py:219
  131.8 9.8 %all-to-all-start.3 = ((bf16[16,256,384]{2,1,0:T(8,128)(2,1)}), bf16[16,256,384]{2,1,0:T(8,128)(2,1)}, u32[]{:S(2)}, u32[]{:S(2)}) async-start(bf16[16,256,384]{2,1,0:T(8,128)(2,1)} %shard_map.67), calls=%async_computation.3 | async-start | bytes 6291456 | tf_op jit(solution)/shard_map/all_to_all | solution.py:219
  141.7 1.6 gather_fusion.1
  143.3 3.8 %dynamic_update_slice.9 = bf16[8,256,1024]{2,1,0:T(8,128)(2,1)} pad(bf16[8,256,256]{2,1,0:T(8,128)(2,1)} %gather_fusion.1, bf16[]{:T(256)} %constant.49.clone.1), padding=0_0x0_0x0_768 | pad | bytes 5242882 | tf_op jit(solution)/shard_map/dynamic_update_slice | solution.py:229
  147.0 2.8 %gather_fusion.2 = bf16[8,256,384]{2,1,0:T(8,128)(2,1)S(1)} fusion(bf16[16,256,384]{2,1,0:T(8,128)(2,1)} %all-to-all-done.2, s32[1024]{0:T(1024)S(1)} %pad_clamp_fusion.1), kind=kCustom, calls=%fused_computation.2 | custom fusion | bytes 3145760 | tf_op jit(solution)/shard_map/jit(_take)/gather | solution.py:230
  149.8 1.3 constant_dynamic-update-slice_fusion
  151.2 30.1 %all-to-all-done.3 = bf16[16,256,384]{2,1,0:T(8,128)(2,1)} async-done(((bf16[16,256,384]{2,1,0:T(8,128)(2,1)}), bf16[16,256,384]{2,1,0:T(8,128)(2,1)}, u32[]{:S(2)}, u32[]{:S(2)}) %all-to-all-start.3) | async-done | bytes 3145760 | tf_op jit(solution)/shard_map/all_to_all | solution.py:219
  181.3 2.8 %gather_fusion.3 = bf16[8,256,384]{2,1,0:T(8,128)(2,1)S(1)} fusion(bf16[16,256,384]{2,1,0:T(8,128)(2,1)} %all-to-all-done.3, s32[1024]{0:T(1024)S(1)} %pad_clamp_fusion.1), kind=kCustom, calls=%fused_computation.3 | custom fusion | bytes 3145760 | tf_op jit(solution)/shard_map/jit(_take)/gather | solution.py:230
  184.1 1.3 constant_dynamic-update-slice_fusion.1
  (32 shorter events, 1.4 us)
Async XLA Ops:
  0.0 1.0 copy-start
  2.3 7.3 %copy-start.5 = (s32[128]{0:T(128)S(1)}, s32[128]{0:T(128)}, u32[]{:S(2)}) copy-start(s32[128]{0:T(128)} %param.10) | copy-start | bytes 1540
  2.4 7.7 %copy-start.6 = (f32[64]{0:T(128)S(1)}, f32[64]{0:T(128)}, u32[]{:S(2)}) copy-start(f32[64]{0:T(128)} %param.9) | copy-start | bytes 772
  3.5 22.1 %all-to-all-start = ((bf16[8,256,256]{2,1,0:T(8,128)(2,1)}), bf16[8,256,256]{2,1,0:T(8,128)(2,1)S(1)}, u32[]{:S(2)}, u32[]{:S(2)}) async-start(bf16[8,256,256]{2,1,0:T(8,128)(2,1)} %pad_maximum_fusion), calls=%async_computation | async-start | bytes 2097152 | tf_op jit(solution)/shard_map/all_to_all | solution.py:170
  14.0 7.1 %copy-start.4 = (s32[16,8]{0,1:T(8,128)S(1)}, s32[16,8]{0,1:T(8,128)}, u32[]{:S(2)}) copy-start(s32[16,8]{0,1:T(8,128)} %param.11) | copy-start | bytes 1540
  26.4 6.4 %copy-start.1 = (f32[2560,256]{1,0:T(8,128)S(1)}, f32[2560,256]{1,0:T(8,128)}, u32[]{:S(2)}) copy-start(f32[2560,256]{1,0:T(8,128)} %gather_fusion) | copy-start | bytes 7864324
  26.8 17.7 %collective-permute-start = (bf16[512,256]{1,0:T(8,128)(2,1)S(1)}, bf16[512,256]{1,0:T(8,128)(2,1)S(1)}, u32[]{:S(2)}, u32[]{:S(2)}) collective-permute-start(bf16[512,256]{1,0:T(8,128)(2,1)S(1)} %bitcast.22), channel_id=1, source_target_pairs={{0,8},{8,16},{16,24},{24,32},{32,40},{40,48},{48,56},{56,64},{64,7... | collective-permute-start | bytes 786440 | tf_op jit(solution)/shard_map/ppermute | solution.py:17
  44.5 1.5 copy-start.3
  44.5 2.4 %copy-start.2 = (bf16[2048,128]{1,0:T(8,128)(2,1)S(1)}, bf16[2048,128]{1,0:T(8,128)(2,1)}, u32[]{:S(2)}) copy-start(bf16[2048,128]{1,0:T(8,128)(2,1)} %get-tuple-element.5.refs_5_) | copy-start | bytes 1572868
  53.2 33.0 %all-to-all-start.1 = ((bf16[16,256,256]{2,1,0:T(8,128)(2,1)}), bf16[16,256,256]{2,1,0:T(8,128)(2,1)S(1)}, u32[]{:S(2)}, u32[]{:S(2)}) async-start(bf16[16,256,256]{2,1,0:T(8,128)(2,1)} %shard_map.65), calls=%async_computation.1 | async-start | bytes 4194304 | tf_op jit(solution)/shard_map/all_to_all | solution.py:219
  86.2 45.5 %all-to-all-start.2 = ((bf16[16,256,384]{2,1,0:T(8,128)(2,1)}), bf16[16,256,384]{2,1,0:T(8,128)(2,1)}, u32[]{:S(2)}, u32[]{:S(2)}) async-start(bf16[16,256,384]{2,1,0:T(8,128)(2,1)} %shard_map.66), calls=%async_computation.2 | async-start | bytes 6291456 | tf_op jit(solution)/shard_map/all_to_all | solution.py:219
  131.8 49.5 %all-to-all-start.3 = ((bf16[16,256,384]{2,1,0:T(8,128)(2,1)}), bf16[16,256,384]{2,1,0:T(8,128)(2,1)}, u32[]{:S(2)}, u32[]{:S(2)}) async-start(bf16[16,256,384]{2,1,0:T(8,128)(2,1)} %shard_map.67), calls=%async_computation.3 | async-start | bytes 6291456 | tf_op jit(solution)/shard_map/all_to_all | solution.py:219

commit v11 on v10

--- a/solution.py
+++ b/solution.py
@@ -207,9 +207,10 @@
                 owner_row, queries, table, k_own, v_own, lo, ctx_size, head_dim, first, heads,
                 tail_blocks, per_dev - tail_blocks, tail_rows,
             )
+            near = tail_rows + tail_rows
             send = attend(
-                owner_row, queries, table, k_ext, v_ext, lo, ctx_size, head_dim, first, heads,
-                0, tail_blocks, 0, prev=send,
+                owner_row, queries, table, k_ext[:near], v_ext[:near], lo, ctx_size, head_dim,
+                first, heads, 0, tail_blocks, 0, prev=send,
             )
         else:
             send = attend(

time: 188 us -> 187 us (level)
  transfers between devices with their start and end apart: 5 -> 5, of which waited for: 4 -> 4; matrix products, arithmetic and copies ran while one was open for 12% -> 13% of each run, Pallas kernels for 23% -> 23%
where the time goes in v11:
time: 187 us; the launch traced here: 185 us
  waiting for transfers between devices  68 us (36%)
  Pallas kernels  48.3 us (26%)
  starting transfers between devices  32.5 us (17%)
  local copies, waits for them, and re-layouts  25.3 us (14%)
  other arithmetic  10.5 us (6%)
    all_to_all x3, waiting for transfers between devices, local(): lax.all_to_all(send, 'ctx', split_axis=0, concat_axis=0, tiled=True)  64.3 us
    pallas_call x4, Pallas kernels, attend(): pl.pallas_call(kernel, grid_spec=grid_spec, out_shape=jax.ShapeDtypeStruc...  48.3 us
    all_to_all x3, starting transfers between devices, local(): lax.all_to_all(send, 'ctx', split_axis=0, concat_axis=0, tiled=True)  20.3 us
    gather x3, local copies, waits for them, and re-layouts, local(): jnp.take(a, my_sources, axis=0, mode='clip')  7.76 us
    gather x1, local copies, waits for them, and re-layouts, rotation_rows(): jnp.take(table, jnp.clip(offsets, 0, distinct - 1), axis=0, mode='clip')  7.01 us
    all_to_all x1, starting transfers between devices, local(): kv = lax.all_to_all(kv, 'tp', split_axis=0, concat_axis=0, tiled=True)  6.19 us
    ppermute x1, starting transfers between devices, passed_along(): return lax.ppermute(shard, axis, pairs)  6.02 us
    dynamic_update_slice x3, local copies, waits for them, and re-layouts, local(): lax.dynamic_update_slice(finished, jnp.take(a, my_sources, axis=0, mode='...  5.2 us
  transfers between devices with their start and end apart: 5, of which 4 were waited for; matrix products, arithmetic and copies ran while one was open for 13% of the time, Pallas kernels for 23%

profile of v11, /device:TPU:1, one launch (start us, length us, event | category | flops | bytes accessed | tf_op | source)
XLA Modules:
  0.0 184.9 jit_solution(2790103491595418799)
XLA Ops:
  0.0 1.0 copy-done
  1.0 1.3 bitcast_bitcast_fusion
  2.4 1.1 pad_maximum_fusion
  3.5 6.2 %all-to-all-start = ((bf16[8,256,256]{2,1,0:T(8,128)(2,1)}), bf16[8,256,256]{2,1,0:T(8,128)(2,1)S(1)}, u32[]{:S(2)}, u32[]{:S(2)}) async-start(bf16[8,256,256]{2,1,0:T(8,128)(2,1)} %pad_maximum_fusion), calls=%async_computation | async-start | bytes 2097152 | tf_op jit(solution)/shard_map/all_to_all | solution.py:170
  10.9 1.6 select_reduce_fusion
  12.6 1.4 copy.30.refs_6_.refs_7_
  14.0 7.0 %gather_fusion = f32[2560,256]{1,0:T(8,128)} fusion(f32[512,256]{1,0:T(8,128)S(1)} %copy.26, s32[3072]{0:T(1024)S(1)} %pad_clamp_fusion), kind=kCustom, calls=%fused_computation | custom fusion | bytes 5253120 | tf_op jit(solution)/shard_map/jit(_take)/gather | solution.py:39
  21.0 0.8 dynamic-slice_reduce_fusion.dest_ref
  21.8 3.7 %all-to-all-done = bf16[8,256,256]{2,1,0:T(8,128)(2,1)S(1)} async-done(((bf16[8,256,256]{2,1,0:T(8,128)(2,1)}), bf16[8,256,256]{2,1,0:T(8,128)(2,1)S(1)}, u32[]{:S(2)}, u32[]{:S(2)}) %all-to-all-start) | async-done | bytes 1048608 | tf_op jit(solution)/shard_map/all_to_all | solution.py:170
  25.5 0.9 fusion.12
  26.8 6.0 %collective-permute-start = (bf16[512,256]{1,0:T(8,128)(2,1)S(1)}, bf16[512,256]{1,0:T(8,128)(2,1)S(1)}, u32[]{:S(2)}, u32[]{:S(2)}) collective-permute-start(bf16[512,256]{1,0:T(8,128)(2,1)S(1)} %bitcast.22), channel_id=1, source_target_pairs={{0,8},{8,16},{16,24},{24,32},{32,40},{40,48},{48,56},{56,64},{64,7... | collective-permute-start | bytes 786440 | tf_op jit(solution)/shard_map/ppermute | solution.py:17
  32.8 1.2 fusion.1.refs_4_
  34.1 10.4 %shard_map.64.refs_7_ = bf16[16,256,256]{2,1,0:T(8,128)(2,1)} custom-call(s32[8]{0:T(128)} %dynamic-slice_reduce_fusion.dest_ref, bf16[2048,1024]{1,0:T(8,128)(2,1)} %refs_2_.3, bf16[2048,1024]{1,0:T(8,128)(2,1)} %refs_2_.3, f32[2560,256]{1,0:T(8,128)} %gather_fusion, f32[2560,256]{1,0:T(8,128)} %gather_fusion, bf16[2048,128]{1,0:T(8,128)(2,1)} %fusion.1.refs_4_, ...), custom_call_target="tpu_custom_call" | custom-call | flops 1207959552 | bytes 2621440 | tf_op jit(solution)/shard_map/pallas_call | solution.py:135
  44.7 1.3 fusion.5
  46.7 0.7 fusion.2.refs_5_
  47.4 5.2 %shard_map.65 = bf16[16,256,256]{2,1,0:T(8,128)(2,1)} custom-call(s32[8]{0:T(128)} %dynamic-slice_reduce_fusion.dest_ref, bf16[2048,1024]{1,0:T(8,128)(2,1)} %refs_2_.3, bf16[2048,1024]{1,0:T(8,128)(2,1)} %refs_2_.3, f32[2560,256]{1,0:T(8,128)} %gather_fusion, f32[2560,256]{1,0:T(8,128)} %gather_fusion, ...), custom_call_target="tpu_custom_call", output_to_operand_aliasing={{}: (8, {})} | custom-call | flops 402653184 | bytes 1048576 | tf_op jit(solution)/shard_map/pallas_call | solution.py:135
  52.6 4.7 %all-to-all-start.1 = ((bf16[16,256,256]{2,1,0:T(8,128)(2,1)}), bf16[16,256,256]{2,1,0:T(8,128)(2,1)}, u32[]{:S(2)}, u32[]{:S(2)}) async-start(bf16[16,256,256]{2,1,0:T(8,128)(2,1)} %shard_map.65), calls=%async_computation.1 | async-start | bytes 4194304 | tf_op jit(solution)/shard_map/all_to_all | solution.py:220
  57.3 0.9 pad_maximum_fusion.1.refs_5_
  58.2 0.9 pad_maximum_fusion.2.refs_6_
  59.1 16.4 %shard_map.66 = bf16[16,256,384]{2,1,0:T(8,128)(2,1)} custom-call(s32[8]{0:T(128)} %dynamic-slice_reduce_fusion.dest_ref, bf16[2048,1024]{1,0:T(8,128)(2,1)} %refs_2_.3, bf16[2048,1024]{1,0:T(8,128)(2,1)} %refs_2_.3, bf16[2048,1024]{1,0:T(8,128)(2,1)} %refs_2_.3, f32[2560,256]{1,0:T(8,128)} %gather_fusion, f32[2560,256]{1,0:T(8,128)} %gather_fusion, ...), custom_call_target="tpu_custom_call" | custom-call | flops 2415919104 | bytes 4456448 | tf_op jit(solution)/shard_map/pallas_call | solution.py:135
  75.5 10.2 %all-to-all-done.1 = bf16[16,256,256]{2,1,0:T(8,128)(2,1)} async-done(((bf16[16,256,256]{2,1,0:T(8,128)(2,1)}), bf16[16,256,256]{2,1,0:T(8,128)(2,1)}, u32[]{:S(2)}, u32[]{:S(2)}) %all-to-all-start.1) | async-done | bytes 2097184 | tf_op jit(solution)/shard_map/all_to_all | solution.py:220
  85.7 5.8 %all-to-all-start.2 = ((bf16[16,256,384]{2,1,0:T(8,128)(2,1)}), bf16[16,256,384]{2,1,0:T(8,128)(2,1)}, u32[]{:S(2)}, u32[]{:S(2)}) async-start(bf16[16,256,384]{2,1,0:T(8,128)(2,1)} %shard_map.66), calls=%async_computation.2 | async-start | bytes 6291456 | tf_op jit(solution)/shard_map/all_to_all | solution.py:220
  91.5 16.4 %shard_map.67 = bf16[16,256,384]{2,1,0:T(8,128)(2,1)} custom-call(s32[8]{0:T(128)} %dynamic-slice_reduce_fusion.dest_ref, bf16[2048,1024]{1,0:T(8,128)(2,1)} %refs_2_.3, bf16[2048,1024]{1,0:T(8,128)(2,1)} %refs_2_.3, bf16[2048,1024]{1,0:T(8,128)(2,1)} %refs_2_.3, f32[2560,256]{1,0:T(8,128)} %gather_fusion, f32[2560,256]{1,0:T(8,128)} %gather_fusion, ...), custom_call_target="tpu_custom_call" | custom-call | flops 2415919104 | bytes 4456448 | tf_op jit(solution)/shard_map/pallas_call | solution.py:135
  107.9 23.3 %all-to-all-done.2 = bf16[16,256,384]{2,1,0:T(8,128)(2,1)} async-done(((bf16[16,256,384]{2,1,0:T(8,128)(2,1)}), bf16[16,256,384]{2,1,0:T(8,128)(2,1)}, u32[]{:S(2)}, u32[]{:S(2)}) %all-to-all-start.2) | async-done | bytes 3145760 | tf_op jit(solution)/shard_map/all_to_all | solution.py:220
  131.2 9.8 %all-to-all-start.3 = ((bf16[16,256,384]{2,1,0:T(8,128)(2,1)}), bf16[16,256,384]{2,1,0:T(8,128)(2,1)}, u32[]{:S(2)}, u32[]{:S(2)}) async-start(bf16[16,256,384]{2,1,0:T(8,128)(2,1)} %shard_map.67), calls=%async_computation.3 | async-start | bytes 6291456 | tf_op jit(solution)/shard_map/all_to_all | solution.py:220
  141.2 2.2 %gather_fusion.1 = bf16[8,256,256]{2,1,0:T(8,128)(2,1)S(1)} fusion(bf16[16,256,256]{2,1,0:T(8,128)(2,1)} %all-to-all-done.1, s32[1024]{0:T(1024)S(1)} %pad_clamp_fusion.1), kind=kCustom, calls=%fused_computation.1 | custom fusion | bytes 2097184 | tf_op jit(solution)/shard_map/jit(_take)/gather | solution.py:231
  143.4 2.6 %dynamic_update_slice.9 = bf16[8,256,1024]{2,1,0:T(8,128)(2,1)} pad(bf16[8,256,256]{2,1,0:T(8,128)(2,1)S(1)} %gather_fusion.1, bf16[]{:T(256)} %constant.49.clone.1), padding=0_0x0_0x0_768 | pad | bytes 5242882 | tf_op jit(solution)/shard_map/dynamic_update_slice | solution.py:230
  146.0 2.8 %gather_fusion.2 = bf16[8,256,384]{2,1,0:T(8,128)(2,1)S(1)} fusion(bf16[16,256,384]{2,1,0:T(8,128)(2,1)} %all-to-all-done.2, s32[1024]{0:T(1024)S(1)} %pad_clamp_fusion.1), kind=kCustom, calls=%fused_computation.2 | custom fusion | bytes 3145760 | tf_op jit(solution)/shard_map/jit(_take)/gather | solution.py:231
  148.7 1.3 constant_dynamic-update-slice_fusion
  150.1 30.7 %all-to-all-done.3 = bf16[16,256,384]{2,1,0:T(8,128)(2,1)} async-done(((bf16[16,256,384]{2,1,0:T(8,128)(2,1)}), bf16[16,256,384]{2,1,0:T(8,128)(2,1)}, u32[]{:S(2)}, u32[]{:S(2)}) %all-to-all-start.3) | async-done | bytes 3145760 | tf_op jit(solution)/shard_map/all_to_all | solution.py:220
  180.8 2.8 %gather_fusion.3 = bf16[8,256,384]{2,1,0:T(8,128)(2,1)S(1)} fusion(bf16[16,256,384]{2,1,0:T(8,128)(2,1)} %all-to-all-done.3, s32[1024]{0:T(1024)S(1)} %pad_clamp_fusion.1), kind=kCustom, calls=%fused_computation.3 | custom fusion | bytes 3145760 | tf_op jit(solution)/shard_map/jit(_take)/gather | solution.py:231
  183.6 1.3 constant_dynamic-update-slice_fusion.1
  (34 shorter events, 2.7 us)
Async XLA Ops:
  0.0 1.0 copy-start
  2.3 7.3 %copy-start.5 = (s32[128]{0:T(128)S(1)}, s32[128]{0:T(128)}, u32[]{:S(2)}) copy-start(s32[128]{0:T(128)} %param.10) | copy-start | bytes 1540
  2.4 7.7 %copy-start.6 = (f32[64]{0:T(128)S(1)}, f32[64]{0:T(128)}, u32[]{:S(2)}) copy-start(f32[64]{0:T(128)} %param.9) | copy-start | bytes 772
  3.5 22.1 %all-to-all-start = ((bf16[8,256,256]{2,1,0:T(8,128)(2,1)}), bf16[8,256,256]{2,1,0:T(8,128)(2,1)S(1)}, u32[]{:S(2)}, u32[]{:S(2)}) async-start(bf16[8,256,256]{2,1,0:T(8,128)(2,1)} %pad_maximum_fusion), calls=%async_computation | async-start | bytes 2097152 | tf_op jit(solution)/shard_map/all_to_all | solution.py:170
  14.0 7.0 %copy-start.4 = (s32[16,8]{0,1:T(8,128)S(1)}, s32[16,8]{0,1:T(8,128)}, u32[]{:S(2)}) copy-start(s32[16,8]{0,1:T(8,128)} %param.11) | copy-start | bytes 1540
  26.4 6.4 %copy-start.1 = (f32[2560,256]{1,0:T(8,128)S(1)}, f32[2560,256]{1,0:T(8,128)}, u32[]{:S(2)}) copy-start(f32[2560,256]{1,0:T(8,128)} %gather_fusion) | copy-start | bytes 7864324
  26.8 17.7 %collective-permute-start = (bf16[512,256]{1,0:T(8,128)(2,1)S(1)}, bf16[512,256]{1,0:T(8,128)(2,1)S(1)}, u32[]{:S(2)}, u32[]{:S(2)}) collective-permute-start(bf16[512,256]{1,0:T(8,128)(2,1)S(1)} %bitcast.22), channel_id=1, source_target_pairs={{0,8},{8,16},{16,24},{24,32},{32,40},{40,48},{48,56},{56,64},{64,7... | collective-permute-start | bytes 786440 | tf_op jit(solution)/shard_map/ppermute | solution.py:17
  44.5 1.5 copy-start.3
  44.5 2.2 %copy-start.2 = (bf16[2048,128]{1,0:T(8,128)(2,1)S(1)}, bf16[2048,128]{1,0:T(8,128)(2,1)}, u32[]{:S(2)}) copy-start(bf16[2048,128]{1,0:T(8,128)(2,1)} %get-tuple-element.5.refs_5_) | copy-start | bytes 1572868
  52.6 33.1 %all-to-all-start.1 = ((bf16[16,256,256]{2,1,0:T(8,128)(2,1)}), bf16[16,256,256]{2,1,0:T(8,128)(2,1)}, u32[]{:S(2)}, u32[]{:S(2)}) async-start(bf16[16,256,256]{2,1,0:T(8,128)(2,1)} %shard_map.65), calls=%async_computation.1 | async-start | bytes 4194304 | tf_op jit(solution)/shard_map/all_to_all | solution.py:220
  85.7 45.5 %all-to-all-start.2 = ((bf16[16,256,384]{2,1,0:T(8,128)(2,1)}), bf16[16,256,384]{2,1,0:T(8,128)(2,1)}, u32[]{:S(2)}, u32[]{:S(2)}) async-start(bf16[16,256,384]{2,1,0:T(8,128)(2,1)} %shard_map.66), calls=%async_computation.2 | async-start | bytes 6291456 | tf_op jit(solution)/shard_map/all_to_all | solution.py:220
  131.2 49.5 %all-to-all-start.3 = ((bf16[16,256,384]{2,1,0:T(8,128)(2,1)}), bf16[16,256,384]{2,1,0:T(8,128)(2,1)}, u32[]{:S(2)}, u32[]{:S(2)}) async-start(bf16[16,256,384]{2,1,0:T(8,128)(2,1)} %shard_map.67), calls=%async_computation.3 | async-start | bytes 6291456 | tf_op jit(solution)/shard_map/all_to_all | solution.py:220

commit v12 on v10

--- a/solution.py
+++ b/solution.py
@@ -89,7 +89,7 @@
 
 def attend(
     dest, q, table, k_arr, v_arr, lo, n_dest, head_dim, first, heads,
-    first_block, blocks, key_base, prev=None,
+    first_block, blocks, key_base, prev=None, k_col=0, v_col=0,
 ):
     rows, all_width = q.shape
     width = heads * head_dim
@@ -116,8 +116,8 @@
     ] + [
         pl.BlockSpec((block_rows, head_dim), lambda i, dst: (i + first_block + tail_blocks, 0)),
         pl.BlockSpec((block_rows, head_dim), lambda i, dst: (i + first_block + tail_blocks, 1)),
-        pl.BlockSpec((k_rows, head_dim), lambda i, dst: (0, 0)),
-        pl.BlockSpec((k_rows, head_dim), lambda i, dst: (0, 0)),
+        pl.BlockSpec((k_rows, head_dim), lambda i, dst: (0, k_col)),
+        pl.BlockSpec((k_rows, head_dim), lambda i, dst: (0, v_col)),
         pl.BlockSpec((1, block_rows, 1), lambda i, dst: (i + first_block, 0, 0)),
     ]
     args = [dest] + [q] * heads + [table, table, k_arr, v_arr, lo]
@@ -207,9 +207,16 @@
                 owner_row, queries, table, k_own, v_own, lo, ctx_size, head_dim, first, heads,
                 tail_blocks, per_dev - tail_blocks, tail_rows,
             )
+            near = jnp.concatenate(
+                [
+                    jnp.concatenate([k_tail, kv_tail[:, kv_width:]], axis=1),
+                    jnp.concatenate([k_own[:tail_rows], v_own[:tail_rows]], axis=1),
+                ],
+                axis=0,
+            )
             send = attend(
-                owner_row, queries, table, k_ext, v_ext, lo, ctx_size, head_dim, first, heads,
-                0, tail_blocks, 0, prev=send,
+                owner_row, queries, table, near, near, lo, ctx_size, head_dim,
+                first, heads, 0, tail_blocks, 0, prev=send, k_col=0, v_col=1,
             )
         else:
             send = attend(

time: 188 us -> 187 us (level)
  transfers between devices with their start and end apart: 5 -> 5, of which waited for: 4 -> 4; matrix products, arithmetic and copies ran while one was open for 12% -> 13% of each run, Pallas kernels for 23% -> 23%
where the time goes in v12:
time: 187 us; the launch traced here: 184 us
  waiting for transfers between devices  68 us (36%)
  Pallas kernels  48.3 us (26%)
  starting transfers between devices  32.7 us (17%)
  local copies, waits for them, and re-layouts  26.1 us (14%)
  other arithmetic  9.05 us (5%)
    all_to_all x3, waiting for transfers between devices, local(): lax.all_to_all(send, 'ctx', split_axis=0, concat_axis=0, tiled=True)  64.3 us
    pallas_call x4, Pallas kernels, attend(): pl.pallas_call(kernel, grid_spec=grid_spec, out_shape=jax.ShapeDtypeStruc...  48.3 us
    all_to_all x3, starting transfers between devices, local(): lax.all_to_all(send, 'ctx', split_axis=0, concat_axis=0, tiled=True)  20.5 us
    gather x3, local copies, waits for them, and re-layouts, local(): jnp.take(a, my_sources, axis=0, mode='clip')  7.76 us
    gather x1, local copies, waits for them, and re-layouts, rotation_rows(): jnp.take(table, jnp.clip(offsets, 0, distinct - 1), axis=0, mode='clip')  7 us
    all_to_all x1, starting transfers between devices, local(): kv = lax.all_to_all(kv, 'tp', split_axis=0, concat_axis=0, tiled=True)  6.19 us
    ppermute x1, starting transfers between devices, passed_along(): return lax.ppermute(shard, axis, pairs)  6.02 us
    dynamic_update_slice x3, local copies, waits for them, and re-layouts, local(): lax.dynamic_update_slice(finished, jnp.take(a, my_sources, axis=0, mode='...  5.2 us
  transfers between devices with their start and end apart: 5, of which 4 were waited for; matrix products, arithmetic and copies ran while one was open for 13% of the time, Pallas kernels for 23%

profile of v12, /device:TPU:1, one launch (start us, length us, event | category | flops | bytes accessed | tf_op | source)
XLA Modules:
  0.0 184.4 jit_solution(2046055288737656430)
XLA Ops:
  0.0 1.0 copy-done
  1.0 1.3 bitcast_bitcast_fusion
  2.4 1.1 pad_maximum_fusion
  3.5 6.2 %all-to-all-start = ((bf16[8,256,256]{2,1,0:T(8,128)(2,1)}), bf16[8,256,256]{2,1,0:T(8,128)(2,1)S(1)}, u32[]{:S(2)}, u32[]{:S(2)}) async-start(bf16[8,256,256]{2,1,0:T(8,128)(2,1)} %pad_maximum_fusion), calls=%async_computation | async-start | bytes 2097152 | tf_op jit(solution)/shard_map/all_to_all | solution.py:170
  10.9 1.6 select_reduce_fusion
  12.5 1.4 copy.30.refs_6_.refs_7_
  14.0 7.0 %gather_fusion = f32[2560,256]{1,0:T(8,128)} fusion(f32[512,256]{1,0:T(8,128)S(1)} %copy.26, s32[3072]{0:T(1024)S(1)} %pad_clamp_fusion), kind=kCustom, calls=%fused_computation | custom fusion | bytes 5253120 | tf_op jit(solution)/shard_map/jit(_take)/gather | solution.py:39
  21.0 0.7 dynamic-slice_reduce_fusion.dest_ref
  21.7 3.8 %all-to-all-done = bf16[8,256,256]{2,1,0:T(8,128)(2,1)S(1)} async-done(((bf16[8,256,256]{2,1,0:T(8,128)(2,1)}), bf16[8,256,256]{2,1,0:T(8,128)(2,1)S(1)}, u32[]{:S(2)}, u32[]{:S(2)}) %all-to-all-start) | async-done | bytes 1048608 | tf_op jit(solution)/shard_map/all_to_all | solution.py:170
  25.5 0.9 fusion.10
  26.8 6.0 %collective-permute-start = (bf16[512,256]{1,0:T(8,128)(2,1)S(1)}, bf16[512,256]{1,0:T(8,128)(2,1)S(1)}, u32[]{:S(2)}, u32[]{:S(2)}) collective-permute-start(bf16[512,256]{1,0:T(8,128)(2,1)S(1)} %bitcast.23), channel_id=1, source_target_pairs={{0,8},{8,16},{16,24},{24,32},{32,40},{40,48},{48,56},{56,64},{64,7... | collective-permute-start | bytes 786440 | tf_op jit(solution)/shard_map/ppermute | solution.py:17
  33.4 0.8 copy-done.2
  34.2 10.4 %shard_map.64.refs_7_ = bf16[16,256,256]{2,1,0:T(8,128)(2,1)} custom-call(s32[8]{0:T(128)} %dynamic-slice_reduce_fusion.dest_ref, bf16[2048,1024]{1,0:T(8,128)(2,1)} %refs_2_.3, bf16[2048,1024]{1,0:T(8,128)(2,1)} %refs_2_.3, f32[2560,256]{1,0:T(8,128)} %gather_fusion, f32[2560,256]{1,0:T(8,128)} %gather_fusion, bf16[2048,128]{1,0:T(8,128)(2,1)} %copy-done.2, ...), custom_call_target="tpu_custom_call" | custom-call | flops 1207959552 | bytes 2621440 | tf_op jit(solution)/shard_map/pallas_call | solution.py:135
  44.8 1.2 fusion.3
  46.0 0.8 maximum_maximum_fusion.refs_4_.refs_5_
  46.8 5.2 %shard_map.65 = bf16[16,256,256]{2,1,0:T(8,128)(2,1)} custom-call(s32[8]{0:T(128)} %dynamic-slice_reduce_fusion.dest_ref, bf16[2048,1024]{1,0:T(8,128)(2,1)} %refs_2_.3, bf16[2048,1024]{1,0:T(8,128)(2,1)} %refs_2_.3, f32[2560,256]{1,0:T(8,128)} %gather_fusion, f32[2560,256]{1,0:T(8,128)} %gather_fusion, ...), custom_call_target="tpu_custom_call", output_to_operand_aliasing={{}: (8, {})} | custom-call | flops 402653184 | bytes 1048576 | tf_op jit(solution)/shard_map/pallas_call | solution.py:135
  52.0 4.8 %all-to-all-start.1 = ((bf16[16,256,256]{2,1,0:T(8,128)(2,1)}), bf16[16,256,256]{2,1,0:T(8,128)(2,1)}, u32[]{:S(2)}, u32[]{:S(2)}) async-start(bf16[16,256,256]{2,1,0:T(8,128)(2,1)} %shard_map.65), calls=%async_computation.1 | async-start | bytes 4194304 | tf_op jit(solution)/shard_map/all_to_all | solution.py:226
  56.9 0.9 pad_maximum_fusion.1.refs_5_
  57.8 0.9 pad_maximum_fusion.2.refs_6_
  58.7 16.4 %shard_map.66 = bf16[16,256,384]{2,1,0:T(8,128)(2,1)} custom-call(s32[8]{0:T(128)} %dynamic-slice_reduce_fusion.dest_ref, bf16[2048,1024]{1,0:T(8,128)(2,1)} %refs_2_.3, bf16[2048,1024]{1,0:T(8,128)(2,1)} %refs_2_.3, bf16[2048,1024]{1,0:T(8,128)(2,1)} %refs_2_.3, f32[2560,256]{1,0:T(8,128)} %gather_fusion, f32[2560,256]{1,0:T(8,128)} %gather_fusion, ...), custom_call_target="tpu_custom_call" | custom-call | flops 2415919104 | bytes 4456448 | tf_op jit(solution)/shard_map/pallas_call | solution.py:135
  75.1 10.2 %all-to-all-done.1 = bf16[16,256,256]{2,1,0:T(8,128)(2,1)} async-done(((bf16[16,256,256]{2,1,0:T(8,128)(2,1)}), bf16[16,256,256]{2,1,0:T(8,128)(2,1)}, u32[]{:S(2)}, u32[]{:S(2)}) %all-to-all-start.1) | async-done | bytes 2097184 | tf_op jit(solution)/shard_map/all_to_all | solution.py:226
  85.3 5.8 %all-to-all-start.2 = ((bf16[16,256,384]{2,1,0:T(8,128)(2,1)}), bf16[16,256,384]{2,1,0:T(8,128)(2,1)}, u32[]{:S(2)}, u32[]{:S(2)}) async-start(bf16[16,256,384]{2,1,0:T(8,128)(2,1)} %shard_map.66), calls=%async_computation.2 | async-start | bytes 6291456 | tf_op jit(solution)/shard_map/all_to_all | solution.py:226
  91.1 16.4 %shard_map.67 = bf16[16,256,384]{2,1,0:T(8,128)(2,1)} custom-call(s32[8]{0:T(128)} %dynamic-slice_reduce_fusion.dest_ref, bf16[2048,1024]{1,0:T(8,128)(2,1)} %refs_2_.3, bf16[2048,1024]{1,0:T(8,128)(2,1)} %refs_2_.3, bf16[2048,1024]{1,0:T(8,128)(2,1)} %refs_2_.3, f32[2560,256]{1,0:T(8,128)} %gather_fusion, f32[2560,256]{1,0:T(8,128)} %gather_fusion, ...), custom_call_target="tpu_custom_call" | custom-call | flops 2415919104 | bytes 4456448 | tf_op jit(solution)/shard_map/pallas_call | solution.py:135
  107.5 23.3 %all-to-all-done.2 = bf16[16,256,384]{2,1,0:T(8,128)(2,1)} async-done(((bf16[16,256,384]{2,1,0:T(8,128)(2,1)}), bf16[16,256,384]{2,1,0:T(8,128)(2,1)}, u32[]{:S(2)}, u32[]{:S(2)}) %all-to-all-start.2) | async-done | bytes 3145760 | tf_op jit(solution)/shard_map/all_to_all | solution.py:226
  130.8 9.8 %all-to-all-start.3 = ((bf16[16,256,384]{2,1,0:T(8,128)(2,1)}), bf16[16,256,384]{2,1,0:T(8,128)(2,1)}, u32[]{:S(2)}, u32[]{:S(2)}) async-start(bf16[16,256,384]{2,1,0:T(8,128)(2,1)} %shard_map.67), calls=%async_computation.3 | async-start | bytes 6291456 | tf_op jit(solution)/shard_map/all_to_all | solution.py:226
  140.7 2.2 %gather_fusion.1 = bf16[8,256,256]{2,1,0:T(8,128)(2,1)S(1)} fusion(bf16[16,256,256]{2,1,0:T(8,128)(2,1)} %all-to-all-done.1, s32[1024]{0:T(1024)S(1)} %pad_clamp_fusion.1), kind=kCustom, calls=%fused_computation.1 | custom fusion | bytes 2097184 | tf_op jit(solution)/shard_map/jit(_take)/gather | solution.py:237
  143.0 2.6 %dynamic_update_slice.9 = bf16[8,256,1024]{2,1,0:T(8,128)(2,1)} pad(bf16[8,256,256]{2,1,0:T(8,128)(2,1)S(1)} %gather_fusion.1, bf16[]{:T(256)} %constant.49.clone.1), padding=0_0x0_0x0_768 | pad | bytes 5242882 | tf_op jit(solution)/shard_map/dynamic_update_slice | solution.py:236
  145.5 2.8 %gather_fusion.2 = bf16[8,256,384]{2,1,0:T(8,128)(2,1)S(1)} fusion(bf16[16,256,384]{2,1,0:T(8,128)(2,1)} %all-to-all-done.2, s32[1024]{0:T(1024)S(1)} %pad_clamp_fusion.1), kind=kCustom, calls=%fused_computation.2 | custom fusion | bytes 3145760 | tf_op jit(solution)/shard_map/jit(_take)/gather | solution.py:237
  148.3 1.3 constant_dynamic-update-slice_fusion
  149.6 30.7 %all-to-all-done.3 = bf16[16,256,384]{2,1,0:T(8,128)(2,1)} async-done(((bf16[16,256,384]{2,1,0:T(8,128)(2,1)}), bf16[16,256,384]{2,1,0:T(8,128)(2,1)}, u32[]{:S(2)}, u32[]{:S(2)}) %all-to-all-start.3) | async-done | bytes 3145760 | tf_op jit(solution)/shard_map/all_to_all | solution.py:226
  180.3 2.8 %gather_fusion.3 = bf16[8,256,384]{2,1,0:T(8,128)(2,1)S(1)} fusion(bf16[16,256,384]{2,1,0:T(8,128)(2,1)} %all-to-all-done.3, s32[1024]{0:T(1024)S(1)} %pad_clamp_fusion.1), kind=kCustom, calls=%fused_computation.3 | custom fusion | bytes 3145760 | tf_op jit(solution)/shard_map/jit(_take)/gather | solution.py:237
  183.1 1.3 constant_dynamic-update-slice_fusion.1
  (38 shorter events, 2.4 us)
Async XLA Ops:
  0.0 1.0 copy-start
  2.3 7.3 %copy-start.6 = (s32[128]{0:T(128)S(1)}, s32[128]{0:T(128)}, u32[]{:S(2)}) copy-start(s32[128]{0:T(128)} %param.10) | copy-start | bytes 1540
  2.4 7.7 %copy-start.7 = (f32[64]{0:T(128)S(1)}, f32[64]{0:T(128)}, u32[]{:S(2)}) copy-start(f32[64]{0:T(128)} %param.9) | copy-start | bytes 772
  3.5 22.1 %all-to-all-start = ((bf16[8,256,256]{2,1,0:T(8,128)(2,1)}), bf16[8,256,256]{2,1,0:T(8,128)(2,1)S(1)}, u32[]{:S(2)}, u32[]{:S(2)}) async-start(bf16[8,256,256]{2,1,0:T(8,128)(2,1)} %pad_maximum_fusion), calls=%async_computation | async-start | bytes 2097152 | tf_op jit(solution)/shard_map/all_to_all | solution.py:170
  14.0 7.0 %copy-start.5 = (s32[16,8]{0,1:T(8,128)S(1)}, s32[16,8]{0,1:T(8,128)}, u32[]{:S(2)}) copy-start(s32[16,8]{0,1:T(8,128)} %param.11) | copy-start | bytes 1540
  26.4 6.4 %copy-start.1 = (f32[2560,256]{1,0:T(8,128)S(1)}, f32[2560,256]{1,0:T(8,128)}, u32[]{:S(2)}) copy-start(f32[2560,256]{1,0:T(8,128)} %gather_fusion) | copy-start | bytes 7864324
  26.8 17.8 %collective-permute-start = (bf16[512,256]{1,0:T(8,128)(2,1)S(1)}, bf16[512,256]{1,0:T(8,128)(2,1)S(1)}, u32[]{:S(2)}, u32[]{:S(2)}) collective-permute-start(bf16[512,256]{1,0:T(8,128)(2,1)S(1)} %bitcast.23), channel_id=1, source_target_pairs={{0,8},{8,16},{16,24},{24,32},{32,40},{40,48},{48,56},{56,64},{64,7... | collective-permute-start | bytes 786440 | tf_op jit(solution)/shard_map/ppermute | solution.py:17
  33.3 0.9 copy-start.2
  44.6 1.4 slice-start
  52.0 4.9 %copy-start.3 = (bf16[2048,128]{1,0:T(8,128)(2,1)S(1)}, bf16[2048,128]{1,0:T(8,128)(2,1)}, u32[]{:S(2)}) copy-start(bf16[2048,128]{1,0:T(8,128)(2,1)} %copy-done.2) | copy-start | bytes 1572868
  52.0 5.7 %copy-start.4 = (bf16[2048,128]{1,0:T(8,128)(2,1)S(1)}, bf16[2048,128]{1,0:T(8,128)(2,1)}, u32[]{:S(2)}) copy-start(bf16[2048,128]{1,0:T(8,128)(2,1)} %get-tuple-element.5.refs_5_) | copy-start | bytes 1572868
  52.0 33.3 %all-to-all-start.1 = ((bf16[16,256,256]{2,1,0:T(8,128)(2,1)}), bf16[16,256,256]{2,1,0:T(8,128)(2,1)}, u32[]{:S(2)}, u32[]{:S(2)}) async-start(bf16[16,256,256]{2,1,0:T(8,128)(2,1)} %shard_map.65), calls=%async_computation.1 | async-start | bytes 4194304 | tf_op jit(solution)/shard_map/all_to_all | solution.py:226
  85.3 45.5 %all-to-all-start.2 = ((bf16[16,256,384]{2,1,0:T(8,128)(2,1)}), bf16[16,256,384]{2,1,0:T(8,128)(2,1)}, u32[]{:S(2)}, u32[]{:S(2)}) async-start(bf16[16,256,384]{2,1,0:T(8,128)(2,1)} %shard_map.66), calls=%async_computation.2 | async-start | bytes 6291456 | tf_op jit(solution)/shard_map/all_to_all | solution.py:226
  130.8 49.5 %all-to-all-start.3 = ((bf16[16,256,384]{2,1,0:T(8,128)(2,1)}), bf16[16,256,384]{2,1,0:T(8,128)(2,1)}, u32[]{:S(2)}, u32[]{:S(2)}) async-start(bf16[16,256,384]{2,1,0:T(8,128)(2,1)} %shard_map.67), calls=%async_computation.3 | async-start | bytes 6291456 | tf_op jit(solution)/shard_map/all_to_all | solution.py:226

commit v13 on v12

--- a/solution.py
+++ b/solution.py
@@ -56,39 +56,53 @@
 
 
 def attend_kernel(
-    dest_ref, *refs, heads, head_dim, block_rows, span, scale, first_block, key_base, aliased
+    dest_ref, kmin_ref, *refs, heads, head_dim, block_rows, span, scale, first_block, key_base,
+    aliased,
 ):
     q_refs = refs[:heads]
     cos_ref, sin_ref, k_ref, v_ref, lo_ref = refs[heads : heads + 5]
     o_ref = refs[-1]
     r = pl.program_id(0) + first_block
     start = pl.multiple_of(r * block_rows - key_base, block_rows)
-    k = k_ref[pl.ds(start, span), :]
-    v = v_ref[pl.ds(start, span), :]
     tail = span - block_rows
     lo = lo_ref[0]
     hi = lax.broadcasted_iota(jnp.int32, (block_rows, 1), 0) + tail
-    col = lax.broadcasted_iota(jnp.int32, (block_rows, span), 1)
-    visible = (col >= lo) & (col <= hi)
     cos = cos_ref[...]
     sin = sin_ref[...]
-    for h in range(heads):
-        cols = slice(h * head_dim, (h + 1) * head_dim)
-        qh = q_refs[h][...].astype(jnp.float32)
-        qr = (qh * cos + pltpu.roll(qh, head_dim // 2, 1) * sin).astype(jnp.bfloat16)
-        s = lax.dot_general(
-            qr, k, (((1,), (1,)), ((), ())), preferred_element_type=jnp.float32
-        ) * scale
-        s = jnp.where(visible, s, -1e30)
-        m = jnp.max(s, axis=1, keepdims=True)
-        p = jnp.exp(s - m)
-        l = jnp.sum(p, axis=1, keepdims=True)
-        o = jnp.dot(p.astype(jnp.bfloat16), v, preferred_element_type=jnp.float32)
-        o_ref[0, :, cols] = (o / l).astype(o_ref.dtype)
+
+    def window(skip):
+        width = span - skip
+        k = k_ref[pl.ds(start + skip, width), :]
+        v = v_ref[pl.ds(start + skip, width), :]
+        col = lax.broadcasted_iota(jnp.int32, (block_rows, width), 1) + skip
+        visible = (col >= lo) & (col <= hi)
+        for h in range(heads):
+            cols = slice(h * head_dim, (h + 1) * head_dim)
+            qh = q_refs[h][...].astype(jnp.float32)
+            qr = (qh * cos + pltpu.roll(qh, head_dim // 2, 1) * sin).astype(jnp.bfloat16)
+            s = lax.dot_general(
+                qr, k, (((1,), (1,)), ((), ())), preferred_element_type=jnp.float32
+            ) * scale
+            s = jnp.where(visible, s, -1e30)
+            m = jnp.max(s, axis=1, keepdims=True)
+            p = jnp.exp(s - m)
+            l = jnp.sum(p, axis=1, keepdims=True)
+            o = jnp.dot(p.astype(jnp.bfloat16), v, preferred_element_type=jnp.float32)
+            o_ref[0, :, cols] = (o / l).astype(o_ref.dtype)
+
+    kmin = kmin_ref[r]
+
+    @pl.when(kmin >= block_rows)
+    def _():
+        window(block_rows)
+
+    @pl.when(kmin < block_rows)
+    def _():
+        window(0)
 
 
 def attend(
-    dest, q, table, k_arr, v_arr, lo, n_dest, head_dim, first, heads,
+    dest, kmin, q, table, k_arr, v_arr, lo, n_dest, head_dim, first, heads,
     first_block, blocks, key_base, prev=None, k_col=0, v_col=0,
 ):
     rows, all_width = q.shape
@@ -111,26 +125,28 @@
     flops = 4 * blocks * heads * block_rows * span * head_dim
     in_specs = [
         pl.BlockSpec((block_rows, head_dim), functools.partial(
-            lambda i, dst, col: (i + first_block, col), col=first + head))
+            lambda i, dst, km, col: (i + first_block, col), col=first + head))
         for head in range(heads)
     ] + [
-        pl.BlockSpec((block_rows, head_dim), lambda i, dst: (i + first_block + tail_blocks, 0)),
-        pl.BlockSpec((block_rows, head_dim), lambda i, dst: (i + first_block + tail_blocks, 1)),
-        pl.BlockSpec((k_rows, head_dim), lambda i, dst: (0, k_col)),
-        pl.BlockSpec((k_rows, head_dim), lambda i, dst: (0, v_col)),
-        pl.BlockSpec((1, block_rows, 1), lambda i, dst: (i + first_block, 0, 0)),
+        pl.BlockSpec((block_rows, head_dim), lambda i, dst, km: (i + first_block + tail_blocks, 0)),
+        pl.BlockSpec((block_rows, head_dim), lambda i, dst, km: (i + first_block + tail_blocks, 1)),
+        pl.BlockSpec((k_rows, head_dim), lambda i, dst, km: (0, k_col)),
+        pl.BlockSpec((k_rows, head_dim), lambda i, dst, km: (0, v_col)),
+        pl.BlockSpec((1, block_rows, 1), lambda i, dst, km: (i + first_block, 0, 0)),
     ]
-    args = [dest] + [q] * heads + [table, table, k_arr, v_arr, lo]
+    args = [dest, kmin] + [q] * heads + [table, table, k_arr, v_arr, lo]
     aliases = {}
     if prev is not None:
         in_specs.append(pl.BlockSpec(memory_space=pl.ANY))
         args.append(prev)
         aliases = {len(args) - 1: 0}
     grid_spec = pltpu.PrefetchScalarGridSpec(
-        num_scalar_prefetch=1,
+        num_scalar_prefetch=2,
         grid=(blocks,),
         in_specs=in_specs,
-        out_specs=pl.BlockSpec((1, block_rows, width), lambda i, dst: (dst[i + first_block], 0, 0)),
+        out_specs=pl.BlockSpec(
+            (1, block_rows, width), lambda i, dst, km: (dst[i + first_block], 0, 0)
+        ),
     )
     return pl.pallas_call(
         kernel,
@@ -192,6 +208,7 @@
 
     lo = (tail_rows + jnp.arange(row_count, dtype=jnp.int32) % block_rows - off_ext[tail_rows:])
     lo = lo.reshape(per_dev, block_rows, 1)
+    kmin = lo[:, 0, 0]
 
     devices = jnp.arange(ctx_size, dtype=jnp.int32)
     owner_row = lax.dynamic_index_in_dim(owner_map, ctx_index, 0, keepdims=False)
@@ -204,7 +221,7 @@
     for number, heads in enumerate(sizes):
         if number == 0:
             send = attend(
-                owner_row, queries, table, k_own, v_own, lo, ctx_size, head_dim, first, heads,
+                owner_row, kmin, queries, table, k_own, v_own, lo, ctx_size, head_dim, first, heads,
                 tail_blocks, per_dev - tail_blocks, tail_rows,
             )
             near = jnp.concatenate(
@@ -215,12 +232,12 @@
                 axis=0,
             )
             send = attend(
-                owner_row, queries, table, near, near, lo, ctx_size, head_dim,
+                owner_row, kmin, queries, table, near, near, lo, ctx_size, head_dim,
                 first, heads, 0, tail_blocks, 0, prev=send, k_col=0, v_col=1,
             )
         else:
             send = attend(
-                owner_row, queries, table, k_ext, v_ext, lo, ctx_size, head_dim, first, heads,
+                owner_row, kmin, queries, table, k_ext, v_ext, lo, ctx_size, head_dim, first, heads,
                 0, per_dev, 0,
             )
         arrived.append(lax.all_to_all(send, "ctx", split_axis=0, concat_axis=0, tiled=True))

time: 187 us -> 186 us (level)
  Pallas kernels: 48.3 us -> 44.9 us
  waiting for transfers between devices: 68 us -> 70 us
    pallas_call x4, Pallas kernels: 48.3 us -> 44.9 us  [attend(): pl.pallas_call(kernel, grid_spec=grid_spec, out_shape=jax.ShapeDtypeStruc...]
    all_to_all x3, waiting for transfers between devices: 64.3 us -> 66.9 us  [local(): lax.all_to_all(send, 'ctx', split_axis=0, concat_axis=0, tiled=True)]
  transfers between devices with their start and end apart: 5 -> 5, of which waited for: 4 -> 4; matrix products, arithmetic and copies ran while one was open for 13% -> 13% of each run, Pallas kernels for 23% -> 22%
where the time goes in v13:
time: 186 us; the launch traced here: 184 us
  waiting for transfers between devices  70 us (38%)
  Pallas kernels  44.9 us (24%)
  starting transfers between devices  32.7 us (18%)
  local copies, waits for them, and re-layouts  26.7 us (14%)
  other arithmetic  9.08 us (5%)
    all_to_all x3, waiting for transfers between devices, local(): lax.all_to_all(send, 'ctx', split_axis=0, concat_axis=0, tiled=True)  66.9 us
    pallas_call x4, Pallas kernels, attend(): pl.pallas_call(kernel, grid_spec=grid_spec, out_shape=jax.ShapeDtypeStruc...  44.9 us
    all_to_all x3, starting transfers between devices, local(): lax.all_to_all(send, 'ctx', split_axis=0, concat_axis=0, tiled=True)  20.5 us
    gather x3, local copies, waits for them, and re-layouts, local(): jnp.take(a, my_sources, axis=0, mode='clip')  7.76 us
    gather x1, local copies, waits for them, and re-layouts, rotation_rows(): jnp.take(table, jnp.clip(offsets, 0, distinct - 1), axis=0, mode='clip')  7.01 us
    all_to_all x1, starting transfers between devices, local(): kv = lax.all_to_all(kv, 'tp', split_axis=0, concat_axis=0, tiled=True)  6.19 us
    ppermute x1, starting transfers between devices, passed_along(): return lax.ppermute(shard, axis, pairs)  6.02 us
    dynamic_update_slice x3, local copies, waits for them, and re-layouts, local(): lax.dynamic_update_slice(finished, jnp.take(a, my_sources, axis=0, mode='...  5.2 us
  transfers between devices with their start and end apart: 5, of which 4 were waited for; matrix products, arithmetic and copies ran while one was open for 13% of the time, Pallas kernels for 22%

profile of v13, /device:TPU:1, one launch (start us, length us, event | category | flops | bytes accessed | tf_op | source)
XLA Modules:
  0.0 183.7 jit_solution(3365679393040825495)
XLA Ops:
  0.0 1.0 copy-done
  1.0 1.3 bitcast_bitcast_fusion
  2.4 1.1 pad_maximum_fusion
  3.5 6.2 %all-to-all-start = ((bf16[8,256,256]{2,1,0:T(8,128)(2,1)}), bf16[8,256,256]{2,1,0:T(8,128)(2,1)S(1)}, u32[]{:S(2)}, u32[]{:S(2)}) async-start(bf16[8,256,256]{2,1,0:T(8,128)(2,1)} %pad_maximum_fusion), calls=%async_computation | async-start | bytes 2097152 | tf_op jit(solution)/shard_map/all_to_all | solution.py:186
  10.9 1.6 select_reduce_fusion
  12.6 1.4 copy.30.refs_6_.refs_7_
  14.0 7.0 %gather_fusion = f32[2560,256]{1,0:T(8,128)} fusion(f32[512,256]{1,0:T(8,128)S(1)} %copy.26, s32[3072]{0:T(1024)S(1)} %pad_clamp_fusion), kind=kCustom, calls=%fused_computation | custom fusion | bytes 5253120 | tf_op jit(solution)/shard_map/jit(_take)/gather | solution.py:39
  21.0 0.8 dynamic-slice_reduce_fusion.dest_ref
  22.4 3.1 %all-to-all-done = bf16[8,256,256]{2,1,0:T(8,128)(2,1)S(1)} async-done(((bf16[8,256,256]{2,1,0:T(8,128)(2,1)}), bf16[8,256,256]{2,1,0:T(8,128)(2,1)S(1)}, u32[]{:S(2)}, u32[]{:S(2)}) %all-to-all-start) | async-done | bytes 1048608 | tf_op jit(solution)/shard_map/all_to_all | solution.py:186
  25.5 0.9 fusion.10
  26.8 6.0 %collective-permute-start = (bf16[512,256]{1,0:T(8,128)(2,1)S(1)}, bf16[512,256]{1,0:T(8,128)(2,1)S(1)}, u32[]{:S(2)}, u32[]{:S(2)}) collective-permute-start(bf16[512,256]{1,0:T(8,128)(2,1)S(1)} %bitcast.23), channel_id=1, source_target_pairs={{0,8},{8,16},{16,24},{24,32},{32,40},{40,48},{48,56},{56,64},{64,7... | collective-permute-start | bytes 786440 | tf_op jit(solution)/shard_map/ppermute | solution.py:17
  33.4 0.8 copy-done.2
  34.2 9.9 %shard_map.64.refs_7_ = bf16[16,256,256]{2,1,0:T(8,128)(2,1)} custom-call(s32[8]{0:T(128)} %dynamic-slice_reduce_fusion.dest_ref, s32[8]{0:T(128)} %slice_reduce_fusion.kmin_ref, bf16[2048,1024]{1,0:T(8,128)(2,1)} %refs_2_.3, bf16[2048,1024]{1,0:T(8,128)(2,1)} %refs_2_.3, f32[2560,256]{1,0:T(8,128)} %gather_fusion, f32[2560,256]{1,0:T(8,128)} %gather_fusion, ...), custom_call_target="tpu_custom_call" | custom-call | flops 1207959552 | bytes 2621440 | tf_op jit(solution)/shard_map/pallas_call | solution.py:151
  44.3 1.2 fusion.3
  45.5 0.9 maximum_maximum_fusion.refs_4_.refs_5_
  46.3 4.9 %shard_map.65 = bf16[16,256,256]{2,1,0:T(8,128)(2,1)} custom-call(s32[8]{0:T(128)} %dynamic-slice_reduce_fusion.dest_ref, s32[8]{0:T(128)} %slice_reduce_fusion.kmin_ref, bf16[2048,1024]{1,0:T(8,128)(2,1)} %refs_2_.3, bf16[2048,1024]{1,0:T(8,128)(2,1)} %refs_2_.3, f32[2560,256]{1,0:T(8,128)} %gather_fusion, ...), custom_call_target="tpu_custom_call", output_to_operand_aliasing={{}: (9, {})} | custom-call | flops 402653184 | bytes 1048576 | tf_op jit(solution)/shard_map/pallas_call | solution.py:151
  51.3 4.9 %all-to-all-start.1 = ((bf16[16,256,256]{2,1,0:T(8,128)(2,1)}), bf16[16,256,256]{2,1,0:T(8,128)(2,1)}, u32[]{:S(2)}, u32[]{:S(2)}) async-start(bf16[16,256,256]{2,1,0:T(8,128)(2,1)} %shard_map.65), calls=%async_computation.1 | async-start | bytes 4194304 | tf_op jit(solution)/shard_map/all_to_all | solution.py:243
  56.1 0.9 pad_maximum_fusion.1.refs_5_
  57.0 0.9 pad_maximum_fusion.2.refs_6_
  58.0 15.0 %shard_map.66 = bf16[16,256,384]{2,1,0:T(8,128)(2,1)} custom-call(s32[8]{0:T(128)} %dynamic-slice_reduce_fusion.dest_ref, s32[8]{0:T(128)} %slice_reduce_fusion.kmin_ref, bf16[2048,1024]{1,0:T(8,128)(2,1)} %refs_2_.3, bf16[2048,1024]{1,0:T(8,128)(2,1)} %refs_2_.3, bf16[2048,1024]{1,0:T(8,128)(2,1)} %refs_2_.3, f32[2560,256]{1,0:T(8,128)} %gather_fusion, ...), custom_call_target="tpu_custom_call" | custom-call | flops 2415919104 | bytes 4456448 | tf_op jit(solution)/shard_map/pallas_call | solution.py:151
  73.0 11.5 %all-to-all-done.1 = bf16[16,256,256]{2,1,0:T(8,128)(2,1)} async-done(((bf16[16,256,256]{2,1,0:T(8,128)(2,1)}), bf16[16,256,256]{2,1,0:T(8,128)(2,1)}, u32[]{:S(2)}, u32[]{:S(2)}) %all-to-all-start.1) | async-done | bytes 2097184 | tf_op jit(solution)/shard_map/all_to_all | solution.py:243
  84.5 5.8 %all-to-all-start.2 = ((bf16[16,256,384]{2,1,0:T(8,128)(2,1)}), bf16[16,256,384]{2,1,0:T(8,128)(2,1)}, u32[]{:S(2)}, u32[]{:S(2)}) async-start(bf16[16,256,384]{2,1,0:T(8,128)(2,1)} %shard_map.66), calls=%async_computation.2 | async-start | bytes 6291456 | tf_op jit(solution)/shard_map/all_to_all | solution.py:243
  90.4 15.0 %shard_map.67 = bf16[16,256,384]{2,1,0:T(8,128)(2,1)} custom-call(s32[8]{0:T(128)} %dynamic-slice_reduce_fusion.dest_ref, s32[8]{0:T(128)} %slice_reduce_fusion.kmin_ref, bf16[2048,1024]{1,0:T(8,128)(2,1)} %refs_2_.3, bf16[2048,1024]{1,0:T(8,128)(2,1)} %refs_2_.3, bf16[2048,1024]{1,0:T(8,128)(2,1)} %refs_2_.3, f32[2560,256]{1,0:T(8,128)} %gather_fusion, ...), custom_call_target="tpu_custom_call" | custom-call | flops 2415919104 | bytes 4456448 | tf_op jit(solution)/shard_map/pallas_call | solution.py:151
  105.4 24.7 %all-to-all-done.2 = bf16[16,256,384]{2,1,0:T(8,128)(2,1)} async-done(((bf16[16,256,384]{2,1,0:T(8,128)(2,1)}), bf16[16,256,384]{2,1,0:T(8,128)(2,1)}, u32[]{:S(2)}, u32[]{:S(2)}) %all-to-all-start.2) | async-done | bytes 3145760 | tf_op jit(solution)/shard_map/all_to_all | solution.py:243
  130.1 9.8 %all-to-all-start.3 = ((bf16[16,256,384]{2,1,0:T(8,128)(2,1)}), bf16[16,256,384]{2,1,0:T(8,128)(2,1)}, u32[]{:S(2)}, u32[]{:S(2)}) async-start(bf16[16,256,384]{2,1,0:T(8,128)(2,1)} %shard_map.67), calls=%async_computation.3 | async-start | bytes 6291456 | tf_op jit(solution)/shard_map/all_to_all | solution.py:243
  140.0 2.2 %gather_fusion.1 = bf16[8,256,256]{2,1,0:T(8,128)(2,1)S(1)} fusion(bf16[16,256,256]{2,1,0:T(8,128)(2,1)} %all-to-all-done.1, s32[1024]{0:T(1024)S(1)} %pad_clamp_fusion.1), kind=kCustom, calls=%fused_computation.1 | custom fusion | bytes 2097184 | tf_op jit(solution)/shard_map/jit(_take)/gather | solution.py:254
  142.2 2.6 %dynamic_update_slice.9 = bf16[8,256,1024]{2,1,0:T(8,128)(2,1)} pad(bf16[8,256,256]{2,1,0:T(8,128)(2,1)S(1)} %gather_fusion.1, bf16[]{:T(256)} %constant.49.clone.1), padding=0_0x0_0x0_768 | pad | bytes 5242882 | tf_op jit(solution)/shard_map/dynamic_update_slice | solution.py:253
  144.8 2.8 %gather_fusion.2 = bf16[8,256,384]{2,1,0:T(8,128)(2,1)S(1)} fusion(bf16[16,256,384]{2,1,0:T(8,128)(2,1)} %all-to-all-done.2, s32[1024]{0:T(1024)S(1)} %pad_clamp_fusion.1), kind=kCustom, calls=%fused_computation.2 | custom fusion | bytes 3145760 | tf_op jit(solution)/shard_map/jit(_take)/gather | solution.py:254
  147.6 1.3 constant_dynamic-update-slice_fusion.1
  148.9 30.7 %all-to-all-done.3 = bf16[16,256,384]{2,1,0:T(8,128)(2,1)} async-done(((bf16[16,256,384]{2,1,0:T(8,128)(2,1)}), bf16[16,256,384]{2,1,0:T(8,128)(2,1)}, u32[]{:S(2)}, u32[]{:S(2)}) %all-to-all-start.3) | async-done | bytes 3145760 | tf_op jit(solution)/shard_map/all_to_all | solution.py:243
  179.6 2.8 %gather_fusion.3 = bf16[8,256,384]{2,1,0:T(8,128)(2,1)S(1)} fusion(bf16[16,256,384]{2,1,0:T(8,128)(2,1)} %all-to-all-done.3, s32[1024]{0:T(1024)S(1)} %pad_clamp_fusion.1), kind=kCustom, calls=%fused_computation.3 | custom fusion | bytes 3145760 | tf_op jit(solution)/shard_map/jit(_take)/gather | solution.py:254
  182.4 1.3 constant_dynamic-update-slice_fusion
  (39 shorter events, 3.0 us)
Async XLA Ops:
  0.0 1.0 copy-start
  2.3 7.3 %copy-start.7 = (f32[64]{0:T(128)S(1)}, f32[64]{0:T(128)}, u32[]{:S(2)}) copy-start(f32[64]{0:T(128)} %param.9) | copy-start | bytes 772
  2.4 7.9 %copy-start.6 = (s32[128]{0:T(128)S(1)}, s32[128]{0:T(128)}, u32[]{:S(2)}) copy-start(s32[128]{0:T(128)} %param.10) | copy-start | bytes 1540
  3.5 22.1 %all-to-all-start = ((bf16[8,256,256]{2,1,0:T(8,128)(2,1)}), bf16[8,256,256]{2,1,0:T(8,128)(2,1)S(1)}, u32[]{:S(2)}, u32[]{:S(2)}) async-start(bf16[8,256,256]{2,1,0:T(8,128)(2,1)} %pad_maximum_fusion), calls=%async_computation | async-start | bytes 2097152 | tf_op jit(solution)/shard_map/all_to_all | solution.py:186
  14.0 7.0 %copy-start.5 = (s32[16,8]{0,1:T(8,128)S(1)}, s32[16,8]{0,1:T(8,128)}, u32[]{:S(2)}) copy-start(s32[16,8]{0,1:T(8,128)} %param.11) | copy-start | bytes 1540
  26.4 6.4 %copy-start.1 = (f32[2560,256]{1,0:T(8,128)S(1)}, f32[2560,256]{1,0:T(8,128)}, u32[]{:S(2)}) copy-start(f32[2560,256]{1,0:T(8,128)} %gather_fusion) | copy-start | bytes 7864324
  26.8 17.3 %collective-permute-start = (bf16[512,256]{1,0:T(8,128)(2,1)S(1)}, bf16[512,256]{1,0:T(8,128)(2,1)S(1)}, u32[]{:S(2)}, u32[]{:S(2)}) collective-permute-start(bf16[512,256]{1,0:T(8,128)(2,1)S(1)} %bitcast.23), channel_id=1, source_target_pairs={{0,8},{8,16},{16,24},{24,32},{32,40},{40,48},{48,56},{56,64},{64,7... | collective-permute-start | bytes 786440 | tf_op jit(solution)/shard_map/ppermute | solution.py:17
  33.3 0.8 copy-start.2
  44.1 1.4 slice-start
  51.3 4.9 %copy-start.3 = (bf16[2048,128]{1,0:T(8,128)(2,1)S(1)}, bf16[2048,128]{1,0:T(8,128)(2,1)}, u32[]{:S(2)}) copy-start(bf16[2048,128]{1,0:T(8,128)(2,1)} %copy-done.2) | copy-start | bytes 1572868
  51.3 5.8 %copy-start.4 = (bf16[2048,128]{1,0:T(8,128)(2,1)S(1)}, bf16[2048,128]{1,0:T(8,128)(2,1)}, u32[]{:S(2)}) copy-start(bf16[2048,128]{1,0:T(8,128)(2,1)} %get-tuple-element.5.refs_5_) | copy-start | bytes 1572868
  51.3 33.3 %all-to-all-start.1 = ((bf16[16,256,256]{2,1,0:T(8,128)(2,1)}), bf16[16,256,256]{2,1,0:T(8,128)(2,1)}, u32[]{:S(2)}, u32[]{:S(2)}) async-start(bf16[16,256,256]{2,1,0:T(8,128)(2,1)} %shard_map.65), calls=%async_computation.1 | async-start | bytes 4194304 | tf_op jit(solution)/shard_map/all_to_all | solution.py:243
  84.5 45.5 %all-to-all-start.2 = ((bf16[16,256,384]{2,1,0:T(8,128)(2,1)}), bf16[16,256,384]{2,1,0:T(8,128)(2,1)}, u32[]{:S(2)}, u32[]{:S(2)}) async-start(bf16[16,256,384]{2,1,0:T(8,128)(2,1)} %shard_map.66), calls=%async_computation.2 | async-start | bytes 6291456 | tf_op jit(solution)/shard_map/all_to_all | solution.py:243
  130.1 49.5 %all-to-all-start.3 = ((bf16[16,256,384]{2,1,0:T(8,128)(2,1)}), bf16[16,256,384]{2,1,0:T(8,128)(2,1)}, u32[]{:S(2)}, u32[]{:S(2)}) async-start(bf16[16,256,384]{2,1,0:T(8,128)(2,1)} %shard_map.67), calls=%async_computation.3 | async-start | bytes 6291456 | tf_op jit(solution)/shard_map/all_to_all | solution.py:243

commit v14 on v13

--- a/solution.py
+++ b/solution.py
@@ -72,8 +72,9 @@
 
     def window(skip):
         width = span - skip
-        k = k_ref[pl.ds(start + skip, width), :]
-        v = v_ref[pl.ds(start + skip, width), :]
+        first_key = pl.multiple_of(start + skip, 128)
+        k = k_ref[pl.ds(first_key, width), :]
+        v = v_ref[pl.ds(first_key, width), :]
         col = lax.broadcasted_iota(jnp.int32, (block_rows, width), 1) + skip
         visible = (col >= lo) & (col <= hi)
         for h in range(heads):
@@ -90,15 +91,13 @@
             o = jnp.dot(p.astype(jnp.bfloat16), v, preferred_element_type=jnp.float32)
             o_ref[0, :, cols] = (o / l).astype(o_ref.dtype)
 
-    kmin = kmin_ref[r]
-
-    @pl.when(kmin >= block_rows)
-    def _():
-        window(block_rows)
-
-    @pl.when(kmin < block_rows)
-    def _():
-        window(0)
+    tile = 128
+    tiles = lax.min(kmin_ref[r] // tile, (span - block_rows) // tile - 1)
+    for skipped in range((span - block_rows) // tile):
+
+        @pl.when(tiles == skipped)
+        def _():
+            window(skipped * tile)
 
 
 def attend(

time: 186 us -> 186 us (level)
  Pallas kernels: 44.9 us -> 41.9 us
  waiting for transfers between devices: 70 us -> 72.3 us
    pallas_call x4, Pallas kernels: 44.9 us -> 41.9 us  [attend(): pl.pallas_call(kernel, grid_spec=grid_spec, out_shape=jax.ShapeDtypeStruc...]
    all_to_all x3, waiting for transfers between devices: 66.9 us -> 69.2 us  [local(): lax.all_to_all(send, 'ctx', split_axis=0, concat_axis=0, tiled=True)]
  transfers between devices with their start and end apart: 5 -> 5, of which waited for: 4 -> 4; matrix products, arithmetic and copies ran while one was open for 13% -> 13% of each run, Pallas kernels for 22% -> 20%
where the time goes in v14:
time: 186 us; the launch traced here: 183 us
  waiting for transfers between devices  72.3 us (39%)
  Pallas kernels  41.9 us (23%)
  starting transfers between devices  32.9 us (18%)
  local copies, waits for them, and re-layouts  26.7 us (14%)
  other arithmetic  9.08 us (5%)
    all_to_all x3, waiting for transfers between devices, local(): lax.all_to_all(send, 'ctx', split_axis=0, concat_axis=0, tiled=True)  69.2 us
    pallas_call x4, Pallas kernels, attend(): pl.pallas_call(kernel, grid_spec=grid_spec, out_shape=jax.ShapeDtypeStruc...  41.9 us
    all_to_all x3, starting transfers between devices, local(): lax.all_to_all(send, 'ctx', split_axis=0, concat_axis=0, tiled=True)  20.7 us
    gather x3, local copies, waits for them, and re-layouts, local(): jnp.take(a, my_sources, axis=0, mode='clip')  7.76 us
    gather x1, local copies, waits for them, and re-layouts, rotation_rows(): jnp.take(table, jnp.clip(offsets, 0, distinct - 1), axis=0, mode='clip')  7.01 us
    all_to_all x1, starting transfers between devices, local(): kv = lax.all_to_all(kv, 'tp', split_axis=0, concat_axis=0, tiled=True)  6.19 us
    ppermute x1, starting transfers between devices, passed_along(): return lax.ppermute(shard, axis, pairs)  6.02 us
    dynamic_update_slice x3, local copies, waits for them, and re-layouts, local(): lax.dynamic_update_slice(finished, jnp.take(a, my_sources, axis=0, mode='...  5.2 us
  transfers between devices with their start and end apart: 5, of which 4 were waited for; matrix products, arithmetic and copies ran while one was open for 13% of the time, Pallas kernels for 20%

profile of v14, /device:TPU:1, one launch (start us, length us, event | category | flops | bytes accessed | tf_op | source)
XLA Modules:
  0.0 183.2 jit_solution(18067717562303093780)
XLA Ops:
  0.0 1.0 copy-done
  1.0 1.3 bitcast_bitcast_fusion
  2.4 1.1 pad_maximum_fusion
  3.5 6.2 %all-to-all-start = ((bf16[8,256,256]{2,1,0:T(8,128)(2,1)}), bf16[8,256,256]{2,1,0:T(8,128)(2,1)S(1)}, u32[]{:S(2)}, u32[]{:S(2)}) async-start(bf16[8,256,256]{2,1,0:T(8,128)(2,1)} %pad_maximum_fusion), calls=%async_computation | async-start | bytes 2097152 | tf_op jit(solution)/shard_map/all_to_all | solution.py:185
  10.9 1.6 select_reduce_fusion
  12.6 1.4 copy.30.refs_6_.refs_7_
  14.0 7.0 %gather_fusion = f32[2560,256]{1,0:T(8,128)} fusion(f32[512,256]{1,0:T(8,128)S(1)} %copy.26, s32[3072]{0:T(1024)S(1)} %pad_clamp_fusion), kind=kCustom, calls=%fused_computation | custom fusion | bytes 5253120 | tf_op jit(solution)/shard_map/jit(_take)/gather | solution.py:39
  21.0 0.8 dynamic-slice_reduce_fusion.dest_ref
  22.4 3.1 %all-to-all-done = bf16[8,256,256]{2,1,0:T(8,128)(2,1)S(1)} async-done(((bf16[8,256,256]{2,1,0:T(8,128)(2,1)}), bf16[8,256,256]{2,1,0:T(8,128)(2,1)S(1)}, u32[]{:S(2)}, u32[]{:S(2)}) %all-to-all-start) | async-done | bytes 1048608 | tf_op jit(solution)/shard_map/all_to_all | solution.py:185
  25.5 0.9 fusion.10
  26.8 6.0 %collective-permute-start = (bf16[512,256]{1,0:T(8,128)(2,1)S(1)}, bf16[512,256]{1,0:T(8,128)(2,1)S(1)}, u32[]{:S(2)}, u32[]{:S(2)}) collective-permute-start(bf16[512,256]{1,0:T(8,128)(2,1)S(1)} %bitcast.23), channel_id=1, source_target_pairs={{0,8},{8,16},{16,24},{24,32},{32,40},{40,48},{48,56},{56,64},{64,7... | collective-permute-start | bytes 786440 | tf_op jit(solution)/shard_map/ppermute | solution.py:17
  33.4 0.8 copy-done.2
  34.2 9.4 %shard_map.64.refs_7_ = bf16[16,256,256]{2,1,0:T(8,128)(2,1)} custom-call(s32[8]{0:T(128)} %dynamic-slice_reduce_fusion.dest_ref, s32[8]{0:T(128)} %slice_reduce_fusion.kmin_ref, bf16[2048,1024]{1,0:T(8,128)(2,1)} %refs_2_.3, bf16[2048,1024]{1,0:T(8,128)(2,1)} %refs_2_.3, f32[2560,256]{1,0:T(8,128)} %gather_fusion, f32[2560,256]{1,0:T(8,128)} %gather_fusion, ...), custom_call_target="tpu_custom_call" | custom-call | flops 1207959552 | bytes 2621440 | tf_op jit(solution)/shard_map/pallas_call | solution.py:150
  43.7 1.2 fusion.3
  44.9 0.9 maximum_maximum_fusion.refs_4_.refs_5_
  45.8 4.7 %shard_map.65 = bf16[16,256,256]{2,1,0:T(8,128)(2,1)} custom-call(s32[8]{0:T(128)} %dynamic-slice_reduce_fusion.dest_ref, s32[8]{0:T(128)} %slice_reduce_fusion.kmin_ref, bf16[2048,1024]{1,0:T(8,128)(2,1)} %refs_2_.3, bf16[2048,1024]{1,0:T(8,128)(2,1)} %refs_2_.3, f32[2560,256]{1,0:T(8,128)} %gather_fusion, ...), custom_call_target="tpu_custom_call", output_to_operand_aliasing={{}: (9, {})} | custom-call | flops 402653184 | bytes 1048576 | tf_op jit(solution)/shard_map/pallas_call | solution.py:150
  50.5 5.1 %all-to-all-start.1 = ((bf16[16,256,256]{2,1,0:T(8,128)(2,1)}), bf16[16,256,256]{2,1,0:T(8,128)(2,1)}, u32[]{:S(2)}, u32[]{:S(2)}) async-start(bf16[16,256,256]{2,1,0:T(8,128)(2,1)} %shard_map.65), calls=%async_computation.1 | async-start | bytes 4194304 | tf_op jit(solution)/shard_map/all_to_all | solution.py:242
  55.6 0.9 pad_maximum_fusion.1.refs_5_
  56.5 0.9 pad_maximum_fusion.2.refs_6_
  57.4 13.9 %shard_map.66 = bf16[16,256,384]{2,1,0:T(8,128)(2,1)} custom-call(s32[8]{0:T(128)} %dynamic-slice_reduce_fusion.dest_ref, s32[8]{0:T(128)} %slice_reduce_fusion.kmin_ref, bf16[2048,1024]{1,0:T(8,128)(2,1)} %refs_2_.3, bf16[2048,1024]{1,0:T(8,128)(2,1)} %refs_2_.3, bf16[2048,1024]{1,0:T(8,128)(2,1)} %refs_2_.3, f32[2560,256]{1,0:T(8,128)} %gather_fusion, ...), custom_call_target="tpu_custom_call" | custom-call | flops 2415919104 | bytes 4456448 | tf_op jit(solution)/shard_map/pallas_call | solution.py:150
  71.4 12.7 %all-to-all-done.1 = bf16[16,256,256]{2,1,0:T(8,128)(2,1)} async-done(((bf16[16,256,256]{2,1,0:T(8,128)(2,1)}), bf16[16,256,256]{2,1,0:T(8,128)(2,1)}, u32[]{:S(2)}, u32[]{:S(2)}) %all-to-all-start.1) | async-done | bytes 2097184 | tf_op jit(solution)/shard_map/all_to_all | solution.py:242
  84.0 5.8 %all-to-all-start.2 = ((bf16[16,256,384]{2,1,0:T(8,128)(2,1)}), bf16[16,256,384]{2,1,0:T(8,128)(2,1)}, u32[]{:S(2)}, u32[]{:S(2)}) async-start(bf16[16,256,384]{2,1,0:T(8,128)(2,1)} %shard_map.66), calls=%async_computation.2 | async-start | bytes 6291456 | tf_op jit(solution)/shard_map/all_to_all | solution.py:242
  89.8 13.9 %shard_map.67 = bf16[16,256,384]{2,1,0:T(8,128)(2,1)} custom-call(s32[8]{0:T(128)} %dynamic-slice_reduce_fusion.dest_ref, s32[8]{0:T(128)} %slice_reduce_fusion.kmin_ref, bf16[2048,1024]{1,0:T(8,128)(2,1)} %refs_2_.3, bf16[2048,1024]{1,0:T(8,128)(2,1)} %refs_2_.3, bf16[2048,1024]{1,0:T(8,128)(2,1)} %refs_2_.3, f32[2560,256]{1,0:T(8,128)} %gather_fusion, ...), custom_call_target="tpu_custom_call" | custom-call | flops 2415919104 | bytes 4456448 | tf_op jit(solution)/shard_map/pallas_call | solution.py:150
  103.7 25.8 %all-to-all-done.2 = bf16[16,256,384]{2,1,0:T(8,128)(2,1)} async-done(((bf16[16,256,384]{2,1,0:T(8,128)(2,1)}), bf16[16,256,384]{2,1,0:T(8,128)(2,1)}, u32[]{:S(2)}, u32[]{:S(2)}) %all-to-all-start.2) | async-done | bytes 3145760 | tf_op jit(solution)/shard_map/all_to_all | solution.py:242
  129.5 9.8 %all-to-all-start.3 = ((bf16[16,256,384]{2,1,0:T(8,128)(2,1)}), bf16[16,256,384]{2,1,0:T(8,128)(2,1)}, u32[]{:S(2)}, u32[]{:S(2)}) async-start(bf16[16,256,384]{2,1,0:T(8,128)(2,1)} %shard_map.67), calls=%async_computation.3 | async-start | bytes 6291456 | tf_op jit(solution)/shard_map/all_to_all | solution.py:242
  139.5 2.2 %gather_fusion.1 = bf16[8,256,256]{2,1,0:T(8,128)(2,1)S(1)} fusion(bf16[16,256,256]{2,1,0:T(8,128)(2,1)} %all-to-all-done.1, s32[1024]{0:T(1024)S(1)} %pad_clamp_fusion.1), kind=kCustom, calls=%fused_computation.1 | custom fusion | bytes 2097184 | tf_op jit(solution)/shard_map/jit(_take)/gather | solution.py:253
  141.7 2.6 %dynamic_update_slice.9 = bf16[8,256,1024]{2,1,0:T(8,128)(2,1)} pad(bf16[8,256,256]{2,1,0:T(8,128)(2,1)S(1)} %gather_fusion.1, bf16[]{:T(256)} %constant.49.clone.1), padding=0_0x0_0x0_768 | pad | bytes 5242882 | tf_op jit(solution)/shard_map/dynamic_update_slice | solution.py:252
  144.2 2.8 %gather_fusion.2 = bf16[8,256,384]{2,1,0:T(8,128)(2,1)S(1)} fusion(bf16[16,256,384]{2,1,0:T(8,128)(2,1)} %all-to-all-done.2, s32[1024]{0:T(1024)S(1)} %pad_clamp_fusion.1), kind=kCustom, calls=%fused_computation.2 | custom fusion | bytes 3145760 | tf_op jit(solution)/shard_map/jit(_take)/gather | solution.py:253
  147.0 1.3 constant_dynamic-update-slice_fusion.1
  148.3 30.7 %all-to-all-done.3 = bf16[16,256,384]{2,1,0:T(8,128)(2,1)} async-done(((bf16[16,256,384]{2,1,0:T(8,128)(2,1)}), bf16[16,256,384]{2,1,0:T(8,128)(2,1)}, u32[]{:S(2)}, u32[]{:S(2)}) %all-to-all-start.3) | async-done | bytes 3145760 | tf_op jit(solution)/shard_map/all_to_all | solution.py:242
  179.0 2.8 %gather_fusion.3 = bf16[8,256,384]{2,1,0:T(8,128)(2,1)S(1)} fusion(bf16[16,256,384]{2,1,0:T(8,128)(2,1)} %all-to-all-done.3, s32[1024]{0:T(1024)S(1)} %pad_clamp_fusion.1), kind=kCustom, calls=%fused_computation.3 | custom fusion | bytes 3145760 | tf_op jit(solution)/shard_map/jit(_take)/gather | solution.py:253
  181.8 1.3 constant_dynamic-update-slice_fusion
  (39 shorter events, 3.0 us)
Async XLA Ops:
  0.0 1.0 copy-start
  2.3 7.3 %copy-start.7 = (f32[64]{0:T(128)S(1)}, f32[64]{0:T(128)}, u32[]{:S(2)}) copy-start(f32[64]{0:T(128)} %param.9) | copy-start | bytes 772
  2.4 7.9 %copy-start.6 = (s32[128]{0:T(128)S(1)}, s32[128]{0:T(128)}, u32[]{:S(2)}) copy-start(s32[128]{0:T(128)} %param.10) | copy-start | bytes 1540
  3.5 22.1 %all-to-all-start = ((bf16[8,256,256]{2,1,0:T(8,128)(2,1)}), bf16[8,256,256]{2,1,0:T(8,128)(2,1)S(1)}, u32[]{:S(2)}, u32[]{:S(2)}) async-start(bf16[8,256,256]{2,1,0:T(8,128)(2,1)} %pad_maximum_fusion), calls=%async_computation | async-start | bytes 2097152 | tf_op jit(solution)/shard_map/all_to_all | solution.py:185
  14.0 7.0 %copy-start.5 = (s32[16,8]{0,1:T(8,128)S(1)}, s32[16,8]{0,1:T(8,128)}, u32[]{:S(2)}) copy-start(s32[16,8]{0,1:T(8,128)} %param.11) | copy-start | bytes 1540
  26.4 6.4 %copy-start.1 = (f32[2560,256]{1,0:T(8,128)S(1)}, f32[2560,256]{1,0:T(8,128)}, u32[]{:S(2)}) copy-start(f32[2560,256]{1,0:T(8,128)} %gather_fusion) | copy-start | bytes 7864324
  26.8 16.7 %collective-permute-start = (bf16[512,256]{1,0:T(8,128)(2,1)S(1)}, bf16[512,256]{1,0:T(8,128)(2,1)S(1)}, u32[]{:S(2)}, u32[]{:S(2)}) collective-permute-start(bf16[512,256]{1,0:T(8,128)(2,1)S(1)} %bitcast.23), channel_id=1, source_target_pairs={{0,8},{8,16},{16,24},{24,32},{32,40},{40,48},{48,56},{56,64},{64,7... | collective-permute-start | bytes 786440 | tf_op jit(solution)/shard_map/ppermute | solution.py:17
  33.3 0.8 copy-start.2
  43.5 1.4 slice-start
  50.5 5.1 %copy-start.3 = (bf16[2048,128]{1,0:T(8,128)(2,1)S(1)}, bf16[2048,128]{1,0:T(8,128)(2,1)}, u32[]{:S(2)}) copy-start(bf16[2048,128]{1,0:T(8,128)(2,1)} %copy-done.2) | copy-start | bytes 1572868
  50.5 6.0 %copy-start.4 = (bf16[2048,128]{1,0:T(8,128)(2,1)S(1)}, bf16[2048,128]{1,0:T(8,128)(2,1)}, u32[]{:S(2)}) copy-start(bf16[2048,128]{1,0:T(8,128)(2,1)} %get-tuple-element.5.refs_5_) | copy-start | bytes 1572868
  50.5 33.5 %all-to-all-start.1 = ((bf16[16,256,256]{2,1,0:T(8,128)(2,1)}), bf16[16,256,256]{2,1,0:T(8,128)(2,1)}, u32[]{:S(2)}, u32[]{:S(2)}) async-start(bf16[16,256,256]{2,1,0:T(8,128)(2,1)} %shard_map.65), calls=%async_computation.1 | async-start | bytes 4194304 | tf_op jit(solution)/shard_map/all_to_all | solution.py:242
  84.0 45.5 %all-to-all-start.2 = ((bf16[16,256,384]{2,1,0:T(8,128)(2,1)}), bf16[16,256,384]{2,1,0:T(8,128)(2,1)}, u32[]{:S(2)}, u32[]{:S(2)}) async-start(bf16[16,256,384]{2,1,0:T(8,128)(2,1)} %shard_map.66), calls=%async_computation.2 | async-start | bytes 6291456 | tf_op jit(solution)/shard_map/all_to_all | solution.py:242
  129.5 49.5 %all-to-all-start.3 = ((bf16[16,256,384]{2,1,0:T(8,128)(2,1)}), bf16[16,256,384]{2,1,0:T(8,128)(2,1)}, u32[]{:S(2)}, u32[]{:S(2)}) async-start(bf16[16,256,384]{2,1,0:T(8,128)(2,1)} %shard_map.67), calls=%async_computation.3 | async-start | bytes 6291456 | tf_op jit(solution)/shard_map/all_to_all | solution.py:242

commit v15 on v13

--- a/solution.py
+++ b/solution.py
@@ -60,10 +60,13 @@
     aliased,
 ):
     q_refs = refs[:heads]
-    cos_ref, sin_ref, k_ref, v_ref, lo_ref = refs[heads : heads + 5]
+    parts = span // block_rows
+    cos_ref, sin_ref = refs[heads : heads + 2]
+    k_refs = refs[heads + 2 : heads + 2 + parts]
+    v_refs = refs[heads + 2 + parts : heads + 2 + 2 * parts]
+    lo_ref = refs[heads + 2 + 2 * parts]
     o_ref = refs[-1]
     r = pl.program_id(0) + first_block
-    start = pl.multiple_of(r * block_rows - key_base, block_rows)
     tail = span - block_rows
     lo = lo_ref[0]
     hi = lax.broadcasted_iota(jnp.int32, (block_rows, 1), 0) + tail
@@ -72,8 +75,9 @@
 
     def window(skip):
         width = span - skip
-        k = k_ref[pl.ds(start + skip, width), :]
-        v = v_ref[pl.ds(start + skip, width), :]
+        used = range(skip // block_rows, parts)
+        k = jnp.concatenate([k_refs[w][...] for w in used], axis=0)
+        v = jnp.concatenate([v_refs[w][...] for w in used], axis=0)
         col = lax.broadcasted_iota(jnp.int32, (block_rows, width), 1) + skip
         visible = (col >= lo) & (col <= hi)
         for h in range(heads):
@@ -130,11 +134,15 @@
     ] + [
         pl.BlockSpec((block_rows, head_dim), lambda i, dst, km: (i + first_block + tail_blocks, 0)),
         pl.BlockSpec((block_rows, head_dim), lambda i, dst, km: (i + first_block + tail_blocks, 1)),
-        pl.BlockSpec((k_rows, head_dim), lambda i, dst, km: (0, k_col)),
-        pl.BlockSpec((k_rows, head_dim), lambda i, dst, km: (0, v_col)),
+    ] + [
+        pl.BlockSpec((block_rows, head_dim), functools.partial(
+            lambda i, dst, km, w, c: (i + first_block - key_base // block_rows + w, c), w=w, c=c))
+        for c in (k_col, v_col) for w in range(tail_blocks + 1)
+    ] + [
         pl.BlockSpec((1, block_rows, 1), lambda i, dst, km: (i + first_block, 0, 0)),
     ]
-    args = [dest, kmin] + [q] * heads + [table, table, k_arr, v_arr, lo]
+    parts = tail_blocks + 1
+    args = [dest, kmin] + [q] * heads + [table, table] + [k_arr] * parts + [v_arr] * parts + [lo]
     aliases = {}
     if prev is not None:
         in_specs.append(pl.BlockSpec(memory_space=pl.ANY))

time: 186 us -> 186 us (level)
  Pallas kernels: 44.9 us -> 42.2 us
  waiting for transfers between devices: 70 us -> 72 us
    pallas_call x4, Pallas kernels: 44.9 us -> 42.2 us  [attend(): pl.pallas_call(kernel, grid_spec=grid_spec, out_shape=jax.ShapeDtypeStruc...]
    all_to_all x3, waiting for transfers between devices: 66.9 us -> 68.9 us  [local(): lax.all_to_all(send, 'ctx', split_axis=0, concat_axis=0, tiled=True)]
  transfers between devices with their start and end apart: 5 -> 5, of which waited for: 4 -> 4; matrix products, arithmetic and copies ran while one was open for 13% -> 13% of each run, Pallas kernels for 22% -> 21%
where the time goes in v15:
time: 186 us; the launch traced here: 183 us
  waiting for transfers between devices  72 us (39%)
  Pallas kernels  42.2 us (23%)
  starting transfers between devices  33 us (18%)
  local copies, waits for them, and re-layouts  26.7 us (14%)
  other arithmetic  9.08 us (5%)
    all_to_all x3, waiting for transfers between devices, local(): lax.all_to_all(send, 'ctx', split_axis=0, concat_axis=0, tiled=True)  68.9 us
    pallas_call x4, Pallas kernels, attend(): pl.pallas_call(kernel, grid_spec=grid_spec, out_shape=jax.ShapeDtypeStruc...  42.2 us
    all_to_all x3, starting transfers between devices, local(): lax.all_to_all(send, 'ctx', split_axis=0, concat_axis=0, tiled=True)  20.8 us
    gather x3, local copies, waits for them, and re-layouts, local(): jnp.take(a, my_sources, axis=0, mode='clip')  7.76 us
    gather x1, local copies, waits for them, and re-layouts, rotation_rows(): jnp.take(table, jnp.clip(offsets, 0, distinct - 1), axis=0, mode='clip')  7.01 us
    all_to_all x1, starting transfers between devices, local(): kv = lax.all_to_all(kv, 'tp', split_axis=0, concat_axis=0, tiled=True)  6.19 us
    ppermute x1, starting transfers between devices, passed_along(): return lax.ppermute(shard, axis, pairs)  6.02 us
    dynamic_update_slice x3, local copies, waits for them, and re-layouts, local(): lax.dynamic_update_slice(finished, jnp.take(a, my_sources, axis=0, mode='...  5.2 us
  transfers between devices with their start and end apart: 5, of which 4 were waited for; matrix products, arithmetic and copies ran while one was open for 13% of the time, Pallas kernels for 21%

profile of v15, /device:TPU:1, one launch (start us, length us, event | category | flops | bytes accessed | tf_op | source)
XLA Modules:
  0.0 183.3 jit_solution(1421671498857037094)
XLA Ops:
  0.0 1.0 copy-done
  1.0 1.3 bitcast_bitcast_fusion
  2.4 1.1 pad_maximum_fusion
  3.5 6.2 %all-to-all-start = ((bf16[8,256,256]{2,1,0:T(8,128)(2,1)}), bf16[8,256,256]{2,1,0:T(8,128)(2,1)S(1)}, u32[]{:S(2)}, u32[]{:S(2)}) async-start(bf16[8,256,256]{2,1,0:T(8,128)(2,1)} %pad_maximum_fusion), calls=%async_computation | async-start | bytes 2097152 | tf_op jit(solution)/shard_map/all_to_all | solution.py:194
  10.9 1.6 select_reduce_fusion
  12.6 1.4 copy.30.refs_10_.refs_11_
  14.0 7.0 %gather_fusion = f32[2560,256]{1,0:T(8,128)} fusion(f32[512,256]{1,0:T(8,128)S(1)} %copy.26, s32[3072]{0:T(1024)S(1)} %pad_clamp_fusion), kind=kCustom, calls=%fused_computation | custom fusion | bytes 5253120 | tf_op jit(solution)/shard_map/jit(_take)/gather | solution.py:39
  21.0 0.8 dynamic-slice_reduce_fusion.dest_ref
  22.4 3.1 %all-to-all-done = bf16[8,256,256]{2,1,0:T(8,128)(2,1)S(1)} async-done(((bf16[8,256,256]{2,1,0:T(8,128)(2,1)}), bf16[8,256,256]{2,1,0:T(8,128)(2,1)S(1)}, u32[]{:S(2)}, u32[]{:S(2)}) %all-to-all-start) | async-done | bytes 1048608 | tf_op jit(solution)/shard_map/all_to_all | solution.py:194
  25.5 0.9 fusion.10
  26.8 6.0 %collective-permute-start = (bf16[512,256]{1,0:T(8,128)(2,1)S(1)}, bf16[512,256]{1,0:T(8,128)(2,1)S(1)}, u32[]{:S(2)}, u32[]{:S(2)}) collective-permute-start(bf16[512,256]{1,0:T(8,128)(2,1)S(1)} %bitcast.23), channel_id=1, source_target_pairs={{0,8},{8,16},{16,24},{24,32},{32,40},{40,48},{48,56},{56,64},{64,7... | collective-permute-start | bytes 786440 | tf_op jit(solution)/shard_map/ppermute | solution.py:17
  33.4 0.8 copy-done.2
  34.2 9.7 %shard_map.64.refs_11_ = bf16[16,256,256]{2,1,0:T(8,128)(2,1)} custom-call(s32[8]{0:T(128)} %dynamic-slice_reduce_fusion.dest_ref, s32[8]{0:T(128)} %slice_reduce_fusion.kmin_ref, bf16[2048,1024]{1,0:T(8,128)(2,1)} %refs_2_.3, bf16[2048,1024]{1,0:T(8,128)(2,1)} %refs_2_.3, f32[2560,256]{1,0:T(8,128)} %gather_fusion, f32[2560,256]{1,0:T(8,128)} %gather_fusion, ...), custom_call_target="tpu_custom_call" | custom-call | flops 1207959552 | bytes 2621440 | tf_op jit(solution)/shard_map/pallas_call | solution.py:159
  44.0 1.2 fusion.3
  45.2 0.9 maximum_maximum_fusion.refs_4_.refs_5_.refs_6_.refs_7_.refs_8_.refs_9_
  46.1 4.5 %shard_map.65 = bf16[16,256,256]{2,1,0:T(8,128)(2,1)} custom-call(s32[8]{0:T(128)} %dynamic-slice_reduce_fusion.dest_ref, s32[8]{0:T(128)} %slice_reduce_fusion.kmin_ref, bf16[2048,1024]{1,0:T(8,128)(2,1)} %refs_2_.3, bf16[2048,1024]{1,0:T(8,128)(2,1)} %refs_2_.3, f32[2560,256]{1,0:T(8,128)} %gather_fusion, ...), custom_call_target="tpu_custom_call", output_to_operand_aliasing={{}: (13, {})} | custom-call | flops 402653184 | bytes 1048576 | tf_op jit(solution)/shard_map/pallas_call | solution.py:159
  50.6 5.2 %all-to-all-start.1 = ((bf16[16,256,256]{2,1,0:T(8,128)(2,1)}), bf16[16,256,256]{2,1,0:T(8,128)(2,1)}, u32[]{:S(2)}, u32[]{:S(2)}) async-start(bf16[16,256,256]{2,1,0:T(8,128)(2,1)} %shard_map.65), calls=%async_computation.1 | async-start | bytes 4194304 | tf_op jit(solution)/shard_map/all_to_all | solution.py:251
  55.8 0.9 pad_maximum_fusion.1.refs_5_.refs_6_.refs_7_
  56.7 0.9 pad_maximum_fusion.2.refs_8_.refs_9_.refs_10_
  57.6 14.0 %shard_map.66 = bf16[16,256,384]{2,1,0:T(8,128)(2,1)} custom-call(s32[8]{0:T(128)} %dynamic-slice_reduce_fusion.dest_ref, s32[8]{0:T(128)} %slice_reduce_fusion.kmin_ref, bf16[2048,1024]{1,0:T(8,128)(2,1)} %refs_2_.3, bf16[2048,1024]{1,0:T(8,128)(2,1)} %refs_2_.3, bf16[2048,1024]{1,0:T(8,128)(2,1)} %refs_2_.3, f32[2560,256]{1,0:T(8,128)} %gather_fusion, ...), custom_call_target="tpu_custom_call" | custom-call | flops 2415919104 | bytes 4456448 | tf_op jit(solution)/shard_map/pallas_call | solution.py:159
  71.6 12.6 %all-to-all-done.1 = bf16[16,256,256]{2,1,0:T(8,128)(2,1)} async-done(((bf16[16,256,256]{2,1,0:T(8,128)(2,1)}), bf16[16,256,256]{2,1,0:T(8,128)(2,1)}, u32[]{:S(2)}, u32[]{:S(2)}) %all-to-all-start.1) | async-done | bytes 2097184 | tf_op jit(solution)/shard_map/all_to_all | solution.py:251
  84.2 5.8 %all-to-all-start.2 = ((bf16[16,256,384]{2,1,0:T(8,128)(2,1)}), bf16[16,256,384]{2,1,0:T(8,128)(2,1)}, u32[]{:S(2)}, u32[]{:S(2)}) async-start(bf16[16,256,384]{2,1,0:T(8,128)(2,1)} %shard_map.66), calls=%async_computation.2 | async-start | bytes 6291456 | tf_op jit(solution)/shard_map/all_to_all | solution.py:251
  90.0 14.0 %shard_map.67 = bf16[16,256,384]{2,1,0:T(8,128)(2,1)} custom-call(s32[8]{0:T(128)} %dynamic-slice_reduce_fusion.dest_ref, s32[8]{0:T(128)} %slice_reduce_fusion.kmin_ref, bf16[2048,1024]{1,0:T(8,128)(2,1)} %refs_2_.3, bf16[2048,1024]{1,0:T(8,128)(2,1)} %refs_2_.3, bf16[2048,1024]{1,0:T(8,128)(2,1)} %refs_2_.3, f32[2560,256]{1,0:T(8,128)} %gather_fusion, ...), custom_call_target="tpu_custom_call" | custom-call | flops 2415919104 | bytes 4456448 | tf_op jit(solution)/shard_map/pallas_call | solution.py:159
  104.1 25.7 %all-to-all-done.2 = bf16[16,256,384]{2,1,0:T(8,128)(2,1)} async-done(((bf16[16,256,384]{2,1,0:T(8,128)(2,1)}), bf16[16,256,384]{2,1,0:T(8,128)(2,1)}, u32[]{:S(2)}, u32[]{:S(2)}) %all-to-all-start.2) | async-done | bytes 3145760 | tf_op jit(solution)/shard_map/all_to_all | solution.py:251
  129.7 9.8 %all-to-all-start.3 = ((bf16[16,256,384]{2,1,0:T(8,128)(2,1)}), bf16[16,256,384]{2,1,0:T(8,128)(2,1)}, u32[]{:S(2)}, u32[]{:S(2)}) async-start(bf16[16,256,384]{2,1,0:T(8,128)(2,1)} %shard_map.67), calls=%async_computation.3 | async-start | bytes 6291456 | tf_op jit(solution)/shard_map/all_to_all | solution.py:251
  139.7 2.2 %gather_fusion.1 = bf16[8,256,256]{2,1,0:T(8,128)(2,1)S(1)} fusion(bf16[16,256,256]{2,1,0:T(8,128)(2,1)} %all-to-all-done.1, s32[1024]{0:T(1024)S(1)} %pad_clamp_fusion.1), kind=kCustom, calls=%fused_computation.1 | custom fusion | bytes 2097184 | tf_op jit(solution)/shard_map/jit(_take)/gather | solution.py:262
  141.9 2.6 %dynamic_update_slice.9 = bf16[8,256,1024]{2,1,0:T(8,128)(2,1)} pad(bf16[8,256,256]{2,1,0:T(8,128)(2,1)S(1)} %gather_fusion.1, bf16[]{:T(256)} %constant.49.clone.1), padding=0_0x0_0x0_768 | pad | bytes 5242882 | tf_op jit(solution)/shard_map/dynamic_update_slice | solution.py:261
  144.4 2.8 %gather_fusion.2 = bf16[8,256,384]{2,1,0:T(8,128)(2,1)S(1)} fusion(bf16[16,256,384]{2,1,0:T(8,128)(2,1)} %all-to-all-done.2, s32[1024]{0:T(1024)S(1)} %pad_clamp_fusion.1), kind=kCustom, calls=%fused_computation.2 | custom fusion | bytes 3145760 | tf_op jit(solution)/shard_map/jit(_take)/gather | solution.py:262
  147.2 1.3 constant_dynamic-update-slice_fusion.1
  148.5 30.7 %all-to-all-done.3 = bf16[16,256,384]{2,1,0:T(8,128)(2,1)} async-done(((bf16[16,256,384]{2,1,0:T(8,128)(2,1)}), bf16[16,256,384]{2,1,0:T(8,128)(2,1)}, u32[]{:S(2)}, u32[]{:S(2)}) %all-to-all-start.3) | async-done | bytes 3145760 | tf_op jit(solution)/shard_map/all_to_all | solution.py:251
  179.2 2.8 %gather_fusion.3 = bf16[8,256,384]{2,1,0:T(8,128)(2,1)S(1)} fusion(bf16[16,256,384]{2,1,0:T(8,128)(2,1)} %all-to-all-done.3, s32[1024]{0:T(1024)S(1)} %pad_clamp_fusion.1), kind=kCustom, calls=%fused_computation.3 | custom fusion | bytes 3145760 | tf_op jit(solution)/shard_map/jit(_take)/gather | solution.py:262
  182.0 1.3 constant_dynamic-update-slice_fusion
  (39 shorter events, 3.1 us)
Async XLA Ops:
  0.0 1.0 copy-start
  2.3 7.3 %copy-start.7 = (f32[64]{0:T(128)S(1)}, f32[64]{0:T(128)}, u32[]{:S(2)}) copy-start(f32[64]{0:T(128)} %param.9) | copy-start | bytes 772
  2.4 7.9 %copy-start.6 = (s32[128]{0:T(128)S(1)}, s32[128]{0:T(128)}, u32[]{:S(2)}) copy-start(s32[128]{0:T(128)} %param.10) | copy-start | bytes 1540
  3.5 22.1 %all-to-all-start = ((bf16[8,256,256]{2,1,0:T(8,128)(2,1)}), bf16[8,256,256]{2,1,0:T(8,128)(2,1)S(1)}, u32[]{:S(2)}, u32[]{:S(2)}) async-start(bf16[8,256,256]{2,1,0:T(8,128)(2,1)} %pad_maximum_fusion), calls=%async_computation | async-start | bytes 2097152 | tf_op jit(solution)/shard_map/all_to_all | solution.py:194
  14.0 7.0 %copy-start.5 = (s32[16,8]{0,1:T(8,128)S(1)}, s32[16,8]{0,1:T(8,128)}, u32[]{:S(2)}) copy-start(s32[16,8]{0,1:T(8,128)} %param.11) | copy-start | bytes 1540
  26.4 6.4 %copy-start.1 = (f32[2560,256]{1,0:T(8,128)S(1)}, f32[2560,256]{1,0:T(8,128)}, u32[]{:S(2)}) copy-start(f32[2560,256]{1,0:T(8,128)} %gather_fusion) | copy-start | bytes 7864324
  26.8 17.0 %collective-permute-start = (bf16[512,256]{1,0:T(8,128)(2,1)S(1)}, bf16[512,256]{1,0:T(8,128)(2,1)S(1)}, u32[]{:S(2)}, u32[]{:S(2)}) collective-permute-start(bf16[512,256]{1,0:T(8,128)(2,1)S(1)} %bitcast.23), channel_id=1, source_target_pairs={{0,8},{8,16},{16,24},{24,32},{32,40},{40,48},{48,56},{56,64},{64,7... | collective-permute-start | bytes 786440 | tf_op jit(solution)/shard_map/ppermute | solution.py:17
  33.3 0.8 copy-start.2
  43.8 1.4 slice-start
  50.6 5.2 %copy-start.3 = (bf16[2048,128]{1,0:T(8,128)(2,1)S(1)}, bf16[2048,128]{1,0:T(8,128)(2,1)}, u32[]{:S(2)}) copy-start(bf16[2048,128]{1,0:T(8,128)(2,1)} %copy-done.2) | copy-start | bytes 1572868
  50.6 6.1 %copy-start.4 = (bf16[2048,128]{1,0:T(8,128)(2,1)S(1)}, bf16[2048,128]{1,0:T(8,128)(2,1)}, u32[]{:S(2)}) copy-start(bf16[2048,128]{1,0:T(8,128)(2,1)} %get-tuple-element.5.refs_7_.refs_8_.refs_9_) | copy-start | bytes 1572868
  50.6 33.6 %all-to-all-start.1 = ((bf16[16,256,256]{2,1,0:T(8,128)(2,1)}), bf16[16,256,256]{2,1,0:T(8,128)(2,1)}, u32[]{:S(2)}, u32[]{:S(2)}) async-start(bf16[16,256,256]{2,1,0:T(8,128)(2,1)} %shard_map.65), calls=%async_computation.1 | async-start | bytes 4194304 | tf_op jit(solution)/shard_map/all_to_all | solution.py:251
  84.2 45.5 %all-to-all-start.2 = ((bf16[16,256,384]{2,1,0:T(8,128)(2,1)}), bf16[16,256,384]{2,1,0:T(8,128)(2,1)}, u32[]{:S(2)}, u32[]{:S(2)}) async-start(bf16[16,256,384]{2,1,0:T(8,128)(2,1)} %shard_map.66), calls=%async_computation.2 | async-start | bytes 6291456 | tf_op jit(solution)/shard_map/all_to_all | solution.py:251
  129.7 49.5 %all-to-all-start.3 = ((bf16[16,256,384]{2,1,0:T(8,128)(2,1)}), bf16[16,256,384]{2,1,0:T(8,128)(2,1)}, u32[]{:S(2)}, u32[]{:S(2)}) async-start(bf16[16,256,384]{2,1,0:T(8,128)(2,1)} %shard_map.67), calls=%async_computation.3 | async-start | bytes 6291456 | tf_op jit(solution)/shard_map/all_to_all | solution.py:251

commit v16 on v13

--- a/solution.py
+++ b/solution.py
@@ -249,10 +249,15 @@
     )
     finished = jnp.zeros((per_dev, block_rows, queries.shape[1]), queries.dtype)
     first = 0
-    for heads, a in zip(sizes, arrived):
-        finished = lax.dynamic_update_slice(
-            finished, jnp.take(a, my_sources, axis=0, mode="clip"), (0, 0, first * head_dim)
-        )
+    for number, (heads, a) in enumerate(zip(sizes, arrived)):
+        if number + 1 < len(sizes):
+            finished = lax.dynamic_update_slice(
+                finished, jnp.take(a, my_sources, axis=0, mode="clip"), (0, 0, first * head_dim)
+            )
+        else:
+            for r in range(per_dev):
+                piece = lax.dynamic_index_in_dim(a, my_sources[r], 0, keepdims=True)
+                finished = lax.dynamic_update_slice(finished, piece, (r, 0, first * head_dim))
         first += heads
     return finished.reshape(row_count, queries.shape[1])
 

time: 186 us -> 196 us (1.054)
  between operations: 0.26 us -> 14.9 us
  waiting for transfers between devices: 70 us -> 55.6 us
  local copies, waits for them, and re-layouts: 26.7 us -> 36.8 us
    all_to_all x3, waiting for transfers between devices: 66.9 us -> 52.4 us  [local(): lax.all_to_all(send, 'ctx', split_axis=0, concat_axis=0, tiled=True)]
    dynamic_update_slice x0 -> x8, local copies, waits for them, and re-layouts: none -> 13 us  [local(): lax.dynamic_update_slice(finished, piece, (r, 0, first * head_dim))]
    gather x3 -> x2, local copies, waits for them, and re-layouts: 7.76 us -> 4.98 us  [local(): jnp.take(a, my_sources, axis=0, mode='clip')]
    dynamic_update_slice x3 -> x2, local copies, waits for them, and re-layouts: 5.2 us -> 3.88 us  [local(): lax.dynamic_update_slice(finished, jnp.take(a, my_sources, axis=0, mode='...]
  transfers between devices with their start and end apart: 5 -> 5, of which waited for: 4 -> 4; matrix products, arithmetic and copies ran while one was open for 13% -> 13% of each run, Pallas kernels for 22% -> 20%
where the time goes in v16:
time: 196 us; the launch traced here: 193 us
  waiting for transfers between devices  55.6 us (28%)
  Pallas kernels  43.7 us (22%)
  local copies, waits for them, and re-layouts  36.8 us (19%)
  starting transfers between devices  32.7 us (17%)
  between operations  14.9 us (8%)
  other arithmetic  9.05 us (5%)
    all_to_all x3, waiting for transfers between devices, local(): lax.all_to_all(send, 'ctx', split_axis=0, concat_axis=0, tiled=True)  52.4 us
    pallas_call x4, Pallas kernels, attend(): pl.pallas_call(kernel, grid_spec=grid_spec, out_shape=jax.ShapeDtypeStruc...  43.7 us
    all_to_all x3, starting transfers between devices, local(): lax.all_to_all(send, 'ctx', split_axis=0, concat_axis=0, tiled=True)  20.5 us
    dynamic_update_slice x8, local copies, waits for them, and re-layouts, local(): lax.dynamic_update_slice(finished, piece, (r, 0, first * head_dim))  13 us
    gather x1, local copies, waits for them, and re-layouts, rotation_rows(): jnp.take(table, jnp.clip(offsets, 0, distinct - 1), axis=0, mode='clip')  7.04 us
    all_to_all x1, starting transfers between devices, local(): kv = lax.all_to_all(kv, 'tp', split_axis=0, concat_axis=0, tiled=True)  6.32 us
    ppermute x1, starting transfers between devices, passed_along(): return lax.ppermute(shard, axis, pairs)  5.89 us
    gather x2, local copies, waits for them, and re-layouts, local(): jnp.take(a, my_sources, axis=0, mode='clip')  4.98 us
  transfers between devices with their start and end apart: 5, of which 4 were waited for; matrix products, arithmetic and copies ran while one was open for 13% of the time, Pallas kernels for 20%

profile of v16, /device:TPU:1, one launch (start us, length us, event | category | flops | bytes accessed | tf_op | source)
XLA Modules:
  0.0 192.8 jit_solution(1147384505762465282)
XLA Ops:
  0.0 1.0 copy-done
  1.0 1.3 bitcast_bitcast_fusion
  2.3 1.1 pad_maximum_fusion
  3.4 6.3 %all-to-all-start = ((bf16[8,256,256]{2,1,0:T(8,128)(2,1)}), bf16[8,256,256]{2,1,0:T(8,128)(2,1)S(1)}, u32[]{:S(2)}, u32[]{:S(2)}) async-start(bf16[8,256,256]{2,1,0:T(8,128)(2,1)} %pad_maximum_fusion), calls=%async_computation | async-start | bytes 2097152 | tf_op jit(solution)/shard_map/all_to_all | solution.py:186
  10.2 1.6 select_reduce_fusion
  12.6 1.3 copy.30.refs_6_.refs_7_
  14.8 7.0 %gather_fusion = f32[2560,256]{1,0:T(8,128)} fusion(f32[512,256]{1,0:T(8,128)S(1)} %copy.26, s32[3072]{0:T(1024)S(1)} %pad_clamp_fusion), kind=kCustom, calls=%fused_computation | custom fusion | bytes 5253120 | tf_op jit(solution)/shard_map/jit(_take)/gather | solution.py:39
  22.5 3.2 %all-to-all-done = bf16[8,256,256]{2,1,0:T(8,128)(2,1)S(1)} async-done(((bf16[8,256,256]{2,1,0:T(8,128)(2,1)}), bf16[8,256,256]{2,1,0:T(8,128)(2,1)S(1)}, u32[]{:S(2)}, u32[]{:S(2)}) %all-to-all-start) | async-done | bytes 1048608 | tf_op jit(solution)/shard_map/all_to_all | solution.py:186
  25.6 5.9 %collective-permute-start = (bf16[512,256]{1,0:T(8,128)(2,1)S(1)}, bf16[512,256]{1,0:T(8,128)(2,1)S(1)}, u32[]{:S(2)}, u32[]{:S(2)}) collective-permute-start(bf16[512,256]{1,0:T(8,128)(2,1)S(1)} %bitcast.31), channel_id=1, source_target_pairs={{0,8},{8,16},{16,24},{24,32},{32,40},{40,48},{48,56},{56,64},{64,7... | collective-permute-start | bytes 786440 | tf_op jit(solution)/shard_map/ppermute | solution.py:17
  34.8 9.9 %shard_map.64.refs_7_ = bf16[16,256,256]{2,1,0:T(8,128)(2,1)} custom-call(s32[8]{0:T(128)} %fusion.10.dest_ref, s32[8]{0:T(128)} %slice_reduce_fusion.kmin_ref, bf16[2048,1024]{1,0:T(8,128)(2,1)} %refs_2_.3, bf16[2048,1024]{1,0:T(8,128)(2,1)} %refs_2_.3, f32[2560,256]{1,0:T(8,128)} %gather_fusion, f32[2560,256]{1,0:T(8,128)} %gather_fusion, ...), custom_call_target="tpu_custom_call" | custom-call | flops 1207959552 | bytes 2621440 | tf_op jit(solution)/shard_map/pallas_call | solution.py:151
  44.9 1.2 fusion.3
  46.9 4.6 %shard_map.65 = bf16[16,256,256]{2,1,0:T(8,128)(2,1)} custom-call(s32[8]{0:T(128)} %fusion.10.dest_ref, s32[8]{0:T(128)} %slice_reduce_fusion.kmin_ref, bf16[2048,1024]{1,0:T(8,128)(2,1)} %refs_2_.3, bf16[2048,1024]{1,0:T(8,128)(2,1)} %refs_2_.3, f32[2560,256]{1,0:T(8,128)} %gather_fusion, f32[2560,256]{1,0:T(8,128)} %gather_fusion, ...), custom_call_target="tpu_custom_call", output_to_operand_aliasing={{}: (9, {})} | custom-call | flops 402653184 | bytes 1048576 | tf_op jit(solution)/shard_map/pallas_call | solution.py:151
  51.5 4.8 %all-to-all-start.1 = ((bf16[16,256,256]{2,1,0:T(8,128)(2,1)}), bf16[16,256,256]{2,1,0:T(8,128)(2,1)}, u32[]{:S(2)}, u32[]{:S(2)}) async-start(bf16[16,256,256]{2,1,0:T(8,128)(2,1)} %shard_map.65), calls=%async_computation.1 | async-start | bytes 4194304 | tf_op jit(solution)/shard_map/all_to_all | solution.py:243
  58.2 14.6 %shard_map.66 = bf16[16,256,384]{2,1,0:T(8,128)(2,1)} custom-call(s32[8]{0:T(128)} %fusion.10.dest_ref, s32[8]{0:T(128)} %slice_reduce_fusion.kmin_ref, bf16[2048,1024]{1,0:T(8,128)(2,1)} %refs_2_.3, bf16[2048,1024]{1,0:T(8,128)(2,1)} %refs_2_.3, bf16[2048,1024]{1,0:T(8,128)(2,1)} %refs_2_.3, f32[2560,256]{1,0:T(8,128)} %gather_fusion, ...), custom_call_target="tpu_custom_call" | custom-call | flops 2415919104 | bytes 4456448 | tf_op jit(solution)/shard_map/pallas_call | solution.py:151
  72.8 12.0 %all-to-all-done.1 = bf16[16,256,256]{2,1,0:T(8,128)(2,1)} async-done(((bf16[16,256,256]{2,1,0:T(8,128)(2,1)}), bf16[16,256,256]{2,1,0:T(8,128)(2,1)}, u32[]{:S(2)}, u32[]{:S(2)}) %all-to-all-start.1) | async-done | bytes 2097184 | tf_op jit(solution)/shard_map/all_to_all | solution.py:243
  84.8 5.8 %all-to-all-start.2 = ((bf16[16,256,384]{2,1,0:T(8,128)(2,1)}), bf16[16,256,384]{2,1,0:T(8,128)(2,1)}, u32[]{:S(2)}, u32[]{:S(2)}) async-start(bf16[16,256,384]{2,1,0:T(8,128)(2,1)} %shard_map.66), calls=%async_computation.2 | async-start | bytes 6291456 | tf_op jit(solution)/shard_map/all_to_all | solution.py:243
  90.6 14.6 %shard_map.67 = bf16[16,256,384]{2,1,0:T(8,128)(2,1)} custom-call(s32[8]{0:T(128)} %fusion.10.dest_ref, s32[8]{0:T(128)} %slice_reduce_fusion.kmin_ref, bf16[2048,1024]{1,0:T(8,128)(2,1)} %refs_2_.3, bf16[2048,1024]{1,0:T(8,128)(2,1)} %refs_2_.3, bf16[2048,1024]{1,0:T(8,128)(2,1)} %refs_2_.3, f32[2560,256]{1,0:T(8,128)} %gather_fusion, ...), custom_call_target="tpu_custom_call" | custom-call | flops 2415919104 | bytes 4456448 | tf_op jit(solution)/shard_map/pallas_call | solution.py:151
  105.2 25.1 %all-to-all-done.2 = bf16[16,256,384]{2,1,0:T(8,128)(2,1)} async-done(((bf16[16,256,384]{2,1,0:T(8,128)(2,1)}), bf16[16,256,384]{2,1,0:T(8,128)(2,1)}, u32[]{:S(2)}, u32[]{:S(2)}) %all-to-all-start.2) | async-done | bytes 3145760 | tf_op jit(solution)/shard_map/all_to_all | solution.py:243
  130.3 9.8 %all-to-all-start.3 = ((bf16[16,256,384]{2,1,0:T(8,128)(2,1)}), bf16[16,256,384]{2,1,0:T(8,128)(2,1)}, u32[]{:S(2)}, u32[]{:S(2)}) async-start(bf16[16,256,384]{2,1,0:T(8,128)(2,1)} %shard_map.67), calls=%async_computation.3 | async-start | bytes 6291456 | tf_op jit(solution)/shard_map/all_to_all | solution.py:243
  155.6 2.2 %gather_fusion.1 = bf16[8,256,256]{2,1,0:T(8,128)(2,1)S(1)} fusion(bf16[16,256,256]{2,1,0:T(8,128)(2,1)} %all-to-all-done.1, s32[1024]{0:T(1024)S(1)} %pad_clamp_fusion.1), kind=kCustom, calls=%fused_computation.1 | custom fusion | bytes 2097184 | tf_op jit(solution)/shard_map/jit(_take)/gather | solution.py:255
  157.8 2.6 %dynamic_update_slice.30 = bf16[8,256,1024]{2,1,0:T(8,128)(2,1)} pad(bf16[8,256,256]{2,1,0:T(8,128)(2,1)S(1)} %gather_fusion.1, bf16[]{:T(256)} %constant.74.clone.1), padding=0_0x0_0x0_768 | pad | bytes 5242882 | tf_op jit(solution)/shard_map/dynamic_update_slice | solution.py:254
  160.4 2.8 %gather_fusion.2 = bf16[8,256,384]{2,1,0:T(8,128)(2,1)S(1)} fusion(bf16[16,256,384]{2,1,0:T(8,128)(2,1)} %all-to-all-done.2, s32[1024]{0:T(1024)S(1)} %pad_clamp_fusion.1), kind=kCustom, calls=%fused_computation.2 | custom fusion | bytes 3145760 | tf_op jit(solution)/shard_map/jit(_take)/gather | solution.py:255
  163.2 1.3 constant_dynamic-update-slice_fusion
  164.5 15.3 %all-to-all-done.3 = bf16[16,256,384]{2,1,0:T(8,128)(2,1)} async-done(((bf16[16,256,384]{2,1,0:T(8,128)(2,1)}), bf16[16,256,384]{2,1,0:T(8,128)(2,1)}, u32[]{:S(2)}, u32[]{:S(2)}) %all-to-all-start.3) | async-done | bytes 3145760 | tf_op jit(solution)/shard_map/all_to_all | solution.py:243
  179.8 1.6 dynamic-slice_dynamic-update-slice_fusion.7
  181.4 1.6 dynamic-slice_dynamic-update-slice_fusion.6
  183.0 1.6 dynamic-slice_dynamic-update-slice_fusion.5
  184.7 1.6 dynamic-slice_dynamic-update-slice_fusion.4
  186.3 1.6 dynamic-slice_dynamic-update-slice_fusion.3
  187.9 1.6 dynamic-slice_dynamic-update-slice_fusion.2
  189.5 1.6 dynamic-slice_dynamic-update-slice_fusion.1
  191.2 1.6 dynamic-slice_dynamic-update-slice_fusion
  (45 shorter events, 9.5 us)
Async XLA Ops:
  0.0 1.0 copy-start
  0.0 9.8 %copy-start.7 = (f32[64]{0:T(128)S(1)}, f32[64]{0:T(128)}, u32[]{:S(2)}) copy-start(f32[64]{0:T(128)} %param.9) | copy-start | bytes 772
  0.0 9.8 %copy-start.6 = (s32[128]{0:T(128)S(1)}, s32[128]{0:T(128)}, u32[]{:S(2)}) copy-start(s32[128]{0:T(128)} %param.10) | copy-start | bytes 1540
  3.4 10.6 %copy-start.5 = (s32[16,8]{0,1:T(8,128)S(1)}, s32[16,8]{0,1:T(8,128)}, u32[]{:S(2)}) copy-start(s32[16,8]{0,1:T(8,128)} %param.11) | copy-start | bytes 1540
  3.4 22.2 %all-to-all-start = ((bf16[8,256,256]{2,1,0:T(8,128)(2,1)}), bf16[8,256,256]{2,1,0:T(8,128)(2,1)S(1)}, u32[]{:S(2)}, u32[]{:S(2)}) async-start(bf16[8,256,256]{2,1,0:T(8,128)(2,1)} %pad_maximum_fusion), calls=%async_computation | async-start | bytes 2097152 | tf_op jit(solution)/shard_map/all_to_all | solution.py:186
  25.6 19.0 %collective-permute-start = (bf16[512,256]{1,0:T(8,128)(2,1)S(1)}, bf16[512,256]{1,0:T(8,128)(2,1)S(1)}, u32[]{:S(2)}, u32[]{:S(2)}) collective-permute-start(bf16[512,256]{1,0:T(8,128)(2,1)S(1)} %bitcast.31), channel_id=1, source_target_pairs={{0,8},{8,16},{16,24},{24,32},{32,40},{40,48},{48,56},{56,64},{64,7... | collective-permute-start | bytes 786440 | tf_op jit(solution)/shard_map/ppermute | solution.py:17
  31.5 1.9 %copy-start.1 = (f32[2560,256]{1,0:T(8,128)S(1)}, f32[2560,256]{1,0:T(8,128)}, u32[]{:S(2)}) copy-start(f32[2560,256]{1,0:T(8,128)} %gather_fusion) | copy-start | bytes 7864324
  34.0 0.8 copy-start.2
  51.5 4.8 %copy-start.4 = (bf16[2048,128]{1,0:T(8,128)(2,1)S(1)}, bf16[2048,128]{1,0:T(8,128)(2,1)}, u32[]{:S(2)}) copy-start(bf16[2048,128]{1,0:T(8,128)(2,1)} %get-tuple-element.5.refs_5_) | copy-start | bytes 1572868
  51.5 5.7 %copy-start.3 = (bf16[2048,128]{1,0:T(8,128)(2,1)S(1)}, bf16[2048,128]{1,0:T(8,128)(2,1)}, u32[]{:S(2)}) copy-start(bf16[2048,128]{1,0:T(8,128)(2,1)} %copy-done.2) | copy-start | bytes 1572868
  51.5 33.3 %all-to-all-start.1 = ((bf16[16,256,256]{2,1,0:T(8,128)(2,1)}), bf16[16,256,256]{2,1,0:T(8,128)(2,1)}, u32[]{:S(2)}, u32[]{:S(2)}) async-start(bf16[16,256,256]{2,1,0:T(8,128)(2,1)} %shard_map.65), calls=%async_computation.1 | async-start | bytes 4194304 | tf_op jit(solution)/shard_map/all_to_all | solution.py:243
  84.8 45.5 %all-to-all-start.2 = ((bf16[16,256,384]{2,1,0:T(8,128)(2,1)}), bf16[16,256,384]{2,1,0:T(8,128)(2,1)}, u32[]{:S(2)}, u32[]{:S(2)}) async-start(bf16[16,256,384]{2,1,0:T(8,128)(2,1)} %shard_map.66), calls=%async_computation.2 | async-start | bytes 6291456 | tf_op jit(solution)/shard_map/all_to_all | solution.py:243
  130.3 49.5 %all-to-all-start.3 = ((bf16[16,256,384]{2,1,0:T(8,128)(2,1)}), bf16[16,256,384]{2,1,0:T(8,128)(2,1)}, u32[]{:S(2)}, u32[]{:S(2)}) async-start(bf16[16,256,384]{2,1,0:T(8,128)(2,1)} %shard_map.67), calls=%async_computation.3 | async-start | bytes 6291456 | tf_op jit(solution)/shard_map/all_to_all | solution.py:243

commit v17 on v13

--- a/solution.py
+++ b/solution.py
@@ -57,10 +57,10 @@
 
 def attend_kernel(
     dest_ref, kmin_ref, *refs, heads, head_dim, block_rows, span, scale, first_block, key_base,
-    aliased,
+    aliased, q_inputs,
 ):
-    q_refs = refs[:heads]
-    cos_ref, sin_ref, k_ref, v_ref, lo_ref = refs[heads : heads + 5]
+    q_refs = refs[:q_inputs]
+    cos_ref, sin_ref, k_ref, v_ref, lo_ref = refs[q_inputs : q_inputs + 5]
     o_ref = refs[-1]
     r = pl.program_id(0) + first_block
     start = pl.multiple_of(r * block_rows - key_base, block_rows)
@@ -78,7 +78,10 @@
         visible = (col >= lo) & (col <= hi)
         for h in range(heads):
             cols = slice(h * head_dim, (h + 1) * head_dim)
-            qh = q_refs[h][...].astype(jnp.float32)
+            if q_inputs == heads:
+                qh = q_refs[h][...].astype(jnp.float32)
+            else:
+                qh = q_refs[0][:, cols].astype(jnp.float32)
             qr = (qh * cos + pltpu.roll(qh, head_dim // 2, 1) * sin).astype(jnp.bfloat16)
             s = lax.dot_general(
                 qr, k, (((1,), (1,)), ((), ())), preferred_element_type=jnp.float32
@@ -121,20 +124,26 @@
         first_block=first_block,
         key_base=key_base,
         aliased=prev is not None,
+        q_inputs=1 if first % heads == 0 else heads,
     )
     flops = 4 * blocks * heads * block_rows * span * head_dim
-    in_specs = [
-        pl.BlockSpec((block_rows, head_dim), functools.partial(
-            lambda i, dst, km, col: (i + first_block, col), col=first + head))
-        for head in range(heads)
-    ] + [
+    if first % heads == 0:
+        q_specs = [pl.BlockSpec((block_rows, width), functools.partial(
+            lambda i, dst, km, col: (i + first_block, col), col=first // heads))]
+    else:
+        q_specs = [
+            pl.BlockSpec((block_rows, head_dim), functools.partial(
+                lambda i, dst, km, col: (i + first_block, col), col=first + head))
+            for head in range(heads)
+        ]
+    in_specs = q_specs + [
         pl.BlockSpec((block_rows, head_dim), lambda i, dst, km: (i + first_block + tail_blocks, 0)),
         pl.BlockSpec((block_rows, head_dim), lambda i, dst, km: (i + first_block + tail_blocks, 1)),
         pl.BlockSpec((k_rows, head_dim), lambda i, dst, km: (0, k_col)),
         pl.BlockSpec((k_rows, head_dim), lambda i, dst, km: (0, v_col)),
         pl.BlockSpec((1, block_rows, 1), lambda i, dst, km: (i + first_block, 0, 0)),
     ]
-    args = [dest, kmin] + [q] * heads + [table, table, k_arr, v_arr, lo]
+    args = [dest, kmin] + [q] * len(q_specs) + [table, table, k_arr, v_arr, lo]
     aliases = {}
     if prev is not None:
         in_specs.append(pl.BlockSpec(memory_space=pl.ANY))

time: 186 us -> 186 us (level)
  Pallas kernels: 44.9 us -> 42.3 us
    pallas_call x4, Pallas kernels: 44.9 us -> 42.3 us  [attend(): pl.pallas_call(kernel, grid_spec=grid_spec, out_shape=jax.ShapeDtypeStruc...]
  transfers between devices with their start and end apart: 5 -> 5, of which waited for: 4 -> 4; matrix products, arithmetic and copies ran while one was open for 13% -> 13% of each run, Pallas kernels for 22% -> 21%
where the time goes in v17:
time: 186 us; the launch traced here: 183 us
  waiting for transfers between devices  71.7 us (39%)
  Pallas kernels  42.3 us (23%)
  starting transfers between devices  33.1 us (18%)
  local copies, waits for them, and re-layouts  26.7 us (14%)
  other arithmetic  9.08 us (5%)
    all_to_all x3, waiting for transfers between devices, local(): lax.all_to_all(send, 'ctx', split_axis=0, concat_axis=0, tiled=True)  68.6 us
    pallas_call x4, Pallas kernels, attend(): pl.pallas_call(kernel, grid_spec=grid_spec, out_shape=jax.ShapeDtypeStruc...  42.3 us
    all_to_all x3, starting transfers between devices, local(): lax.all_to_all(send, 'ctx', split_axis=0, concat_axis=0, tiled=True)  20.9 us
    gather x3, local copies, waits for them, and re-layouts, local(): jnp.take(a, my_sources, axis=0, mode='clip')  7.76 us
    gather x1, local copies, waits for them, and re-layouts, rotation_rows(): jnp.take(table, jnp.clip(offsets, 0, distinct - 1), axis=0, mode='clip')  7.01 us
    all_to_all x1, starting transfers between devices, local(): kv = lax.all_to_all(kv, 'tp', split_axis=0, concat_axis=0, tiled=True)  6.19 us
    ppermute x1, starting transfers between devices, passed_along(): return lax.ppermute(shard, axis, pairs)  6.02 us
    dynamic_update_slice x3, local copies, waits for them, and re-layouts, local(): lax.dynamic_update_slice(finished, jnp.take(a, my_sources, axis=0, mode='...  5.2 us
  transfers between devices with their start and end apart: 5, of which 4 were waited for; matrix products, arithmetic and copies ran while one was open for 13% of the time, Pallas kernels for 21%

profile of v17, /device:TPU:1, one launch (start us, length us, event | category | flops | bytes accessed | tf_op | source)
XLA Modules:
  0.0 183.1 jit_solution(4057184577833767485)
XLA Ops:
  0.0 1.0 copy-done
  1.0 1.3 bitcast_bitcast_fusion
  2.4 1.1 pad_maximum_fusion
  3.5 6.2 %all-to-all-start = ((bf16[8,256,256]{2,1,0:T(8,128)(2,1)}), bf16[8,256,256]{2,1,0:T(8,128)(2,1)S(1)}, u32[]{:S(2)}, u32[]{:S(2)}) async-start(bf16[8,256,256]{2,1,0:T(8,128)(2,1)} %pad_maximum_fusion), calls=%async_computation | async-start | bytes 2097152 | tf_op jit(solution)/shard_map/all_to_all | solution.py:195
  10.9 1.6 select_reduce_fusion
  12.6 1.4 copy.30.refs_5_.refs_7_
  14.0 7.0 %gather_fusion = f32[2560,256]{1,0:T(8,128)} fusion(f32[512,256]{1,0:T(8,128)S(1)} %copy.26, s32[3072]{0:T(1024)S(1)} %pad_clamp_fusion), kind=kCustom, calls=%fused_computation | custom fusion | bytes 5253120 | tf_op jit(solution)/shard_map/jit(_take)/gather | solution.py:39
  21.0 0.8 dynamic-slice_reduce_fusion.dest_ref
  22.4 3.1 %all-to-all-done = bf16[8,256,256]{2,1,0:T(8,128)(2,1)S(1)} async-done(((bf16[8,256,256]{2,1,0:T(8,128)(2,1)}), bf16[8,256,256]{2,1,0:T(8,128)(2,1)S(1)}, u32[]{:S(2)}, u32[]{:S(2)}) %all-to-all-start) | async-done | bytes 1048608 | tf_op jit(solution)/shard_map/all_to_all | solution.py:195
  25.5 0.9 fusion.10
  26.8 6.0 %collective-permute-start = (bf16[512,256]{1,0:T(8,128)(2,1)S(1)}, bf16[512,256]{1,0:T(8,128)(2,1)S(1)}, u32[]{:S(2)}, u32[]{:S(2)}) collective-permute-start(bf16[512,256]{1,0:T(8,128)(2,1)S(1)} %bitcast.23), channel_id=1, source_target_pairs={{0,8},{8,16},{16,24},{24,32},{32,40},{40,48},{48,56},{56,64},{64,7... | collective-permute-start | bytes 786440 | tf_op jit(solution)/shard_map/ppermute | solution.py:17
  33.4 0.8 copy-done.2
  34.2 9.4 %shard_map.64.refs_6_ = bf16[16,256,256]{2,1,0:T(8,128)(2,1)} custom-call(s32[8]{0:T(128)} %dynamic-slice_reduce_fusion.dest_ref, s32[8]{0:T(128)} %slice_reduce_fusion.kmin_ref, bf16[2048,1024]{1,0:T(8,128)(2,1)} %refs_2_.3, f32[2560,256]{1,0:T(8,128)} %gather_fusion, f32[2560,256]{1,0:T(8,128)} %gather_fusion, bf16[2048,128]{1,0:T(8,128)(2,1)} %copy-done.2, ...), custom_call_target="tpu_custom_call" | custom-call | flops 1207959552 | bytes 2621440 | tf_op jit(solution)/shard_map/pallas_call | solution.py:160
  43.7 1.2 fusion.3
  44.9 0.9 maximum_maximum_fusion.refs_3_.refs_4_
  45.8 4.6 %shard_map.65 = bf16[16,256,256]{2,1,0:T(8,128)(2,1)} custom-call(s32[8]{0:T(128)} %dynamic-slice_reduce_fusion.dest_ref, s32[8]{0:T(128)} %slice_reduce_fusion.kmin_ref, bf16[2048,1024]{1,0:T(8,128)(2,1)} %refs_2_.3, f32[2560,256]{1,0:T(8,128)} %gather_fusion, f32[2560,256]{1,0:T(8,128)} %gather_fusion, ...), custom_call_target="tpu_custom_call", output_to_operand_aliasing={{}: (8, {})} | custom-call | flops 402653184 | bytes 1048576 | tf_op jit(solution)/shard_map/pallas_call | solution.py:160
  50.3 5.2 %all-to-all-start.1 = ((bf16[16,256,256]{2,1,0:T(8,128)(2,1)}), bf16[16,256,256]{2,1,0:T(8,128)(2,1)}, u32[]{:S(2)}, u32[]{:S(2)}) async-start(bf16[16,256,256]{2,1,0:T(8,128)(2,1)} %shard_map.65), calls=%async_computation.1 | async-start | bytes 4194304 | tf_op jit(solution)/shard_map/all_to_all | solution.py:252
  55.6 0.9 pad_maximum_fusion.1.refs_5_
  56.5 0.9 pad_maximum_fusion.2.refs_6_
  57.4 14.2 %shard_map.66 = bf16[16,256,384]{2,1,0:T(8,128)(2,1)} custom-call(s32[8]{0:T(128)} %dynamic-slice_reduce_fusion.dest_ref, s32[8]{0:T(128)} %slice_reduce_fusion.kmin_ref, bf16[2048,1024]{1,0:T(8,128)(2,1)} %refs_2_.3, bf16[2048,1024]{1,0:T(8,128)(2,1)} %refs_2_.3, bf16[2048,1024]{1,0:T(8,128)(2,1)} %refs_2_.3, f32[2560,256]{1,0:T(8,128)} %gather_fusion, ...), custom_call_target="tpu_custom_call" | custom-call | flops 2415919104 | bytes 4456448 | tf_op jit(solution)/shard_map/pallas_call | solution.py:160
  71.6 12.4 %all-to-all-done.1 = bf16[16,256,256]{2,1,0:T(8,128)(2,1)} async-done(((bf16[16,256,256]{2,1,0:T(8,128)(2,1)}), bf16[16,256,256]{2,1,0:T(8,128)(2,1)}, u32[]{:S(2)}, u32[]{:S(2)}) %all-to-all-start.1) | async-done | bytes 2097184 | tf_op jit(solution)/shard_map/all_to_all | solution.py:252
  84.0 5.8 %all-to-all-start.2 = ((bf16[16,256,384]{2,1,0:T(8,128)(2,1)}), bf16[16,256,384]{2,1,0:T(8,128)(2,1)}, u32[]{:S(2)}, u32[]{:S(2)}) async-start(bf16[16,256,384]{2,1,0:T(8,128)(2,1)} %shard_map.66), calls=%async_computation.2 | async-start | bytes 6291456 | tf_op jit(solution)/shard_map/all_to_all | solution.py:252
  89.8 14.2 %shard_map.67 = bf16[16,256,384]{2,1,0:T(8,128)(2,1)} custom-call(s32[8]{0:T(128)} %dynamic-slice_reduce_fusion.dest_ref, s32[8]{0:T(128)} %slice_reduce_fusion.kmin_ref, bf16[2048,1024]{1,0:T(8,128)(2,1)} %refs_2_.3, bf16[2048,1024]{1,0:T(8,128)(2,1)} %refs_2_.3, bf16[2048,1024]{1,0:T(8,128)(2,1)} %refs_2_.3, f32[2560,256]{1,0:T(8,128)} %gather_fusion, ...), custom_call_target="tpu_custom_call" | custom-call | flops 2415919104 | bytes 4456448 | tf_op jit(solution)/shard_map/pallas_call | solution.py:160
  104.0 25.5 %all-to-all-done.2 = bf16[16,256,384]{2,1,0:T(8,128)(2,1)} async-done(((bf16[16,256,384]{2,1,0:T(8,128)(2,1)}), bf16[16,256,384]{2,1,0:T(8,128)(2,1)}, u32[]{:S(2)}, u32[]{:S(2)}) %all-to-all-start.2) | async-done | bytes 3145760 | tf_op jit(solution)/shard_map/all_to_all | solution.py:252
  129.5 9.8 %all-to-all-start.3 = ((bf16[16,256,384]{2,1,0:T(8,128)(2,1)}), bf16[16,256,384]{2,1,0:T(8,128)(2,1)}, u32[]{:S(2)}, u32[]{:S(2)}) async-start(bf16[16,256,384]{2,1,0:T(8,128)(2,1)} %shard_map.67), calls=%async_computation.3 | async-start | bytes 6291456 | tf_op jit(solution)/shard_map/all_to_all | solution.py:252
  139.5 2.2 %gather_fusion.1 = bf16[8,256,256]{2,1,0:T(8,128)(2,1)S(1)} fusion(bf16[16,256,256]{2,1,0:T(8,128)(2,1)} %all-to-all-done.1, s32[1024]{0:T(1024)S(1)} %pad_clamp_fusion.1), kind=kCustom, calls=%fused_computation.1 | custom fusion | bytes 2097184 | tf_op jit(solution)/shard_map/jit(_take)/gather | solution.py:263
  141.7 2.6 %dynamic_update_slice.9 = bf16[8,256,1024]{2,1,0:T(8,128)(2,1)} pad(bf16[8,256,256]{2,1,0:T(8,128)(2,1)S(1)} %gather_fusion.1, bf16[]{:T(256)} %constant.49.clone.1), padding=0_0x0_0x0_768 | pad | bytes 5242882 | tf_op jit(solution)/shard_map/dynamic_update_slice | solution.py:262
  144.2 2.8 %gather_fusion.2 = bf16[8,256,384]{2,1,0:T(8,128)(2,1)S(1)} fusion(bf16[16,256,384]{2,1,0:T(8,128)(2,1)} %all-to-all-done.2, s32[1024]{0:T(1024)S(1)} %pad_clamp_fusion.1), kind=kCustom, calls=%fused_computation.2 | custom fusion | bytes 3145760 | tf_op jit(solution)/shard_map/jit(_take)/gather | solution.py:263
  147.0 1.3 constant_dynamic-update-slice_fusion.1
  148.3 30.7 %all-to-all-done.3 = bf16[16,256,384]{2,1,0:T(8,128)(2,1)} async-done(((bf16[16,256,384]{2,1,0:T(8,128)(2,1)}), bf16[16,256,384]{2,1,0:T(8,128)(2,1)}, u32[]{:S(2)}, u32[]{:S(2)}) %all-to-all-start.3) | async-done | bytes 3145760 | tf_op jit(solution)/shard_map/all_to_all | solution.py:252
  179.0 2.8 %gather_fusion.3 = bf16[8,256,384]{2,1,0:T(8,128)(2,1)S(1)} fusion(bf16[16,256,384]{2,1,0:T(8,128)(2,1)} %all-to-all-done.3, s32[1024]{0:T(1024)S(1)} %pad_clamp_fusion.1), kind=kCustom, calls=%fused_computation.3 | custom fusion | bytes 3145760 | tf_op jit(solution)/shard_map/jit(_take)/gather | solution.py:263
  181.8 1.3 constant_dynamic-update-slice_fusion
  (39 shorter events, 3.0 us)
Async XLA Ops:
  0.0 1.0 copy-start
  2.3 7.3 %copy-start.7 = (f32[64]{0:T(128)S(1)}, f32[64]{0:T(128)}, u32[]{:S(2)}) copy-start(f32[64]{0:T(128)} %param.9) | copy-start | bytes 772
  2.4 7.9 %copy-start.6 = (s32[128]{0:T(128)S(1)}, s32[128]{0:T(128)}, u32[]{:S(2)}) copy-start(s32[128]{0:T(128)} %param.10) | copy-start | bytes 1540
  3.5 22.1 %all-to-all-start = ((bf16[8,256,256]{2,1,0:T(8,128)(2,1)}), bf16[8,256,256]{2,1,0:T(8,128)(2,1)S(1)}, u32[]{:S(2)}, u32[]{:S(2)}) async-start(bf16[8,256,256]{2,1,0:T(8,128)(2,1)} %pad_maximum_fusion), calls=%async_computation | async-start | bytes 2097152 | tf_op jit(solution)/shard_map/all_to_all | solution.py:195
  14.0 7.0 %copy-start.5 = (s32[16,8]{0,1:T(8,128)S(1)}, s32[16,8]{0,1:T(8,128)}, u32[]{:S(2)}) copy-start(s32[16,8]{0,1:T(8,128)} %param.11) | copy-start | bytes 1540
  26.4 6.4 %copy-start.1 = (f32[2560,256]{1,0:T(8,128)S(1)}, f32[2560,256]{1,0:T(8,128)}, u32[]{:S(2)}) copy-start(f32[2560,256]{1,0:T(8,128)} %gather_fusion) | copy-start | bytes 7864324
  26.8 16.7 %collective-permute-start = (bf16[512,256]{1,0:T(8,128)(2,1)S(1)}, bf16[512,256]{1,0:T(8,128)(2,1)S(1)}, u32[]{:S(2)}, u32[]{:S(2)}) collective-permute-start(bf16[512,256]{1,0:T(8,128)(2,1)S(1)} %bitcast.23), channel_id=1, source_target_pairs={{0,8},{8,16},{16,24},{24,32},{32,40},{40,48},{48,56},{56,64},{64,7... | collective-permute-start | bytes 786440 | tf_op jit(solution)/shard_map/ppermute | solution.py:17
  33.3 0.8 copy-start.2
  43.5 1.4 slice-start
  50.3 5.3 %copy-start.3 = (bf16[2048,128]{1,0:T(8,128)(2,1)S(1)}, bf16[2048,128]{1,0:T(8,128)(2,1)}, u32[]{:S(2)}) copy-start(bf16[2048,128]{1,0:T(8,128)(2,1)} %copy-done.2) | copy-start | bytes 1572868
  50.3 6.1 %copy-start.4 = (bf16[2048,128]{1,0:T(8,128)(2,1)S(1)}, bf16[2048,128]{1,0:T(8,128)(2,1)}, u32[]{:S(2)}) copy-start(bf16[2048,128]{1,0:T(8,128)(2,1)} %get-tuple-element.5.refs_4_) | copy-start | bytes 1572868
  50.3 33.7 %all-to-all-start.1 = ((bf16[16,256,256]{2,1,0:T(8,128)(2,1)}), bf16[16,256,256]{2,1,0:T(8,128)(2,1)}, u32[]{:S(2)}, u32[]{:S(2)}) async-start(bf16[16,256,256]{2,1,0:T(8,128)(2,1)} %shard_map.65), calls=%async_computation.1 | async-start | bytes 4194304 | tf_op jit(solution)/shard_map/all_to_all | solution.py:252
  84.0 45.5 %all-to-all-start.2 = ((bf16[16,256,384]{2,1,0:T(8,128)(2,1)}), bf16[16,256,384]{2,1,0:T(8,128)(2,1)}, u32[]{:S(2)}, u32[]{:S(2)}) async-start(bf16[16,256,384]{2,1,0:T(8,128)(2,1)} %shard_map.66), calls=%async_computation.2 | async-start | bytes 6291456 | tf_op jit(solution)/shard_map/all_to_all | solution.py:252
  129.5 49.5 %all-to-all-start.3 = ((bf16[16,256,384]{2,1,0:T(8,128)(2,1)}), bf16[16,256,384]{2,1,0:T(8,128)(2,1)}, u32[]{:S(2)}, u32[]{:S(2)}) async-start(bf16[16,256,384]{2,1,0:T(8,128)(2,1)} %shard_map.67), calls=%async_computation.3 | async-start | bytes 6291456 | tf_op jit(solution)/shard_map/all_to_all | solution.py:252
